TPU v7x, 128 devices: a whole 4x4x4 slice. The times are simulated.
128 devices in a mesh: ctx: 32 (over y, z, x_lo), tp: 4 (over x_hi, core).
Axes of the slice: x: 4 (x_hi: 2, x_lo: 2; x = x_hi * 2 + x_lo), y: 4, z: 4, core: 2. Of those that a mesh axis runs over, the one named last changes fastest.
Arguments:
- queries: bfloat16 [16384, 2048], P('ctx', 'tp'), may hold values from -7 to 7
- keys: bfloat16 [16384, 2048], P('ctx', 'tp'), may hold values from -6 to 6
- values: bfloat16 [16384, 2048], P('ctx', 'tp'), may hold values from -6 to 6
- doc_ids: int32 [128], replicated, may hold values from 0 to 15, never falling along the last dimension, each value on 1 to 80 neighbouring positions
- span_start: int32 [16], replicated, may hold values from 0 to 127, as said below
- span_end: int32 [16], replicated, may hold values from 1 to 128, as said below
- out_weight: bfloat16 [2048, 4096], P('tp'), may hold values from -0.125 to 0.125
Outputs:
- mixed: bfloat16 [16384, 4096], P(('ctx', 'tp'))
Inputs may be any that keep to these rules, and one draw needn't show every extreme that they name: `doc_ids`: each document occupies consecutive blocks. Spans are disjoint and in increasing order; span s covers blocks span_start[s] to span_end[s] - 1. span_end[s] - span_start[s] is 1 to 4.
All inputs are finite; a program needn't handle non-finite values.
Results may differ from a plain program's by a relative error of at most 0.012.
Values may be sent and summed in bfloat16 or wider, within the bound.
No kernel may reach another device: no remote copies, remote signals or barrier semaphores. Data moves between devices by JAX's collectives and lax.ppermute only.
A program may use at most 128 MiB of HBM per device.

v0:
```python
import math

import jax
import jax.numpy as jnp
import numpy as np
from jax import lax
from jax.experimental import pallas as pl
from jax.experimental.pallas import tpu as pltpu
from jax.sharding import Mesh, NamedSharding, PartitionSpec as P

HEAD_DIM = 128
BLOCK = 128
DOC_MOST = 80
SPAN_MOST = 4
TK = 512

NEG = -1e30


def block_spans(span_start, span_end, count):
    blocks = jnp.arange(count, dtype=jnp.int32)
    inside = (blocks[:, None] >= span_start[None, :]) & (blocks[:, None] < span_end[None, :])
    labels = jnp.arange(1, span_start.shape[0] + 1, dtype=jnp.int32)
    return jnp.sum(jnp.where(inside, labels[None, :], 0), axis=1) - 1


def make_kernel(tq):
    scale = 1.0 / math.sqrt(HEAD_DIM)

    def kernel(qt_ref, kt_ref, first_ref, last_ref, mode_ref, qstart_ref,
               q_ref, k_ref, v_ref, qd_ref, qs_ref, kd_ref, ks_ref, o_ref, m_sc, l_sc, acc_sc):
        p = pl.program_id(0)
        mode = mode_ref[p]

        @pl.when(first_ref[p] == 1)
        def _():
            m_sc[...] = jnp.full(m_sc.shape, NEG, jnp.float32)
            l_sc[...] = jnp.zeros(l_sc.shape, jnp.float32)
            acc_sc[...] = jnp.zeros(acc_sc.shape, jnp.float32)

        def update(masked):
            scores = lax.dot_general(
                q_ref[...], k_ref[...], (((1,), (1,)), ((), ())), preferred_element_type=jnp.float32
            ) * scale
            m_old = m_sc[...]
            if masked:
                qpos = qstart_ref[qt_ref[p]] + lax.broadcasted_iota(jnp.int32, (tq, TK), 0)
                kpos = kt_ref[p] * TK + lax.broadcasted_iota(jnp.int32, (tq, TK), 1)
                allowed = (qd_ref[...] == kd_ref[...]) & ((kpos <= qpos) | (qs_ref[...] == ks_ref[...]))
                scores = jnp.where(allowed, scores, NEG)
                m_new = jnp.maximum(m_old, jnp.max(scores, axis=1, keepdims=True))
                weights = jnp.where(allowed, jnp.exp(scores - m_new), 0.0)
            else:
                m_new = jnp.maximum(m_old, jnp.max(scores, axis=1, keepdims=True))
                weights = jnp.exp(scores - m_new)
            factor = jnp.exp(m_old - m_new)
            l_sc[...] = l_sc[...] * factor + jnp.sum(weights, axis=1, keepdims=True)
            acc_sc[...] = acc_sc[...] * factor + jnp.dot(
                weights.astype(jnp.bfloat16), v_ref[...], preferred_element_type=jnp.float32
            )
            m_sc[...] = m_new

        @pl.when(mode == 1)
        def _():
            update(True)

        @pl.when(mode == 2)
        def _():
            update(False)

        @pl.when(last_ref[p] == 1)
        def _():
            o_ref[...] = (acc_sc[...] / l_sc[...]).astype(o_ref.dtype)

    return kernel


def attend_head(tables, q, kv, qd, qs, kd, ks, tq):
    total = tables[0].shape[0]

    def qmap(p, qt, kt, *_):
        return (qt[p], 0)

    def kmap(p, qt, kt, *_):
        return (kt[p], 0)

    def vmap(p, qt, kt, *_):
        return (kt[p], 1)

    def klab(p, qt, kt, *_):
        return (0, kt[p])

    grid_spec = pltpu.PrefetchScalarGridSpec(
        num_scalar_prefetch=len(tables),
        grid=(total,),
        in_specs=[
            pl.BlockSpec((tq, HEAD_DIM), qmap),
            pl.BlockSpec((TK, HEAD_DIM), kmap),
            pl.BlockSpec((TK, HEAD_DIM), vmap),
            pl.BlockSpec((tq, 1), qmap),
            pl.BlockSpec((tq, 1), qmap),
            pl.BlockSpec((1, TK), klab),
            pl.BlockSpec((1, TK), klab),
        ],
        out_specs=pl.BlockSpec((tq, HEAD_DIM), qmap),
        scratch_shapes=[
            pltpu.VMEM((tq, 1), jnp.float32),
            pltpu.VMEM((tq, 1), jnp.float32),
            pltpu.VMEM((tq, HEAD_DIM), jnp.float32),
        ],
    )
    return pl.pallas_call(
        make_kernel(tq),
        out_shape=jax.ShapeDtypeStruct(q.shape, jnp.bfloat16),
        grid_spec=grid_spec,
        compiler_params=pltpu.CompilerParams(dimension_semantics=("arbitrary",)),
    )(*tables, q, kv, kv, qd, qs, kd, ks)


def take(table, index):
    slots = jnp.arange(table.shape[0], dtype=jnp.int32)
    return jnp.sum(jnp.where(index[..., None] == slots, table, 0), axis=-1)


def step_tables(doc_ids, span_blocks, span_end, qstart, tq, seq):
    count = doc_ids.shape[0]
    nq = qstart.shape[0]
    per_q = tq // BLOCK
    per_k = TK // BLOCK
    ntk = seq // TK
    blocks = jnp.arange(count, dtype=jnp.int32)
    same = doc_ids[:, None] == doc_ids[None, :]
    doc_lo = jnp.min(jnp.where(same, blocks[None, :], count), axis=1)
    doc_hi = jnp.max(jnp.where(same, blocks[None, :], -1), axis=1)
    span_hi = jnp.where(span_blocks >= 0, take(span_end, span_blocks) - 1, blocks)
    key_hi = jnp.minimum(jnp.maximum(span_hi, blocks), doc_hi)
    qblocks = (qstart // BLOCK)[:, None] + jnp.arange(per_q, dtype=jnp.int32)[None, :]
    lo_t = jnp.min(take(doc_lo, qblocks), axis=1) // per_k
    hi_t = jnp.max(take(key_hi, qblocks), axis=1) // per_k
    window = (DOC_MOST - 1) + per_q + (SPAN_MOST - 1)
    most = min(ntk, (window - 1) // per_k + 2)
    cnt = jnp.clip(hi_t - lo_t + 1, 1, most)
    ends = jnp.cumsum(cnt)
    starts = ends - cnt
    total = nq * most
    pos = jnp.arange(total, dtype=jnp.int32)
    qt = jnp.minimum(jnp.sum((pos[:, None] >= ends[None, :]).astype(jnp.int32), axis=1), nq - 1)
    live = pos < ends[-1]
    local = jnp.where(live, pos - take(starts, qt), take(cnt, qt) - 1)
    kt = take(lo_t, qt) + local
    first = (live & (local == 0)).astype(jnp.int32)
    last = (live & (local == take(cnt, qt) - 1)).astype(jnp.int32)
    qdoc = take(doc_ids, qblocks)
    kblocks = kt[:, None] * per_k + jnp.arange(per_k, dtype=jnp.int32)[None, :]
    kdoc = take(doc_ids, kblocks)
    qdoc_t = jnp.sum(jnp.where((qt[:, None] == jnp.arange(nq))[:, :, None], qdoc[None], 0), axis=1)
    one_doc = (jnp.min(qdoc_t, axis=1) == jnp.max(qdoc_t, axis=1)) & (
        jnp.min(kdoc, axis=1) == jnp.max(kdoc, axis=1)) & (qdoc_t[:, 0] == kdoc[:, 0])
    below = (kt + 1) * TK - 1 <= take(qstart, qt)
    mode = jnp.where(live, jnp.where(one_doc & below, 2, 1), 0).astype(jnp.int32)
    return (qt.astype(jnp.int32), kt.astype(jnp.int32), first, last, mode, qstart.astype(jnp.int32))


def per_device(queries, keys, values, doc_ids, span_start, span_end, out_weight):
    rows, local_width = queries.shape
    group = lax.axis_size("cl")
    n_cg = lax.axis_size("cg")
    chunk = rows * group
    piece = chunk // n_cg
    j = lax.axis_index("cg")

    stacked = lax.all_to_all(jnp.stack([queries, keys, values]), "cl", 2, 1, tiled=True)
    q1 = lax.all_to_all(stacked[0], "cg", 0, 0, tiled=True)
    kv1 = jnp.concatenate([stacked[1], stacked[2]], axis=1)
    kv_all = lax.all_gather(kv1, "cg", axis=0, tiled=True)
    seq = kv_all.shape[0]

    count = doc_ids.shape[0]
    span_blocks = block_spans(span_start, span_end, count)
    doc_tok = jnp.broadcast_to(doc_ids[:, None], (count, BLOCK)).reshape(seq)
    span_tok = jnp.broadcast_to(span_blocks[:, None], (count, BLOCK)).reshape(seq)
    key_span = jnp.where(span_tok >= 0, span_tok, -2)
    query_span = jnp.where(span_tok >= 0, span_tok, -1)

    def mine(x):
        return lax.dynamic_index_in_dim(x.reshape(n_cg, n_cg, piece), j, axis=1, keepdims=False).reshape(
            chunk, 1)

    qd = mine(doc_tok)
    qs = mine(query_span)
    kd = doc_tok.reshape(1, seq)
    ks = key_span.reshape(1, seq)
    qstart = jnp.arange(n_cg, dtype=jnp.int32) * chunk + j * piece

    tables = step_tables(doc_ids, span_blocks, span_end, qstart, piece, seq)
    att1 = attend_head(tables, q1, kv_all, qd, qs, kd, ks, piece)
    att0 = lax.all_to_all(att1, "cg", 0, 0, tiled=True)
    attended = lax.all_to_all(att0, "cl", 0, 1, tiled=True)
    mixed = lax.psum_scatter(
        jnp.dot(attended, out_weight, preferred_element_type=jnp.float32).astype(jnp.bfloat16),
        "tp",
        scatter_dimension=0,
        tiled=True,
    )
    return mixed


def solution(mesh):
    n_ctx = mesh.shape["ctx"]
    n_tp = mesh.shape["tp"]
    group = 4
    inner = Mesh(np.asarray(mesh.devices).reshape(n_ctx // group, group, n_tp), ("cg", "cl", "tp"))
    out_sharding = NamedSharding(mesh, P(("ctx", "tp"), None))
    body = jax.shard_map(
        per_device,
        mesh=inner,
        in_specs=(
            P(("cg", "cl"), "tp"),
            P(("cg", "cl"), "tp"),
            P(("cg", "cl"), "tp"),
            P(),
            P(),
            P(),
            P("tp", None),
        ),
        out_specs=P(("cg", "cl", "tp"), None),
        check_vma=False,
    )

    def run(*args):
        return lax.with_sharding_constraint(body(*args), out_sharding)

    return run
```

profile of v0, /device:TPU:1, one launch (start us, length us, event | category | flops | bytes accessed | tf_op | source)
XLA Modules:
  0.0 326.2 jit_solution(13195679871961277218)
XLA Ops:
  6.5 2.7 pad_maximum_fusion
  9.2 3.2 copy.38
  12.5 28.7 %all_to_all.54 = bf16[3,512,512]{1,0,2:T(4,128)(2,1)} all-to-all(bf16[3,512,512]{1,0,2:T(4,128)(2,1)S(1)} %copy.38), channel_id=1, replica_groups=mesh['cg'=8,'cl'=4,'tp'=4] {'cl'}, dimensions={2} | all-to-all | bytes 3145728 | tf_op jit(solution)/shard_map/all_to_all | solution.py:172
  41.2 3.2 copy.39
  44.4 0.9 fusion.11
  45.3 1.1 pad_maximum_fusion.1
  46.6 0.1 sub.64
  46.7 0.1 eq.77
  47.0 0.2 fusion
  47.2 0.2 select_reduce_fusion.3
  47.5 0.2 reduce-window.4
  47.7 0.6 slice.22
  48.3 0.1 copy.41
  48.4 0.1 copy.40
  48.7 0.1 select_reduce_fusion.2
  48.8 0.6 broadcast_multiply_fusion
  49.4 0.4 select_reduce_fusion
  50.2 0.7 compare_select_fusion.ks_ref
  50.9 7.2 %all-to-all-start.1 = ((bf16[8,256,128]{2,1,0:T(8,128)(2,1)}), bf16[8,256,128]{2,1,0:T(8,128)(2,1)S(1)}, u32[]{:S(2)}, u32[]{:S(2)}) async-start(bf16[8,256,128]{2,1,0:T(8,128)(2,1)} %bitcast.9), calls=%async_computation.1 | async-start | bytes 1048576 | tf_op jit(solution)/shard_map/all_to_all | solution.py:173
  58.2 1.4 copy.46
  59.6 1.4 copy.48
  61.0 1.2 and_convert_fusion
  62.2 1.2 fusion.4.mode_ref
  63.3 3.9 %all-to-all-done.1 = bf16[8,256,128]{2,1,0:T(8,128)(2,1)S(1)} async-done(((bf16[8,256,128]{2,1,0:T(8,128)(2,1)}), bf16[8,256,128]{2,1,0:T(8,128)(2,1)S(1)}, u32[]{:S(2)}, u32[]{:S(2)}) %all-to-all-start.1) | async-done | bytes 524320 | tf_op jit(solution)/shard_map/all_to_all | solution.py:173
  67.2 93.7 %all-gather.2.cloned.1.call-done.k_ref.v_ref = bf16[16384,256]{1,0:T(8,128)(2,1)} async-done(((bf16[2048,256]{1,0:T(8,128)(2,1)}), bf16[16384,256]{1,0:T(8,128)(2,1)}) %all-gather.2.cloned.1.call-update) | async-done | bytes 8388624 | tf_op jit(solution)/shard_map/all_gather | solution.py:175
  160.9 0.7 eq.61
  161.6 71.6 %shard_map.73 = bf16[2048,128]{1,0:T(8,128)(2,1)} custom-call(s32[176]{0:T(256)} %copy-done.2, s32[176]{0:T(256)} %copy-done.3, s32[176]{0:T(256)} %get-tuple-element.27.first_ref, s32[176]{0:T(256)} %get-tuple-element.26.last_ref, s32[176]{0:T(256)} %fusion.4.mode_ref, s32[8]{0:T(128)} %copy-done.4, bf16[2048,128]{1,0:T(8,128)(2,1)} %bitcast.58, ...), custom_call_target="tpu_custom_call" | custom-call | tf_op jit(solution)/shard_map/pallas_call | solution.py:112
  233.2 18.6 %all_to_all.55 = bf16[8,256,128]{2,1,0:T(8,128)(2,1)S(1)} all-to-all(bf16[8,256,128]{2,1,0:T(8,128)(2,1)} %bitcast.59), channel_id=1, replica_groups=mesh['cg'=8,'cl'=4,'tp'=4] {'cg'}, dimensions={0} | all-to-all | bytes 1048576 | tf_op jit(solution)/shard_map/all_to_all | solution.py:197
  251.8 8.4 %all_to_all.56 = bf16[4,512,128]{2,1,0:T(8,128)(2,1)S(1)} all-to-all(bf16[4,512,128]{2,1,0:T(8,128)(2,1)S(1)} %bitcast.61), channel_id=1, replica_groups=mesh['cg'=8,'cl'=4,'tp'=4] {'cl'}, dimensions={0} | all-to-all | bytes 1048576 | tf_op jit(solution)/shard_map/all_to_all | solution.py:198
  260.2 0.2 copy.44
  260.4 6.5 %convolution_convert_fusion = bf16[512,4096]{1,0:T(8,128)(2,1)} fusion(bf16[512,512]{0,1:T(8,128)(2,1)S(1)} %bitcast.60, bf16[512,4096]{1,0:T(8,128)(2,1)} %param.13), kind=kOutput, calls=%fused_computation | convolution fusion | flops 2149580800 | bytes 8912896 | tf_op jit(solution)/shard_map/dot_general | solution.py:200
  266.9 52.5 %reduce-scatter.2.cloned.1.call-done = bf16[128,4096]{1,0:T(8,128)(2,1)} async-done(((bf16[512,4096]{1,0:T(8,128)(2,1)}), bf16[128,4096]{1,0:T(8,128)(2,1)}) %reduce-scatter.2.cloned.1.call-update) | async-done | bytes 1048592 | tf_op jit(solution)/shard_map/reduce_scatter | solution.py:199
  (44 shorter events, 0.9 us)
Async XLA Ops:
  6.5 154.3 %all-gather.2.cloned.1.call-start = ((), (), s32[]{:S(2)}) async-start(), calls=%async_computation.5 | async-start | bytes 9437184 | tf_op jit(solution)/shard_map/all_gather | solution.py:175
  45.3 1.1 copy-start.5
  45.3 1.1 copy-start.6
  45.3 1.4 copy-start.1
  48.5 113.1 %copy-start.4 = (s32[8]{0:T(128)}, s32[8]{0:T(128)S(1)}, u32[]{:S(2)}) copy-start(s32[8]{0:T(128)S(1)} %multiply_add_fusion.qstart_ref) | copy-start | bytes 100
  48.6 113.0 %copy-start.2 = (s32[176]{0:T(256)}, s32[176]{0:T(256)S(1)}, u32[]{:S(2)}) copy-start(s32[176]{0:T(256)S(1)} %broadcast_minimum_fusion.qt_ref) | copy-start | bytes 2116
  49.4 112.2 %copy-start.3 = (s32[176]{0:T(256)}, s32[176]{0:T(256)S(1)}, u32[]{:S(2)}) copy-start(s32[176]{0:T(256)S(1)} %get-tuple-element.19.kt_ref) | copy-start | bytes 2116
  50.9 16.4 %all-to-all-start.1 = ((bf16[8,256,128]{2,1,0:T(8,128)(2,1)}), bf16[8,256,128]{2,1,0:T(8,128)(2,1)S(1)}, u32[]{:S(2)}, u32[]{:S(2)}) async-start(bf16[8,256,128]{2,1,0:T(8,128)(2,1)} %bitcast.9), calls=%async_computation.1 | async-start | bytes 1048576 | tf_op jit(solution)/shard_map/all_to_all | solution.py:173
  58.1 261.3 %reduce-scatter.2.cloned.1.call-start = ((), (), s32[]{:S(2)}) async-start(), calls=%async_computation.6 | async-start | bytes 5242880 | tf_op jit(solution)/shard_map/reduce_scatter | solution.py:199
  67.2 94.4 %copy-start = (bf16[8,256,128]{2,1,0:T(8,128)(2,1)}, bf16[8,256,128]{2,1,0:T(8,128)(2,1)S(1)}, u32[]{:S(2)}) copy-start(bf16[8,256,128]{2,1,0:T(8,128)(2,1)S(1)} %all-to-all-done.1) | copy-start | bytes 1572868
Sparse Core Ops, SparseCore 0:
  46.6 114.2 all-gather.1
  267.0 52.3 reduce-scatter.1
where the time goes:
time: 329 us; the launch traced here: 326 us
  waiting for transfers between devices  150 us (46%)
  Pallas kernels  71.6 us (22%)
  blocking collectives  55.7 us (17%)
  between operations  13.6 us (4%)
  local copies, waits for them, and re-layouts  12.5 us (4%)
  other arithmetic  9.03 us (3%)
  starting transfers between devices  7.25 us (2%)
  matrix products  6.49 us (2%)
    all_gather x1, waiting for transfers between devices, per_device(): kv_all = lax.all_gather(kv1, 'cg', axis=0, tiled=True)  93.7 us
    pallas_call x1, Pallas kernels, attend_head(): pl.pallas_call(make_kernel(tq), out_shape=jax.ShapeDtypeStruct(q.shape, j...  71.6 us
    reduce_scatter x1, waiting for transfers between devices, per_device(): lax.psum_scatter(jnp.dot(attended, out_weight, preferred_element_type=jnp...  52.5 us
    all_to_all x1, blocking collectives, per_device(): lax.all_to_all(jnp.stack([queries, keys, values]), 'cl', 2, 1, tiled=True)  28.7 us
    all_to_all x1, blocking collectives, per_device(): att0 = lax.all_to_all(att1, 'cg', 0, 0, tiled=True)  18.6 us
    all_to_all x1, blocking collectives, per_device(): attended = lax.all_to_all(att0, 'cl', 0, 1, tiled=True)  8.37 us
    all_to_all x1, starting transfers between devices, per_device(): q1 = lax.all_to_all(stacked[0], 'cg', 0, 0, tiled=True)  7.21 us
  transfers between devices with their start and end apart: 3, of which 3 were waited for; matrix products, arithmetic and copies ran while one was open for 3% of the time, Pallas kernels for 0%

commit v1 on v0

--- a/solution.py
+++ b/solution.py
@@ -27,16 +27,17 @@
 def make_kernel(tq):
     scale = 1.0 / math.sqrt(HEAD_DIM)
 
-    def kernel(qt_ref, kt_ref, first_ref, last_ref, mode_ref, qstart_ref,
-               q_ref, k_ref, v_ref, qd_ref, qs_ref, kd_ref, ks_ref, o_ref, m_sc, l_sc, acc_sc):
+    def kernel(qt_ref, kt_ref, kb_ref, first_ref, mode_ref, qstart_ref,
+               q_ref, k_ref, v_ref, qd_ref, qs_ref, kd_ref, ks_ref, m_in, l_in, acc_in,
+               m_sc, l_sc, acc_sc):
         p = pl.program_id(0)
         mode = mode_ref[p]
 
         @pl.when(first_ref[p] == 1)
         def _():
-            m_sc[...] = jnp.full(m_sc.shape, NEG, jnp.float32)
-            l_sc[...] = jnp.zeros(l_sc.shape, jnp.float32)
-            acc_sc[...] = jnp.zeros(acc_sc.shape, jnp.float32)
+            m_sc[...] = m_in[...]
+            l_sc[...] = l_in[...]
+            acc_sc[...] = acc_in[...]
 
         def update(masked):
             scores = lax.dot_general(
@@ -68,28 +69,25 @@
         def _():
             update(False)
 
-        @pl.when(last_ref[p] == 1)
-        def _():
-            o_ref[...] = (acc_sc[...] / l_sc[...]).astype(o_ref.dtype)
-
     return kernel
 
 
-def attend_head(tables, q, kv, qd, qs, kd, ks, tq):
+def attend_part(tables, q, kv, qd, qs, kd, ks, state, tq):
     total = tables[0].shape[0]
 
-    def qmap(p, qt, kt, *_):
+    def qmap(p, qt, *_):
         return (qt[p], 0)
 
-    def kmap(p, qt, kt, *_):
-        return (kt[p], 0)
-
-    def vmap(p, qt, kt, *_):
-        return (kt[p], 1)
+    def kmap(p, qt, kt, kb, *_):
+        return (kb[p], 0)
+
+    def vmap(p, qt, kt, kb, *_):
+        return (kb[p], 1)
 
     def klab(p, qt, kt, *_):
         return (0, kt[p])
 
+    m, l, acc = state
     grid_spec = pltpu.PrefetchScalarGridSpec(
         num_scalar_prefetch=len(tables),
         grid=(total,),
@@ -101,20 +99,28 @@
             pl.BlockSpec((tq, 1), qmap),
             pl.BlockSpec((1, TK), klab),
             pl.BlockSpec((1, TK), klab),
+            pl.BlockSpec((tq, 1), qmap),
+            pl.BlockSpec((tq, 1), qmap),
+            pl.BlockSpec((tq, HEAD_DIM), qmap),
         ],
-        out_specs=pl.BlockSpec((tq, HEAD_DIM), qmap),
-        scratch_shapes=[
-            pltpu.VMEM((tq, 1), jnp.float32),
-            pltpu.VMEM((tq, 1), jnp.float32),
-            pltpu.VMEM((tq, HEAD_DIM), jnp.float32),
+        out_specs=[
+            pl.BlockSpec((tq, 1), qmap),
+            pl.BlockSpec((tq, 1), qmap),
+            pl.BlockSpec((tq, HEAD_DIM), qmap),
         ],
     )
+    n = len(tables)
     return pl.pallas_call(
         make_kernel(tq),
-        out_shape=jax.ShapeDtypeStruct(q.shape, jnp.bfloat16),
+        out_shape=(
+            jax.ShapeDtypeStruct(m.shape, jnp.float32),
+            jax.ShapeDtypeStruct(l.shape, jnp.float32),
+            jax.ShapeDtypeStruct(acc.shape, jnp.float32),
+        ),
         grid_spec=grid_spec,
+        input_output_aliases={n + 7: 0, n + 8: 1, n + 9: 2},
         compiler_params=pltpu.CompilerParams(dimension_semantics=("arbitrary",)),
-    )(*tables, q, kv, kv, qd, qs, kd, ks)
+    )(*tables, q, kv, kv, qd, qs, kd, ks, m, l, acc)
 
 
 def take(table, index):
@@ -158,7 +164,26 @@
         jnp.min(kdoc, axis=1) == jnp.max(kdoc, axis=1)) & (qdoc_t[:, 0] == kdoc[:, 0])
     below = (kt + 1) * TK - 1 <= take(qstart, qt)
     mode = jnp.where(live, jnp.where(one_doc & below, 2, 1), 0).astype(jnp.int32)
-    return (qt.astype(jnp.int32), kt.astype(jnp.int32), first, last, mode, qstart.astype(jnp.int32))
+    return qt.astype(jnp.int32), kt.astype(jnp.int32), mode, live, most
+
+
+def part_tables(qt, kt, mode, live, part, parts, size, nq):
+    total = qt.shape[0]
+    pos = jnp.arange(total, dtype=jnp.int32)
+    chosen = live & (kt % parts == part)
+    n_sel = jnp.sum(chosen.astype(jnp.int32))
+    order = jnp.argsort(jnp.where(chosen, pos, total + pos))[:size].astype(jnp.int32)
+    i = jnp.arange(size, dtype=jnp.int32)
+    keep = i < n_sel
+    tail = take(order, jnp.maximum(n_sel - 1, 0)[None])[0]
+    src = jnp.where(keep, order, tail)
+    any_sel = n_sel > 0
+    qt_p = jnp.where(any_sel, take(qt, src), nq - 1)
+    kt_p = jnp.where(any_sel, take(kt, src), part)
+    mode_p = jnp.where(keep, take(mode, src), 0)
+    prev = jnp.concatenate([jnp.full((1,), -1, jnp.int32), qt_p[:-1]])
+    first = ((i == 0) | (keep & (qt_p != prev))).astype(jnp.int32)
+    return qt_p, kt_p, kt_p // parts, first, mode_p.astype(jnp.int32)
 
 
 def per_device(queries, keys, values, doc_ids, span_start, span_end, out_weight):
@@ -172,8 +197,9 @@
     stacked = lax.all_to_all(jnp.stack([queries, keys, values]), "cl", 2, 1, tiled=True)
     q1 = lax.all_to_all(stacked[0], "cg", 0, 0, tiled=True)
     kv1 = jnp.concatenate([stacked[1], stacked[2]], axis=1)
-    kv_all = lax.all_gather(kv1, "cg", axis=0, tiled=True)
-    seq = kv_all.shape[0]
+    parts = chunk // TK
+    kv_parts = [lax.all_gather(kv1[p * TK:(p + 1) * TK], "cg", axis=0, tiled=True) for p in range(parts)]
+    seq = chunk * n_cg
 
     count = doc_ids.shape[0]
     span_blocks = block_spans(span_start, span_end, count)
@@ -192,8 +218,20 @@
     ks = key_span.reshape(1, seq)
     qstart = jnp.arange(n_cg, dtype=jnp.int32) * chunk + j * piece
 
-    tables = step_tables(doc_ids, span_blocks, span_end, qstart, piece, seq)
-    att1 = attend_head(tables, q1, kv_all, qd, qs, kd, ks, piece)
+    qt, kt, mode, live, most = step_tables(doc_ids, span_blocks, span_end, qstart, piece, seq)
+    nq = n_cg
+    size = nq * (-(-most // parts) + 1)
+    state = (
+        jnp.full((chunk, 1), NEG, jnp.float32),
+        jnp.zeros((chunk, 1), jnp.float32),
+        jnp.zeros((chunk, HEAD_DIM), jnp.float32),
+    )
+    for p in range(parts):
+        qt_p, kt_p, kb_p, first_p, mode_p = part_tables(qt, kt, mode, live, p, parts, size, nq)
+        tables = (qt_p, kt_p, kb_p, first_p, mode_p, qstart.astype(jnp.int32))
+        state = attend_part(tables, q1, kv_parts[p], qd, qs, kd, ks, state, piece)
+    m, l, acc = state
+    att1 = (acc / l).astype(jnp.bfloat16)
     att0 = lax.all_to_all(att1, "cg", 0, 0, tiled=True)
     attended = lax.all_to_all(att0, "cl", 0, 1, tiled=True)
     mixed = lax.psum_scatter(

time: 329 us -> 403 us (1.22)
  other arithmetic: 9.03 us -> 42.4 us
  Pallas kernels: 71.6 us -> 101 us
  waiting for transfers between devices: 150 us -> 155 us
  between operations: 13.6 us -> 18.5 us
    pallas_call x1 -> x4, Pallas kernels: 71.6 us -> 101 us  [attend_part(): pl.pallas_call(make_kernel(tq), out_shape=(jax.ShapeDtypeStruct(m.shape,...]
    sort x0 -> x4, other arithmetic: none -> 12.7 us  [part_tables(): jnp.argsort(jnp.where(chosen, pos, total + pos))[:size].astype(jnp.int32)]
    select_n x0 -> x13, other arithmetic: none -> 10.5 us  [the longest x4 5.02 us: part_tables(): src = jnp.where(keep, order, tail)]
    convert_element_type x1 -> x5, other arithmetic: 1.17 us -> 6.6 us  [the longest x4 5.03 us: part_tables(): first = ((i == 0) | keep & (qt_p != prev)).astype(jnp.int32)]
    all_gather x1 -> x4, waiting for transfers between devices: 93.7 us -> 97.5 us  [per_device(): lax.all_gather(kv1[p * TK:(p + 1) * TK], 'cg', axis=0, tiled=True)]
  transfers between devices with their start and end apart: 3 -> 6, of which waited for: 3 -> 6; matrix products, arithmetic and copies ran while one was open for 3% -> 11% of each run, Pallas kernels for 0% -> 19%
where the time goes in v1:
time: 403 us; the launch traced here: 401 us
  waiting for transfers between devices  155 us (38%)
  Pallas kernels  101 us (25%)
  blocking collectives  54.2 us (13%)
  other arithmetic  42.4 us (11%)
  between operations  18.5 us (5%)
  local copies, waits for them, and re-layouts  15.6 us (4%)
  starting transfers between devices  7.37 us (2%)
  matrix products  6.49 us (2%)
    pallas_call x4, Pallas kernels, attend_part(): pl.pallas_call(make_kernel(tq), out_shape=(jax.ShapeDtypeStruct(m.shape,...  101 us
    all_gather x4, waiting for transfers between devices, per_device(): lax.all_gather(kv1[p * TK:(p + 1) * TK], 'cg', axis=0, tiled=True)  97.5 us
    reduce_scatter x1, waiting for transfers between devices, per_device(): lax.psum_scatter(jnp.dot(attended, out_weight, preferred_element_type=jnp...  54.3 us
    all_to_all x1, blocking collectives, per_device(): lax.all_to_all(jnp.stack([queries, keys, values]), 'cl', 2, 1, tiled=True)  28.7 us
    all_to_all x1, blocking collectives, per_device(): att0 = lax.all_to_all(att1, 'cg', 0, 0, tiled=True)  16.5 us
    sort x4, other arithmetic, part_tables(): jnp.argsort(jnp.where(chosen, pos, total + pos))[:size].astype(jnp.int32)  12.7 us
    all_to_all x1, blocking collectives, per_device(): attended = lax.all_to_all(att0, 'cl', 0, 1, tiled=True)  9.03 us
  transfers between devices with their start and end apart: 6, of which 6 were waited for; matrix products, arithmetic and copies ran while one was open for 11% of the time, Pallas kernels for 19%

profile of v1, /device:TPU:1, one launch (start us, length us, event | category | flops | bytes accessed | tf_op | source)
XLA Modules:
  0.0 401.2 jit_solution(11425247766646286889)
XLA Ops:
  6.5 2.7 pad_maximum_fusion
  9.2 3.2 copy.87
  12.5 28.7 %all_to_all.54 = bf16[3,512,512]{1,0,2:T(4,128)(2,1)} all-to-all(bf16[3,512,512]{1,0,2:T(4,128)(2,1)S(1)} %copy.87), channel_id=1, replica_groups=mesh['cg'=8,'cl'=4,'tp'=4] {'cl'}, dimensions={2} | all-to-all | bytes 3145728 | tf_op jit(solution)/shard_map/all_to_all | solution.py:197
  41.2 3.2 copy.88
  49.2 1.3 convert_reduce_fusion.1
  55.9 3.2 sort.59
  59.1 3.2 sort.61
  62.2 3.2 sort.60
  65.4 3.2 sort.62
  71.8 1.3 fusion.23
  75.5 1.3 fusion.17
  77.9 1.3 or_convert_fusion.first_ref
  80.5 1.3 or_convert_fusion.2.first_ref
  83.0 1.3 and_select_fusion
  86.4 7.2 %all-to-all-start.1 = ((bf16[8,256,128]{2,1,0:T(8,128)(2,1)}), bf16[8,256,128]{2,1,0:T(8,128)(2,1)S(1)}, u32[]{:S(2)}, u32[]{:S(2)}) async-start(bf16[8,256,128]{2,1,0:T(8,128)(2,1)} %bitcast.9), calls=%async_computation.1 | async-start | bytes 1048576 | tf_op jit(solution)/shard_map/all_to_all | solution.py:198
  93.7 1.3 copy.103
  95.0 1.4 copy.105
  98.9 3.7 all-to-all-done.1
  102.5 10.3 %all-gather.11.cloned.1.call-done.k_ref.v_ref = bf16[4096,256]{1,0:T(8,128)(2,1)} async-done(((bf16[512,256]{1,0:T(8,128)(2,1)}), bf16[4096,256]{1,0:T(8,128)(2,1)}) %all-gather.11.cloned.1.call-update) | async-done | bytes 2097168 | tf_op jit(solution)/shard_map/all_gather | solution.py:201
  116.7 29.2 %shard_map.73 = (f32[2048,1]{1,0:T(8,128)}, f32[2048,1]{1,0:T(8,128)}, f32[2048,128]{1,0:T(8,128)}) custom-call(s32[56]{0:T(128)} %copy-done.6, s32[56]{0:T(128)} %get-tuple-element.77.kt_ref, s32[56]{0:T(128)} %get-tuple-element.76.kb_ref, s32[56]{0:T(128)} %or_convert_fusion.first_ref, ...), custom_call_target="tpu_custom_call", output_to_operand_aliasing={{0}: (13, {}), {1}: (14, {}), {2}: (15, {})} | custom-call | tf_op jit(solution)/shard_map/pallas_call | solution.py:113
  145.9 23.1 %all-gather.9.cloned.1.call-done.k_ref.v_ref = bf16[4096,256]{1,0:T(8,128)(2,1)} async-done(((bf16[512,256]{1,0:T(8,128)(2,1)}), bf16[4096,256]{1,0:T(8,128)(2,1)}) %all-gather.9.cloned.1.call-update) | async-done | bytes 2097168 | tf_op jit(solution)/shard_map/all_gather | solution.py:201
  169.1 23.9 %shard_map.74 = (f32[2048,1]{1,0:T(8,128)}, f32[2048,1]{1,0:T(8,128)}, f32[2048,128]{1,0:T(8,128)}) custom-call(s32[56]{0:T(128)} %copy-done.5, s32[56]{0:T(128)} %get-tuple-element.79.kt_ref, s32[56]{0:T(128)} %get-tuple-element.78.kb_ref, s32[56]{0:T(128)} %or_convert_fusion.1.first_ref, ...), custom_call_target="tpu_custom_call", output_to_operand_aliasing={{0}: (13, {}), {1}: (14, {}), {2}: (15, {})} | custom-call | tf_op jit(solution)/shard_map/pallas_call | solution.py:113
  192.9 32.2 %all-gather.7.cloned.1.call-done.k_ref.v_ref = bf16[4096,256]{1,0:T(8,128)(2,1)} async-done(((bf16[512,256]{1,0:T(8,128)(2,1)}), bf16[4096,256]{1,0:T(8,128)(2,1)}) %all-gather.7.cloned.1.call-update) | async-done | bytes 2097168 | tf_op jit(solution)/shard_map/all_gather | solution.py:201
  225.1 24.1 %shard_map.75 = (f32[2048,1]{1,0:T(8,128)}, f32[2048,1]{1,0:T(8,128)}, f32[2048,128]{1,0:T(8,128)}) custom-call(s32[56]{0:T(128)} %copy-done.4, s32[56]{0:T(128)} %get-tuple-element.81.kt_ref, s32[56]{0:T(128)} %get-tuple-element.80.kb_ref, s32[56]{0:T(128)} %or_convert_fusion.2.first_ref, ...), custom_call_target="tpu_custom_call", output_to_operand_aliasing={{0}: (13, {}), {1}: (14, {}), {2}: (15, {})} | custom-call | tf_op jit(solution)/shard_map/pallas_call | solution.py:113
  249.2 31.8 %all-gather.5.cloned.1.call-done.k_ref.v_ref = bf16[4096,256]{1,0:T(8,128)(2,1)} async-done(((bf16[512,256]{1,0:T(8,128)(2,1)}), bf16[4096,256]{1,0:T(8,128)(2,1)}) %all-gather.5.cloned.1.call-update) | async-done | bytes 2097168 | tf_op jit(solution)/shard_map/all_gather | solution.py:201
  281.1 24.0 %shard_map.76 = (f32[2048,1]{1,0:T(8,128)}, f32[2048,1]{1,0:T(8,128)}, f32[2048,128]{1,0:T(8,128)}) custom-call(s32[56]{0:T(128)} %copy-done.3, s32[56]{0:T(128)} %get-tuple-element.83.kt_ref, s32[56]{0:T(128)} %get-tuple-element.82.kb_ref, s32[56]{0:T(128)} %or_convert_fusion.3.first_ref, ...), custom_call_target="tpu_custom_call", output_to_operand_aliasing={{0}: (13, {}), {1}: (14, {}), {2}: (15, {})} | custom-call | tf_op jit(solution)/shard_map/pallas_call | solution.py:113
  305.0 1.6 reduce.9
  306.6 1.6 divide_convert_fusion
  308.2 16.5 %all_to_all.55 = bf16[8,256,128]{2,1,0:T(8,128)(2,1)S(1)} all-to-all(bf16[8,256,128]{2,1,0:T(8,128)(2,1)S(1)} %bitcast.72), channel_id=1, replica_groups=mesh['cg'=8,'cl'=4,'tp'=4] {'cg'}, dimensions={0} | all-to-all | bytes 1048576 | tf_op jit(solution)/shard_map/all_to_all | solution.py:235
  324.7 9.0 %all_to_all.56 = bf16[4,512,128]{2,1,0:T(8,128)(2,1)S(1)} all-to-all(bf16[4,512,128]{2,1,0:T(8,128)(2,1)S(1)} %bitcast.74), channel_id=1, replica_groups=mesh['cg'=8,'cl'=4,'tp'=4] {'cl'}, dimensions={0} | all-to-all | bytes 1048576 | tf_op jit(solution)/shard_map/all_to_all | solution.py:236
  333.9 6.5 %convolution_convert_fusion = bf16[512,4096]{1,0:T(8,128)(2,1)} fusion(bf16[512,512]{0,1:T(8,128)(2,1)S(1)} %bitcast.73, bf16[512,4096]{1,0:T(8,128)(2,1)} %param.13), kind=kOutput, calls=%fused_computation | convolution fusion | flops 2149580800 | bytes 8912896 | tf_op jit(solution)/shard_map/dot_general | solution.py:238
  340.4 54.3 %reduce-scatter.2.cloned.1.call-done = bf16[128,4096]{1,0:T(8,128)(2,1)} async-done(((bf16[512,4096]{1,0:T(8,128)(2,1)}), bf16[128,4096]{1,0:T(8,128)(2,1)}) %reduce-scatter.2.cloned.1.call-update) | async-done | bytes 1048592 | tf_op jit(solution)/shard_map/reduce_scatter | solution.py:237
  (95 shorter events, 22.6 us)
Async XLA Ops:
  6.5 106.3 %all-gather.11.cloned.1.call-start = ((), (), s32[]{:S(2)}) async-start(), calls=%async_computation.8 | async-start | bytes 2359296 | tf_op jit(solution)/shard_map/all_gather | solution.py:201
  44.4 2.1 copy-start.7
  44.4 2.1 copy-start.8
  44.4 2.3 copy-start.1
  46.4 122.6 %all-gather.9.cloned.1.call-start = ((), (), s32[]{:S(2)}) async-start(), calls=%async_computation.7 | async-start | bytes 2359296 | tf_op jit(solution)/shard_map/all_gather | solution.py:201
  47.2 177.9 %all-gather.7.cloned.1.call-start = ((), (), s32[]{:S(2)}) async-start(), calls=%async_computation.6 | async-start | bytes 2359296 | tf_op jit(solution)/shard_map/all_gather | solution.py:201
  48.4 48.1 %copy-start.2 = (s32[8]{0:T(128)}, s32[8]{0:T(128)S(1)}, u32[]{:S(2)}) copy-start(s32[8]{0:T(128)S(1)} %multiply_add_fusion.qstart_ref) | copy-start | bytes 100
  73.1 207.9 %all-gather.5.cloned.1.call-start = ((), (), s32[]{:S(2)}) async-start(), calls=%async_computation.5 | async-start | bytes 2359296 | tf_op jit(solution)/shard_map/all_gather | solution.py:201
  77.9 36.7 %copy-start.6 = (s32[56]{0:T(128)}, s32[56]{0:T(128)S(1)}, u32[]{:S(2)}) copy-start(s32[56]{0:T(128)S(1)} %broadcast_select_fusion.1.qt_ref) | copy-start | bytes 676
  79.3 35.3 %copy-start.5 = (s32[56]{0:T(128)}, s32[56]{0:T(128)S(1)}, u32[]{:S(2)}) copy-start(s32[56]{0:T(128)S(1)} %broadcast_select_fusion.3.qt_ref) | copy-start | bytes 676
  80.5 34.1 %copy-start.4 = (s32[56]{0:T(128)}, s32[56]{0:T(128)S(1)}, u32[]{:S(2)}) copy-start(s32[56]{0:T(128)S(1)} %broadcast_select_fusion.5.qt_ref) | copy-start | bytes 676
  81.8 32.8 %copy-start.3 = (s32[56]{0:T(128)}, s32[56]{0:T(128)S(1)}, u32[]{:S(2)}) copy-start(s32[56]{0:T(128)S(1)} %broadcast_select_fusion.7.qt_ref) | copy-start | bytes 676
  86.4 16.2 %all-to-all-start.1 = ((bf16[8,256,128]{2,1,0:T(8,128)(2,1)}), bf16[8,256,128]{2,1,0:T(8,128)(2,1)S(1)}, u32[]{:S(2)}, u32[]{:S(2)}) async-start(bf16[8,256,128]{2,1,0:T(8,128)(2,1)} %bitcast.9), calls=%async_computation.1 | async-start | bytes 1048576 | tf_op jit(solution)/shard_map/all_to_all | solution.py:198
  93.6 301.1 %reduce-scatter.2.cloned.1.call-start = ((), (), s32[]{:S(2)}) async-start(), calls=%async_computation.9 | async-start | bytes 5242880 | tf_op jit(solution)/shard_map/reduce_scatter | solution.py:237
  102.5 14.2 %copy-start = (bf16[8,256,128]{2,1,0:T(8,128)(2,1)}, bf16[8,256,128]{2,1,0:T(8,128)(2,1)S(1)}, u32[]{:S(2)}) copy-start(bf16[8,256,128]{2,1,0:T(8,128)(2,1)S(1)} %all-to-all-done.1) | copy-start | bytes 1572868
Sparse Core Ops, SparseCore 0:
  46.5 66.2 all-gather.10
  115.2 53.8 all-gather.8
  171.4 53.6 all-gather.6
  227.3 53.7 all-gather.4
  340.6 54.1 reduce-scatter.1

commit v2 on v1

--- a/solution.py
+++ b/solution.py
@@ -167,23 +167,28 @@
     return qt.astype(jnp.int32), kt.astype(jnp.int32), mode, live, most
 
 
-def part_tables(qt, kt, mode, live, part, parts, size, nq):
+def chunk_tables(qt, kt, mode, live, chunk_id, per_chunk, size, nq):
     total = qt.shape[0]
-    pos = jnp.arange(total, dtype=jnp.int32)
-    chosen = live & (kt % parts == part)
-    n_sel = jnp.sum(chosen.astype(jnp.int32))
-    order = jnp.argsort(jnp.where(chosen, pos, total + pos))[:size].astype(jnp.int32)
+    chosen = live & (kt // per_chunk == chunk_id)
+    counts = jnp.cumsum(chosen.astype(jnp.int32))
+    n_sel = counts[-1]
     i = jnp.arange(size, dtype=jnp.int32)
+    order = jnp.minimum(jnp.sum((counts[None, :] <= i[:, None]).astype(jnp.int32), axis=1), total - 1)
     keep = i < n_sel
     tail = take(order, jnp.maximum(n_sel - 1, 0)[None])[0]
     src = jnp.where(keep, order, tail)
     any_sel = n_sel > 0
     qt_p = jnp.where(any_sel, take(qt, src), nq - 1)
-    kt_p = jnp.where(any_sel, take(kt, src), part)
+    kt_p = jnp.where(any_sel, take(kt, src), chunk_id * per_chunk)
     mode_p = jnp.where(keep, take(mode, src), 0)
     prev = jnp.concatenate([jnp.full((1,), -1, jnp.int32), qt_p[:-1]])
     first = ((i == 0) | (keep & (qt_p != prev))).astype(jnp.int32)
-    return qt_p, kt_p, kt_p // parts, first, mode_p.astype(jnp.int32)
+    return qt_p, kt_p, kt_p - chunk_id * per_chunk, first, mode_p.astype(jnp.int32)
+
+
+def ring_order(n):
+    half = n // 2
+    return [2 * y for y in range(half)] + [2 * y + 1 for y in reversed(range(half))]
 
 
 def per_device(queries, keys, values, doc_ids, span_start, span_end, out_weight):
@@ -197,9 +202,13 @@
     stacked = lax.all_to_all(jnp.stack([queries, keys, values]), "cl", 2, 1, tiled=True)
     q1 = lax.all_to_all(stacked[0], "cg", 0, 0, tiled=True)
     kv1 = jnp.concatenate([stacked[1], stacked[2]], axis=1)
-    parts = chunk // TK
-    kv_parts = [lax.all_gather(kv1[p * TK:(p + 1) * TK], "cg", axis=0, tiled=True) for p in range(parts)]
+    per_chunk = chunk // TK
     seq = chunk * n_cg
+    order = ring_order(n_cg)
+    place = [order.index(g) for g in range(n_cg)]
+    ring = [(order[i], order[(i + 1) % n_cg]) for i in range(n_cg)]
+    order_arr = jnp.asarray(order, jnp.int32)
+    my_place = take(jnp.asarray(place, jnp.int32), j[None])[0]
 
     count = doc_ids.shape[0]
     span_blocks = block_spans(span_start, span_end, count)
@@ -220,16 +229,22 @@
 
     qt, kt, mode, live, most = step_tables(doc_ids, span_blocks, span_end, qstart, piece, seq)
     nq = n_cg
-    size = nq * (-(-most // parts) + 1)
+    size = nq * per_chunk
     state = (
         jnp.full((chunk, 1), NEG, jnp.float32),
         jnp.zeros((chunk, 1), jnp.float32),
         jnp.zeros((chunk, HEAD_DIM), jnp.float32),
     )
-    for p in range(parts):
-        qt_p, kt_p, kb_p, first_p, mode_p = part_tables(qt, kt, mode, live, p, parts, size, nq)
+    kv_now = kv1
+    for step in range(n_cg):
+        if step + 1 < n_cg:
+            kv_next = lax.ppermute(kv_now, "cg", ring)
+        chunk_id = take(order_arr, ((my_place - step) % n_cg)[None])[0]
+        qt_p, kt_p, kb_p, first_p, mode_p = chunk_tables(qt, kt, mode, live, chunk_id, per_chunk, size, nq)
         tables = (qt_p, kt_p, kb_p, first_p, mode_p, qstart.astype(jnp.int32))
-        state = attend_part(tables, q1, kv_parts[p], qd, qs, kd, ks, state, piece)
+        state = attend_part(tables, q1, kv_now, qd, qs, kd, ks, state, piece)
+        if step + 1 < n_cg:
+            kv_now, state = lax.optimization_barrier((kv_next, state))
     m, l, acc = state
     att1 = (acc / l).astype(jnp.bfloat16)
     att0 = lax.all_to_all(att1, "cg", 0, 0, tiled=True)

time: 403 us -> 390 us (0.968)
  waiting for transfers between devices: 155 us -> 89.1 us
  blocking collectives: 54.2 us -> 22.3 us
  starting transfers between devices: 7.37 us -> 36.4 us
  between operations: 18.5 us -> 35.6 us
  Pallas kernels: 101 us -> 117 us
  other arithmetic: 42.4 us -> 54.6 us
  local copies, waits for them, and re-layouts: 15.6 us -> 23.8 us
    all_gather x4 -> x0, waiting for transfers between devices: 97.5 us -> none  [per_device(): lax.all_gather(kv1[p * TK:(p + 1) * TK], 'cg', axis=0, tiled=True)]
    all_to_all x1 -> x0, blocking collectives: 28.7 us -> none  [per_device(): lax.all_to_all(jnp.stack([queries, keys, values]), 'cl', 2, 1, tiled=True)]
    ppermute x0 -> x7, starting transfers between devices: none -> 25.3 us  [per_device(): kv_next = lax.ppermute(kv_now, 'cg', ring)]
    pallas_call x4 -> x8, Pallas kernels: 101 us -> 117 us  [attend_part(): pl.pallas_call(make_kernel(tq), out_shape=(jax.ShapeDtypeStruct(m.shape,...]
    ppermute x0 -> x7, waiting for transfers between devices: none -> 14.5 us  [per_device(): kv_next = lax.ppermute(kv_now, 'cg', ring)]
    sort x4 -> x0, other arithmetic: 12.7 us -> none  [part_tables(): jnp.argsort(jnp.where(chosen, pos, total + pos))[:size].astype(jnp.int32)]
    all_to_all x1, waiting for transfers between devices: 3.65 us -> 15 us  [per_device(): q1 = lax.all_to_all(stacked[0], 'cg', 0, 0, tiled=True)]
    select_n x13 -> x20, other arithmetic: 10.5 us -> 17.1 us  [the longest x8 9.73 us: chunk_tables(): src = jnp.where(keep, order, tail)]
  transfers between devices with their start and end apart: 6 -> 10, of which waited for: 6 -> 7; matrix products, arithmetic and copies ran while one was open for 11% -> 17% of each run, Pallas kernels for 19% -> 25%
where the time goes in v2:
time: 390 us; the launch traced here: 385 us
  Pallas kernels  117 us (30%)
  waiting for transfers between devices  89.1 us (23%)
  other arithmetic  54.6 us (14%)
  starting transfers between devices  36.4 us (9%)
  between operations  35.6 us (9%)
  local copies, waits for them, and re-layouts  23.8 us (6%)
  blocking collectives  22.3 us (6%)
  matrix products  6.49 us (2%)
    pallas_call x8, Pallas kernels, attend_part(): pl.pallas_call(make_kernel(tq), out_shape=(jax.ShapeDtypeStruct(m.shape,...  117 us
    reduce_scatter x1, waiting for transfers between devices, per_device(): lax.psum_scatter(jnp.dot(attended, out_weight, preferred_element_type=jnp...  59.7 us
    ppermute x7, starting transfers between devices, per_device(): kv_next = lax.ppermute(kv_now, 'cg', ring)  25.3 us
    all_to_all x1, waiting for transfers between devices, per_device(): q1 = lax.all_to_all(stacked[0], 'cg', 0, 0, tiled=True)  15 us
    ppermute x7, waiting for transfers between devices, per_device(): kv_next = lax.ppermute(kv_now, 'cg', ring)  14.5 us
    all_to_all x1, blocking collectives, per_device(): att0 = lax.all_to_all(att1, 'cg', 0, 0, tiled=True)  13.9 us
    select_n x8, other arithmetic, chunk_tables(): src = jnp.where(keep, order, tail)  9.73 us
    all_to_all x1, blocking collectives, per_device(): attended = lax.all_to_all(att0, 'cl', 0, 1, tiled=True)  8.37 us
  transfers between devices with their start and end apart: 10, of which 7 were waited for; matrix products, arithmetic and copies ran while one was open for 17% of the time, Pallas kernels for 25%

profile of v2, /device:TPU:1, one launch (start us, length us, event | category | flops | bytes accessed | tf_op | source)
XLA Modules:
  0.0 385.5 jit_solution(18020662525278908406)
XLA Ops:
  8.1 3.0 copy.141
  11.1 4.8 %all-to-all-start = ((bf16[3,512,512]{1,0,2:T(4,128)(2,1)}), bf16[3,512,512]{1,0,2:T(4,128)(2,1)S(1)}, u32[]{:S(2)}, u32[]{:S(2)}) async-start(bf16[3,512,512]{1,0,2:T(4,128)(2,1)} %copy.141), calls=%async_computation | async-start | bytes 4194304 | tf_op jit(solution)/shard_map/all_to_all | solution.py:202
  27.2 5.0 %compare_and_fusion.2 = (pred[176]{0:T(512)(128)(4,1)S(1)}, pred[176]{0:T(512)(128)(4,1)S(1)}, pred[176]{0:T(512)(128)(4,1)S(1)}, pred[176]{0:T(512)(128)(4,1)S(...) fusion(s32[176]{0:T(256)S(1)} %get-tuple-element.193, s32[]{:T(128)} %get-tuple-element.167, ...), kind=kLoop, calls=%fused_computation.97 | loop fusion | flops 2640 | bytes 1968 | tf_op jit(solution)/shard_map/and | solution.py:172
  68.2 2.6 copy.142
  70.8 2.3 fusion.50
  75.2 6.3 %all-to-all-start.1 = ((bf16[8,256,128]{2,1,0:T(8,128)(2,1)}), bf16[8,256,128]{2,1,0:T(8,128)(2,1)S(1)}, u32[]{:S(2)}, u32[]{:S(2)}) async-start(bf16[8,256,128]{2,1,0:T(8,128)(2,1)} %bitcast.12), calls=%async_computation.1 | async-start | bytes 1048576 | tf_op jit(solution)/shard_map/all_to_all | solution.py:203
  88.2 1.9 or_convert_fusion.6
  90.1 15.0 %all-to-all-done.1 = bf16[8,256,128]{2,1,0:T(8,128)(2,1)S(1)} async-done(((bf16[8,256,128]{2,1,0:T(8,128)(2,1)}), bf16[8,256,128]{2,1,0:T(8,128)(2,1)S(1)}, u32[]{:S(2)}, u32[]{:S(2)}) %all-to-all-start.1) | async-done | bytes 524320 | tf_op jit(solution)/shard_map/all_to_all | solution.py:203
  109.1 12.0 %shard_map.91 = (f32[2048,1]{1,0:T(8,128)}, f32[2048,1]{1,0:T(8,128)}, f32[2048,128]{1,0:T(8,128)}) custom-call(s32[32]{0:T(128)} %copy-done.12, s32[32]{0:T(128)} %get-tuple-element.189.kt_ref, s32[32]{0:T(128)} %get-tuple-element.188.kb_ref, s32[32]{0:T(128)} %get-tuple-element.214.first_ref, ...), custom_call_target="tpu_custom_call", output_to_operand_aliasing={{0}: (13, {}), {1}: (14, {}), {2}: (15, {})} | custom-call | tf_op jit(solution)/shard_map/pallas_call | solution.py:113
  121.1 10.2 %collective-permute-start.1 = (bf16[2048,256]{1,0:T(8,128)(2,1)S(1)}, bf16[2048,256]{1,0:T(8,128)(2,1)S(1)}, u32[]{:S(2)}, u32[]{:S(2)}) collective-permute-start(bf16[2048,256]{1,0:T(8,128)(2,1)S(1)} %collective-permute-done.k_ref.v_ref), channel_id=1, source_target_pairs={{0,32},{32,64},{64,96},{96,112},{112,80},{80,48},{48,16},{16,0},{1... | collective-permute-start | bytes 3145736 | tf_op jit(solution)/shard_map/ppermute | solution.py:241
  131.9 1.9 or_convert_fusion.4
  135.6 11.3 %shard_map.92 = (f32[2048,1]{1,0:T(8,128)}, f32[2048,1]{1,0:T(8,128)}, f32[2048,128]{1,0:T(8,128)}) custom-call(s32[32]{0:T(128)} %copy-done.16, s32[32]{0:T(128)} %get-tuple-element.187.kt_ref, s32[32]{0:T(128)} %get-tuple-element.186.kb_ref, s32[32]{0:T(128)} %get-tuple-element.213.first_ref, ...), custom_call_target="tpu_custom_call", output_to_operand_aliasing={{0}: (13, {}), {1}: (14, {}), {2}: (15, {})} | custom-call | tf_op jit(solution)/shard_map/pallas_call | solution.py:113
  146.9 3.8 collective-permute-done.1.k_ref.v_ref
  150.8 2.2 collective-permute-start.2
  156.0 19.1 %shard_map.93 = (f32[2048,1]{1,0:T(8,128)}, f32[2048,1]{1,0:T(8,128)}, f32[2048,128]{1,0:T(8,128)}) custom-call(s32[32]{0:T(128)} %copy-done.15, s32[32]{0:T(128)} %get-tuple-element.185.kt_ref, s32[32]{0:T(128)} %get-tuple-element.184.kb_ref, s32[32]{0:T(128)} %get-tuple-element.212.first_ref, ...), custom_call_target="tpu_custom_call", output_to_operand_aliasing={{0}: (13, {}), {1}: (14, {}), {2}: (15, {})} | custom-call | tf_op jit(solution)/shard_map/pallas_call | solution.py:113
  176.7 1.9 or_convert_fusion.2
  180.5 13.8 %shard_map.94 = (f32[2048,1]{1,0:T(8,128)}, f32[2048,1]{1,0:T(8,128)}, f32[2048,128]{1,0:T(8,128)}) custom-call(s32[32]{0:T(128)} %copy-done.17, s32[32]{0:T(128)} %get-tuple-element.183.kt_ref, s32[32]{0:T(128)} %get-tuple-element.182.kb_ref, s32[32]{0:T(128)} %get-tuple-element.211.first_ref, ...), custom_call_target="tpu_custom_call", output_to_operand_aliasing={{0}: (13, {}), {1}: (14, {}), {2}: (15, {})} | custom-call | tf_op jit(solution)/shard_map/pallas_call | solution.py:113
  194.2 2.2 collective-permute-done.3.k_ref.v_ref
  196.5 6.1 %collective-permute-start.4 = (bf16[2048,256]{1,0:T(8,128)(2,1)S(1)}, bf16[2048,256]{1,0:T(8,128)(2,1)S(1)}, u32[]{:S(2)}, u32[]{:S(2)}) collective-permute-start(bf16[2048,256]{1,0:T(8,128)(2,1)S(1)} %collective-permute-done.3.k_ref.v_ref), channel_id=1, source_target_pairs={{0,32},{32,64},{64,96},{96,112},{112,80},{80,48},{48,16},{16,0},{1... | collective-permute-start | bytes 3145736 | tf_op jit(solution)/shard_map/ppermute | solution.py:241
  205.6 11.3 %shard_map.95 = (f32[2048,1]{1,0:T(8,128)}, f32[2048,1]{1,0:T(8,128)}, f32[2048,128]{1,0:T(8,128)}) custom-call(s32[32]{0:T(128)} %copy-done.14, s32[32]{0:T(128)} %get-tuple-element.181.kt_ref, s32[32]{0:T(128)} %get-tuple-element.180.kb_ref, s32[32]{0:T(128)} %get-tuple-element.210.first_ref, ...), custom_call_target="tpu_custom_call", output_to_operand_aliasing={{0}: (13, {}), {1}: (14, {}), {2}: (15, {})} | custom-call | tf_op jit(solution)/shard_map/pallas_call | solution.py:113
  217.0 3.8 collective-permute-done.4.k_ref.v_ref
  220.8 2.2 collective-permute-start.5
  223.6 1.9 or_convert_fusion
  227.3 11.3 %shard_map.96 = (f32[2048,1]{1,0:T(8,128)}, f32[2048,1]{1,0:T(8,128)}, f32[2048,128]{1,0:T(8,128)}) custom-call(s32[32]{0:T(128)} %copy-done.18, s32[32]{0:T(128)} %get-tuple-element.179.kt_ref, s32[32]{0:T(128)} %get-tuple-element.178.kb_ref, s32[32]{0:T(128)} %get-tuple-element.209.first_ref, ...), custom_call_target="tpu_custom_call", output_to_operand_aliasing={{0}: (13, {}), {1}: (14, {}), {2}: (15, {})} | custom-call | tf_op jit(solution)/shard_map/pallas_call | solution.py:113
  238.6 3.8 collective-permute-done.5.k_ref.v_ref
  242.4 2.2 collective-permute-start.6
  246.9 16.4 %shard_map.97 = (f32[2048,1]{1,0:T(8,128)}, f32[2048,1]{1,0:T(8,128)}, f32[2048,128]{1,0:T(8,128)}) custom-call(s32[32]{0:T(128)} %copy-done.13, s32[32]{0:T(128)} %get-tuple-element.177.kt_ref, s32[32]{0:T(128)} %get-tuple-element.176.kb_ref, s32[32]{0:T(128)} %get-tuple-element.208.first_ref, ...), custom_call_target="tpu_custom_call", output_to_operand_aliasing={{0}: (13, {}), {1}: (14, {}), {2}: (15, {})} | custom-call | tf_op jit(solution)/shard_map/pallas_call | solution.py:113
  265.0 21.7 %shard_map.98 = (f32[2048,1]{1,0:T(8,128)}, f32[2048,1]{1,0:T(8,128)}, f32[2048,128]{1,0:T(8,128)}) custom-call(s32[32]{0:T(128)} %copy-done.11, s32[32]{0:T(128)} %get-tuple-element.191.kt_ref, s32[32]{0:T(128)} %get-tuple-element.190.kb_ref, s32[32]{0:T(128)} %get-tuple-element.215.first_ref, ...), custom_call_target="tpu_custom_call", output_to_operand_aliasing={{0}: (13, {}), {1}: (14, {}), {2}: (15, {})} | custom-call | tf_op jit(solution)/shard_map/pallas_call | solution.py:113
  289.9 13.9 %all_to_all.54 = bf16[8,256,128]{2,1,0:T(8,128)(2,1)S(1)} all-to-all(bf16[8,256,128]{2,1,0:T(8,128)(2,1)S(1)} %bitcast.144), channel_id=1, replica_groups=mesh['cg'=8,'cl'=4,'tp'=4] {'cg'}, dimensions={0} | all-to-all | bytes 1048576 | tf_op jit(solution)/shard_map/all_to_all | solution.py:250
  303.9 8.4 %all_to_all.55 = bf16[4,512,128]{2,1,0:T(8,128)(2,1)S(1)} all-to-all(bf16[4,512,128]{2,1,0:T(8,128)(2,1)S(1)} %bitcast.146), channel_id=1, replica_groups=mesh['cg'=8,'cl'=4,'tp'=4] {'cl'}, dimensions={0} | all-to-all | bytes 1048576 | tf_op jit(solution)/shard_map/all_to_all | solution.py:251
  312.4 6.5 %convolution_convert_fusion = bf16[512,4096]{1,0:T(8,128)(2,1)} fusion(bf16[512,512]{0,1:T(8,128)(2,1)S(1)} %bitcast.145, bf16[512,4096]{1,0:T(8,128)(2,1)} %param.15), kind=kOutput, calls=%fused_computation | convolution fusion | flops 2149580800 | bytes 8912896 | tf_op jit(solution)/shard_map/dot_general | solution.py:253
  318.9 59.7 %reduce-scatter.2.cloned.1.call-done = bf16[128,4096]{1,0:T(8,128)(2,1)} async-done(((bf16[512,4096]{1,0:T(8,128)(2,1)}), bf16[128,4096]{1,0:T(8,128)(2,1)}) %reduce-scatter.2.cloned.1.call-update) | async-done | bytes 1048592 | tf_op jit(solution)/shard_map/reduce_scatter | solution.py:252
  (208 shorter events, 61.2 us)
Async XLA Ops:
  11.1 4.8 %copy-start.22 = (s32[8]{0:T(128)S(1)}, s32[8]{0:T(128)}, u32[]{:S(2)}) copy-start(s32[8]{0:T(128)} %constant.194.clone) | copy-start | bytes 100
  11.1 12.1 %copy-start.20 = (s32[16]{0:T(128)S(1)}, s32[16]{0:T(128)}, u32[]{:S(2)}) copy-start(s32[16]{0:T(128)} %param.13) | copy-start | bytes 196
  11.1 12.1 %copy-start.21 = (s32[16]{0:T(128)S(1)}, s32[16]{0:T(128)}, u32[]{:S(2)}) copy-start(s32[16]{0:T(128)} %param.14) | copy-start | bytes 196
  11.1 12.3 %copy-start.10 = (s32[128]{0:T(128)S(1)}, s32[128]{0:T(128)}, u32[]{:S(2)}) copy-start(s32[128]{0:T(128)} %param.12) | copy-start | bytes 1540
  11.1 14.0 %copy-start.19 = (s32[8]{0:T(128)S(1)}, s32[8]{0:T(128)}, u32[]{:S(2)}) copy-start(s32[8]{0:T(128)} %constant.193.clone) | copy-start | bytes 100
  11.1 57.0 %all-to-all-start = ((bf16[3,512,512]{1,0,2:T(4,128)(2,1)}), bf16[3,512,512]{1,0,2:T(4,128)(2,1)S(1)}, u32[]{:S(2)}, u32[]{:S(2)}) async-start(bf16[3,512,512]{1,0,2:T(4,128)(2,1)} %copy.141), calls=%async_computation | async-start | bytes 4194304 | tf_op jit(solution)/shard_map/all_to_all | solution.py:202
  23.1 47.7 %copy-start.9 = (s32[8]{0:T(128)}, s32[8]{0:T(128)S(1)}, u32[]{:S(2)}) copy-start(s32[8]{0:T(128)S(1)} %multiply_add_fusion.qstart_ref) | copy-start | bytes 100
  67.6 20.6 %copy-start.12 = (s32[32]{0:T(128)}, s32[32]{0:T(128)S(1)}, u32[]{:S(2)}) copy-start(s32[32]{0:T(128)S(1)} %broadcast_select_fusion.13.qt_ref) | copy-start | bytes 388
  73.2 33.8 %copy-start.1 = (bf16[2048,256]{1,0:T(8,128)(2,1)}, bf16[2048,256]{1,0:T(8,128)(2,1)S(1)}, u32[]{:S(2)}) copy-start(bf16[2048,256]{1,0:T(8,128)(2,1)S(1)} %pad_maximum_fusion.1.k_ref.v_ref) | copy-start | bytes 3145732
  73.2 47.9 %collective-permute-start = (bf16[2048,256]{1,0:T(8,128)(2,1)S(1)}, bf16[2048,256]{1,0:T(8,128)(2,1)S(1)}, u32[]{:S(2)}, u32[]{:S(2)}) collective-permute-start(bf16[2048,256]{1,0:T(8,128)(2,1)S(1)} %pad_maximum_fusion.1.k_ref.v_ref), channel_id=1, source_target_pairs={{0,32},{32,64},{64,96},{96,112},{112,80},{80,48},{48,16},{16,0},{1... | collective-permute-start | bytes 3145736 | tf_op jit(solution)/shard_map/ppermute | solution.py:241
  74.5 32.4 %copy-start.11 = (s32[32]{0:T(128)}, s32[32]{0:T(128)S(1)}, u32[]{:S(2)}) copy-start(s32[32]{0:T(128)S(1)} %broadcast_select_fusion.15.qt_ref) | copy-start | bytes 388
  75.2 29.8 %all-to-all-start.1 = ((bf16[8,256,128]{2,1,0:T(8,128)(2,1)}), bf16[8,256,128]{2,1,0:T(8,128)(2,1)S(1)}, u32[]{:S(2)}, u32[]{:S(2)}) async-start(bf16[8,256,128]{2,1,0:T(8,128)(2,1)} %bitcast.12), calls=%async_computation.1 | async-start | bytes 1048576 | tf_op jit(solution)/shard_map/all_to_all | solution.py:203
  81.5 297.1 %reduce-scatter.2.cloned.1.call-start = ((), (), s32[]{:S(2)}) async-start(), calls=%async_computation.5 | async-start | bytes 5242880 | tf_op jit(solution)/shard_map/reduce_scatter | solution.py:252
  105.1 4.0 %copy-start = (bf16[8,256,128]{2,1,0:T(8,128)(2,1)}, bf16[8,256,128]{2,1,0:T(8,128)(2,1)S(1)}, u32[]{:S(2)}) copy-start(bf16[8,256,128]{2,1,0:T(8,128)(2,1)S(1)} %all-to-all-done.1) | copy-start | bytes 1572868
  121.1 14.5 %copy-start.2 = (bf16[2048,256]{1,0:T(8,128)(2,1)}, bf16[2048,256]{1,0:T(8,128)(2,1)S(1)}, u32[]{:S(2)}) copy-start(bf16[2048,256]{1,0:T(8,128)(2,1)S(1)} %collective-permute-done.k_ref.v_ref) | copy-start | bytes 3145732
  121.1 29.7 %collective-permute-start.1 = (bf16[2048,256]{1,0:T(8,128)(2,1)S(1)}, bf16[2048,256]{1,0:T(8,128)(2,1)S(1)}, u32[]{:S(2)}, u32[]{:S(2)}) collective-permute-start(bf16[2048,256]{1,0:T(8,128)(2,1)S(1)} %collective-permute-done.k_ref.v_ref), channel_id=1, source_target_pairs={{0,32},{32,64},{64,96},{96,112},{112,80},{80,48},{48,16},{16,0},{1... | collective-permute-start | bytes 3145736 | tf_op jit(solution)/shard_map/ppermute | solution.py:241
  131.3 4.3 %copy-start.16 = (s32[32]{0:T(128)}, s32[32]{0:T(128)S(1)}, u32[]{:S(2)}) copy-start(s32[32]{0:T(128)S(1)} %broadcast_select_fusion.11.qt_ref) | copy-start | bytes 388
  131.3 15.6 %copy-start.15 = (s32[32]{0:T(128)}, s32[32]{0:T(128)S(1)}, u32[]{:S(2)}) copy-start(s32[32]{0:T(128)S(1)} %broadcast_select_fusion.9.qt_ref) | copy-start | bytes 388
  150.8 5.3 %copy-start.6 = (bf16[2048,256]{1,0:T(8,128)(2,1)}, bf16[2048,256]{1,0:T(8,128)(2,1)S(1)}, u32[]{:S(2)}) copy-start(bf16[2048,256]{1,0:T(8,128)(2,1)S(1)} %collective-permute-done.1.k_ref.v_ref) | copy-start | bytes 3145732
  150.8 24.3 %collective-permute-start.2 = (bf16[2048,256]{1,0:T(8,128)(2,1)S(1)}, bf16[2048,256]{1,0:T(8,128)(2,1)S(1)}, u32[]{:S(2)}, u32[]{:S(2)}) collective-permute-start(bf16[2048,256]{1,0:T(8,128)(2,1)S(1)} %collective-permute-done.1.k_ref.v_ref), channel_id=1, source_target_pairs={{0,32},{32,64},{64,96},{96,112},{112,80},{80,48},{48,16},{16,0},{1... | collective-permute-start | bytes 3145736 | tf_op jit(solution)/shard_map/ppermute | solution.py:241
  175.1 5.3 %copy-start.7 = (bf16[2048,256]{1,0:T(8,128)(2,1)}, bf16[2048,256]{1,0:T(8,128)(2,1)S(1)}, u32[]{:S(2)}) copy-start(bf16[2048,256]{1,0:T(8,128)(2,1)S(1)} %collective-permute-done.2.k_ref.v_ref) | copy-start | bytes 3145732
  175.1 21.3 %collective-permute-start.3 = (bf16[2048,256]{1,0:T(8,128)(2,1)S(1)}, bf16[2048,256]{1,0:T(8,128)(2,1)S(1)}, u32[]{:S(2)}, u32[]{:S(2)}) collective-permute-start(bf16[2048,256]{1,0:T(8,128)(2,1)S(1)} %collective-permute-done.2.k_ref.v_ref), channel_id=1, source_target_pairs={{0,32},{32,64},{64,96},{96,112},{112,80},{80,48},{48,16},{16,0},{1... | collective-permute-start | bytes 3145736 | tf_op jit(solution)/shard_map/ppermute | solution.py:241
  176.2 4.3 %copy-start.17 = (s32[32]{0:T(128)}, s32[32]{0:T(128)S(1)}, u32[]{:S(2)}) copy-start(s32[32]{0:T(128)S(1)} %broadcast_select_fusion.7.qt_ref) | copy-start | bytes 388
  176.2 18.0 %copy-start.14 = (s32[32]{0:T(128)}, s32[32]{0:T(128)S(1)}, u32[]{:S(2)}) copy-start(s32[32]{0:T(128)S(1)} %broadcast_select_fusion.5.qt_ref) | copy-start | bytes 388
  196.5 9.2 %copy-start.5 = (bf16[2048,256]{1,0:T(8,128)(2,1)}, bf16[2048,256]{1,0:T(8,128)(2,1)S(1)}, u32[]{:S(2)}) copy-start(bf16[2048,256]{1,0:T(8,128)(2,1)S(1)} %collective-permute-done.3.k_ref.v_ref) | copy-start | bytes 3145732
  196.5 24.3 %collective-permute-start.4 = (bf16[2048,256]{1,0:T(8,128)(2,1)S(1)}, bf16[2048,256]{1,0:T(8,128)(2,1)S(1)}, u32[]{:S(2)}, u32[]{:S(2)}) collective-permute-start(bf16[2048,256]{1,0:T(8,128)(2,1)S(1)} %collective-permute-done.3.k_ref.v_ref), channel_id=1, source_target_pairs={{0,32},{32,64},{64,96},{96,112},{112,80},{80,48},{48,16},{16,0},{1... | collective-permute-start | bytes 3145736 | tf_op jit(solution)/shard_map/ppermute | solution.py:241
  220.8 6.5 %copy-start.4 = (bf16[2048,256]{1,0:T(8,128)(2,1)}, bf16[2048,256]{1,0:T(8,128)(2,1)S(1)}, u32[]{:S(2)}) copy-start(bf16[2048,256]{1,0:T(8,128)(2,1)S(1)} %collective-permute-done.4.k_ref.v_ref) | copy-start | bytes 3145732
  220.8 21.6 %collective-permute-start.5 = (bf16[2048,256]{1,0:T(8,128)(2,1)S(1)}, bf16[2048,256]{1,0:T(8,128)(2,1)S(1)}, u32[]{:S(2)}, u32[]{:S(2)}) collective-permute-start(bf16[2048,256]{1,0:T(8,128)(2,1)S(1)} %collective-permute-done.4.k_ref.v_ref), channel_id=1, source_target_pairs={{0,32},{32,64},{64,96},{96,112},{112,80},{80,48},{48,16},{16,0},{1... | collective-permute-start | bytes 3145736 | tf_op jit(solution)/shard_map/ppermute | solution.py:241
  223.0 15.6 %copy-start.13 = (s32[32]{0:T(128)}, s32[32]{0:T(128)S(1)}, u32[]{:S(2)}) copy-start(s32[32]{0:T(128)S(1)} %broadcast_select_fusion.1.qt_ref) | copy-start | bytes 388
  223.0 4.3 %copy-start.18 = (s32[32]{0:T(128)}, s32[32]{0:T(128)S(1)}, u32[]{:S(2)}) copy-start(s32[32]{0:T(128)S(1)} %broadcast_select_fusion.3.qt_ref) | copy-start | bytes 388
  242.4 4.5 %copy-start.3 = (bf16[2048,256]{1,0:T(8,128)(2,1)}, bf16[2048,256]{1,0:T(8,128)(2,1)S(1)}, u32[]{:S(2)}) copy-start(bf16[2048,256]{1,0:T(8,128)(2,1)S(1)} %collective-permute-done.5.k_ref.v_ref) | copy-start | bytes 3145732
  242.4 21.6 %collective-permute-start.6 = (bf16[2048,256]{1,0:T(8,128)(2,1)S(1)}, bf16[2048,256]{1,0:T(8,128)(2,1)S(1)}, u32[]{:S(2)}, u32[]{:S(2)}) collective-permute-start(bf16[2048,256]{1,0:T(8,128)(2,1)S(1)} %collective-permute-done.5.k_ref.v_ref), channel_id=1, source_target_pairs={{0,32},{32,64},{64,96},{96,112},{112,80},{80,48},{48,16},{16,0},{1... | collective-permute-start | bytes 3145736 | tf_op jit(solution)/shard_map/ppermute | solution.py:241
  (1 other events, 1.0 us)
Sparse Core Ops, SparseCore 0:
  319.1 59.5 reduce-scatter.1

commit v3 on v0

--- a/solution.py
+++ b/solution.py
@@ -196,34 +196,37 @@
     att1 = attend_head(tables, q1, kv_all, qd, qs, kd, ks, piece)
     att0 = lax.all_to_all(att1, "cg", 0, 0, tiled=True)
     attended = lax.all_to_all(att0, "cl", 0, 1, tiled=True)
-    mixed = lax.psum_scatter(
-        jnp.dot(attended, out_weight, preferred_element_type=jnp.float32).astype(jnp.bfloat16),
-        "tp",
-        scatter_dimension=0,
-        tiled=True,
-    )
-    return mixed
+    tc = lax.axis_index("tc")
+    th = lax.axis_index("th")
+    swap = [(0, 1), (1, 0)]
+    w_other = lax.ppermute(out_weight, "tc", swap)
+    w_pair = jnp.where(tc == 0, jnp.concatenate([out_weight, w_other], axis=0),
+                       jnp.concatenate([w_other, out_weight], axis=0))
+    quarter = rows // 4
+    blocks = attended.reshape(2, 2, quarter, local_width)
+    keep = lax.dynamic_index_in_dim(blocks, tc, axis=1, keepdims=False)
+    give = lax.dynamic_index_in_dim(blocks, 1 - tc, axis=1, keepdims=False)
+    got = lax.ppermute(give, "tc", swap)
+    a_pair = jnp.where(tc == 0, jnp.concatenate([keep, got], axis=2), jnp.concatenate([got, keep], axis=2))
+    partial = jnp.dot(a_pair.reshape(2 * quarter, 2 * local_width), w_pair,
+                      preferred_element_type=jnp.float32).reshape(2, quarter, -1)
+    mine_half = lax.dynamic_index_in_dim(partial, th, axis=0, keepdims=False)
+    other_half = lax.dynamic_index_in_dim(partial, 1 - th, axis=0, keepdims=False).astype(jnp.bfloat16)
+    recv = lax.ppermute(other_half, "th", swap)
+    return (mine_half + recv.astype(jnp.float32)).astype(jnp.bfloat16)
 
 
 def solution(mesh):
     n_ctx = mesh.shape["ctx"]
-    n_tp = mesh.shape["tp"]
     group = 4
-    inner = Mesh(np.asarray(mesh.devices).reshape(n_ctx // group, group, n_tp), ("cg", "cl", "tp"))
+    inner = Mesh(np.asarray(mesh.devices).reshape(n_ctx // group, group, 2, 2), ("cg", "cl", "th", "tc"))
     out_sharding = NamedSharding(mesh, P(("ctx", "tp"), None))
+    split = P(("cg", "cl"), ("th", "tc"))
     body = jax.shard_map(
         per_device,
         mesh=inner,
-        in_specs=(
-            P(("cg", "cl"), "tp"),
-            P(("cg", "cl"), "tp"),
-            P(("cg", "cl"), "tp"),
-            P(),
-            P(),
-            P(),
-            P("tp", None),
-        ),
-        out_specs=P(("cg", "cl", "tp"), None),
+        in_specs=(split, split, split, P(), P(), P(), P(("th", "tc"), None)),
+        out_specs=P(("cg", "cl", "th", "tc"), None),
         check_vma=False,
     )
 

time: 329 us -> 319 us (0.970)
  waiting for transfers between devices: 150 us -> 127 us
  starting transfers between devices: 7.25 us -> 19.4 us
  blocking collectives: 55.7 us -> 51.6 us
    reduce_scatter x1 -> x0, waiting for transfers between devices: 52.5 us -> none  [per_device(): lax.psum_scatter(jnp.dot(attended, out_weight, preferred_element_type=jnp...]
    ppermute x0 -> x3, waiting for transfers between devices: none -> 24.6 us  [the longest x1 23.4 us: per_device(): recv = lax.ppermute(other_half, 'th', swap)]
    ppermute x0 -> x3, starting transfers between devices: none -> 8.75 us  [the longest x1 4 us: per_device(): got = lax.ppermute(give, 'tc', swap)]
    all_to_all x1 -> x0, blocking collectives: 8.37 us -> none  [per_device(): attended = lax.all_to_all(att0, 'cl', 0, 1, tiled=True)]
    all_gather x1, waiting for transfers between devices: 93.7 us -> 86.7 us  [per_device(): kv_all = lax.all_gather(kv1, 'cg', axis=0, tiled=True)]
    all_to_all x1, waiting for transfers between devices: 3.91 us -> 10.1 us  [per_device(): q1 = lax.all_to_all(stacked[0], 'cg', 0, 0, tiled=True)]
    all_to_all x0 -> x1, waiting for transfers between devices: none -> 5.45 us  [per_device(): attended = lax.all_to_all(att0, 'cl', 0, 1, tiled=True)]
    all_to_all x1, blocking collectives: 18.6 us -> 22.9 us  [per_device(): att0 = lax.all_to_all(att1, 'cg', 0, 0, tiled=True)]
  transfers between devices with their start and end apart: 3 -> 6, of which waited for: 3 -> 5; matrix products, arithmetic and copies ran while one was open for 3% -> 3% of each run, Pallas kernels for 0% -> 23%
where the time goes in v3:
time: 319 us
  waiting for transfers between devices  127 us (40%)
  Pallas kernels  73.1 us (23%)
  blocking collectives  51.6 us (16%)
  starting transfers between devices  19.4 us (6%)
  local copies, waits for them, and re-layouts  15 us (5%)
  between operations  13.6 us (4%)
  other arithmetic  11.9 us (4%)
  matrix products  7.45 us (2%)
    all_gather x1, waiting for transfers between devices, per_device(): kv_all = lax.all_gather(kv1, 'cg', axis=0, tiled=True)  86.7 us
    pallas_call x1, Pallas kernels, attend_head(): pl.pallas_call(make_kernel(tq), out_shape=jax.ShapeDtypeStruct(q.shape, j...  73.1 us
    all_to_all x1, blocking collectives, per_device(): lax.all_to_all(jnp.stack([queries, keys, values]), 'cl', 2, 1, tiled=True)  28.7 us
    ppermute x1, waiting for transfers between devices, per_device(): recv = lax.ppermute(other_half, 'th', swap)  23.4 us
    all_to_all x1, blocking collectives, per_device(): att0 = lax.all_to_all(att1, 'cg', 0, 0, tiled=True)  22.9 us
    all_to_all x1, waiting for transfers between devices, per_device(): q1 = lax.all_to_all(stacked[0], 'cg', 0, 0, tiled=True)  10.1 us
    dot_general x1, matrix products, per_device(): jnp.dot(a_pair.reshape(2 * quarter, 2 * local_width), w_pair, preferred_e...  7.45 us
    all_to_all x1, starting transfers between devices, per_device(): q1 = lax.all_to_all(stacked[0], 'cg', 0, 0, tiled=True)  7.21 us
  transfers between devices with their start and end apart: 6, of which 5 were waited for; matrix products, arithmetic and copies ran while one was open for 3% of the time, Pallas kernels for 23%

profile of v3, /device:TPU:1, one launch (start us, length us, event | category | flops | bytes accessed | tf_op | source)
XLA Modules:
  0.0 318.9 jit_solution(2300525595618764828)
XLA Ops:
  6.5 2.7 pad_maximum_fusion
  9.2 3.2 %copy.38 = bf16[3,512,512]{1,0,2:T(4,128)(2,1)S(1)} copy(bf16[3,512,512]{2,1,0:T(8,128)(2,1)} %pad_maximum_fusion) | data formatting | bytes 3145728 | tf_op jit(solution)/shard_map/stack | solution.py:172
  12.5 28.7 %all_to_all.51 = bf16[3,512,512]{1,0,2:T(4,128)(2,1)} all-to-all(bf16[3,512,512]{1,0,2:T(4,128)(2,1)S(1)} %copy.38), channel_id=1, replica_groups=mesh['cg'=8,'cl'=4,'th'=2,'tc'=2] {'cl'}, dimensions={2} | all-to-all | bytes 3145728 | tf_op jit(solution)/shard_map/all_to_all | solution.py:172
  41.2 3.3 %copy.39 = bf16[3,512,4,128]{3,1,2,0:T(8,128)(2,1)S(1)} copy(bf16[3,512,4,128]{1,0,3,2:T(4,128)(2,1)} %bitcast.64) | data formatting | bytes 3145728 | tf_op jit(solution)/shard_map/all_to_all | solution.py:172
  44.5 0.9 fusion.24
  45.4 1.1 pad_maximum_fusion.1
  46.5 2.2 collective-permute-start.1
  49.5 0.2 select_reduce_fusion.3
  50.0 0.6 slice.22
  51.1 0.6 broadcast_multiply_fusion
  51.8 0.4 select_reduce_fusion
  52.5 0.7 compare_select_fusion.ks_ref
  53.2 7.2 %all-to-all-start.1 = ((bf16[8,256,128]{2,1,0:T(8,128)(2,1)}), bf16[8,256,128]{2,1,0:T(8,128)(2,1)S(1)}, u32[]{:S(2)}, u32[]{:S(2)}) async-start(bf16[8,256,128]{2,1,0:T(8,128)(2,1)} %bitcast.9), calls=%async_computation.1 | async-start | bytes 1048576 | tf_op jit(solution)/shard_map/all_to_all | solution.py:173
  60.5 1.4 copy.46
  61.9 1.3 copy.48
  63.2 1.2 and_convert_fusion
  64.5 1.2 fusion.16.mode_ref
  65.6 10.1 %all-to-all-done.1 = bf16[8,256,128]{2,1,0:T(8,128)(2,1)S(1)} async-done(((bf16[8,256,128]{2,1,0:T(8,128)(2,1)}), bf16[8,256,128]{2,1,0:T(8,128)(2,1)S(1)}, u32[]{:S(2)}, u32[]{:S(2)}) %all-to-all-start.1) | async-done | bytes 524320 | tf_op jit(solution)/shard_map/all_to_all | solution.py:173
  75.7 86.7 %all-gather.2.cloned.1.call-done.k_ref.v_ref = bf16[16384,256]{1,0:T(8,128)(2,1)} async-done(((bf16[2048,256]{1,0:T(8,128)(2,1)}), bf16[16384,256]{1,0:T(8,128)(2,1)}) %all-gather.2.cloned.1.call-update) | async-done | bytes 8388624 | tf_op jit(solution)/shard_map/all_gather | solution.py:175
  162.4 0.7 eq.64
  163.1 73.1 %shard_map.73 = bf16[2048,128]{1,0:T(8,128)(2,1)} custom-call(s32[176]{0:T(256)} %copy-done.3, s32[176]{0:T(256)} %copy-done.4, s32[176]{0:T(256)} %get-tuple-element.29.first_ref, s32[176]{0:T(256)} %get-tuple-element.28.last_ref, s32[176]{0:T(256)} %fusion.16.mode_ref, s32[8]{0:T(128)} %copy-done.5, bf16[2048,128]{1,0:T(8,128)(2,1)} %bitcast.68, ...), custom_call_target="tpu_custom_call" | custom-call | tf_op jit(solution)/shard_map/pallas_call | solution.py:112
  236.2 22.9 %all_to_all.52 = bf16[8,256,128]{2,1,0:T(8,128)(2,1)} all-to-all(bf16[8,256,128]{2,1,0:T(8,128)(2,1)} %bitcast.69), channel_id=1, replica_groups=mesh['cg'=8,'cl'=4,'th'=2,'tc'=2] {'cg'}, dimensions={0} | all-to-all | bytes 1048576 | tf_op jit(solution)/shard_map/all_to_all | solution.py:197
  259.0 3.5 %all-to-all-start.3 = ((bf16[4,512,128]{2,1,0:T(8,128)(2,1)}), bf16[4,512,128]{2,1,0:T(8,128)(2,1)S(1)}, u32[]{:S(2)}, u32[]{:S(2)}) async-start(bf16[4,512,128]{2,1,0:T(8,128)(2,1)} %bitcast.18), calls=%async_computation.3 | async-start | bytes 1048576 | tf_op jit(solution)/shard_map/all_to_all | solution.py:198
  262.5 5.4 %all-to-all-done.3 = bf16[4,512,128]{2,1,0:T(8,128)(2,1)S(1)} async-done(((bf16[4,512,128]{2,1,0:T(8,128)(2,1)}), bf16[4,512,128]{2,1,0:T(8,128)(2,1)S(1)}, u32[]{:S(2)}, u32[]{:S(2)}) %all-to-all-start.3) | async-done | bytes 524320 | tf_op jit(solution)/shard_map/all_to_all | solution.py:198
  268.0 0.4 copy.44
  268.6 4.0 %collective-permute-start = (bf16[2,128,512]{2,1,0:T(8,128)(2,1)S(1)}, bf16[2,128,512]{2,1,0:T(8,128)(2,1)S(1)}, u32[]{:S(2)}, u32[]{:S(2)}) collective-permute-start(bf16[2,128,512]{2,1,0:T(8,128)(2,1)S(1)} %get-tuple-element.27), channel_id=1, source_target_pairs={{0,1},{1,0},{2,3},{3,2},{4,5},{5,4},{6,7},{7,6},{8,9},{9,8},{10,11... | collective-permute-start | bytes 786440 | tf_op jit(solution)/shard_map/ppermute | solution.py:209
  272.6 1.2 collective-permute-done
  273.8 7.5 %fusion.1 = f32[2,128,4096]{2,1,0:T(8,128)S(1)} fusion(bf16[512,4096]{1,0:T(8,128)(2,1)} %collective-permute-done.1, bf16[512,4096]{1,0:T(8,128)(2,1)} %param.13, pred[]{:T(512)S(6)} %eq.57, bf16[2,128,512]{2,1,0:T(8,128)(2,1)S(1)} %collective-permute-done, bf16[2,128,512]{2,1,0:T(8,128)(2,1)S(1)} %get-tuple-element.26), kind=kOutput, calls=%fused_computation.2 | convolution fusion | flops 2187591680 | bytes 13107201 | tf_op jit(solution)/shard_map/dot_general | solution.py:211
  281.3 1.9 copy-done
  283.3 2.5 collective-permute-start.2
  285.8 23.4 %collective-permute-done.2 = bf16[128,4096]{1,0:T(8,128)(2,1)S(1)} collective-permute-done((bf16[128,4096]{1,0:T(8,128)(2,1)S(1)}, bf16[128,4096]{1,0:T(8,128)(2,1)S(1)}, u32[]{:S(2)}, u32[]{:S(2)}) %collective-permute-start.2) | collective-permute-done | bytes 1048608 | tf_op jit(solution)/shard_map/ppermute | solution.py:215
  309.2 2.8 fusion.4
  (54 shorter events, 2.2 us)
Async XLA Ops:
  6.5 155.8 %all-gather.2.cloned.1.call-start = ((), (), s32[]{:S(2)}) async-start(), calls=%async_computation.4 | async-start | bytes 9437184 | tf_op jit(solution)/shard_map/all_gather | solution.py:175
  41.2 7.6 %copy-start.6 = (s32[16]{0:T(128)S(1)}, s32[16]{0:T(128)}, u32[]{:S(2)}) copy-start(s32[16]{0:T(128)} %param.11) | copy-start | bytes 196
  41.2 7.6 %copy-start.7 = (s32[16]{0:T(128)S(1)}, s32[16]{0:T(128)}, u32[]{:S(2)}) copy-start(s32[16]{0:T(128)} %param.12) | copy-start | bytes 196
  41.2 7.8 %copy-start.2 = (s32[128]{0:T(128)S(1)}, s32[128]{0:T(128)}, u32[]{:S(2)}) copy-start(s32[128]{0:T(128)} %param.10) | copy-start | bytes 1540
  46.5 226.1 %collective-permute-start.1 = (bf16[512,4096]{1,0:T(8,128)(2,1)}, bf16[512,4096]{1,0:T(8,128)(2,1)}, u32[]{:S(2)}, u32[]{:S(2)}) collective-permute-start(bf16[512,4096]{1,0:T(8,128)(2,1)} %param.13), channel_id=1, source_target_pairs={{0,1},{1,0},{2,3},{3,2},{4,5},{5,4},{6,7},{7,6},{8,9},{9,8},{10,11... | collective-permute-start | bytes 12582920 | tf_op jit(solution)/shard_map/ppermute | solution.py:202
  50.9 112.2 %copy-start.5 = (s32[8]{0:T(128)}, s32[8]{0:T(128)S(1)}, u32[]{:S(2)}) copy-start(s32[8]{0:T(128)S(1)} %multiply_add_fusion.qstart_ref) | copy-start | bytes 100
  51.0 112.1 %copy-start.3 = (s32[176]{0:T(256)}, s32[176]{0:T(256)S(1)}, u32[]{:S(2)}) copy-start(s32[176]{0:T(256)S(1)} %broadcast_minimum_fusion.qt_ref) | copy-start | bytes 2116
  51.7 111.3 %copy-start.4 = (s32[176]{0:T(256)}, s32[176]{0:T(256)S(1)}, u32[]{:S(2)}) copy-start(s32[176]{0:T(256)S(1)} %get-tuple-element.19.kt_ref) | copy-start | bytes 2116
  53.2 22.5 %all-to-all-start.1 = ((bf16[8,256,128]{2,1,0:T(8,128)(2,1)}), bf16[8,256,128]{2,1,0:T(8,128)(2,1)S(1)}, u32[]{:S(2)}, u32[]{:S(2)}) async-start(bf16[8,256,128]{2,1,0:T(8,128)(2,1)} %bitcast.9), calls=%async_computation.1 | async-start | bytes 1048576 | tf_op jit(solution)/shard_map/all_to_all | solution.py:173
  75.7 87.4 %copy-start.1 = (bf16[8,256,128]{2,1,0:T(8,128)(2,1)}, bf16[8,256,128]{2,1,0:T(8,128)(2,1)S(1)}, u32[]{:S(2)}) copy-start(bf16[8,256,128]{2,1,0:T(8,128)(2,1)S(1)} %all-to-all-done.1) | copy-start | bytes 1572868
  259.0 8.9 %all-to-all-start.3 = ((bf16[4,512,128]{2,1,0:T(8,128)(2,1)}), bf16[4,512,128]{2,1,0:T(8,128)(2,1)S(1)}, u32[]{:S(2)}, u32[]{:S(2)}) async-start(bf16[4,512,128]{2,1,0:T(8,128)(2,1)} %bitcast.18), calls=%async_computation.3 | async-start | bytes 1048576 | tf_op jit(solution)/shard_map/all_to_all | solution.py:198
  268.6 5.2 %collective-permute-start = (bf16[2,128,512]{2,1,0:T(8,128)(2,1)S(1)}, bf16[2,128,512]{2,1,0:T(8,128)(2,1)S(1)}, u32[]{:S(2)}, u32[]{:S(2)}) collective-permute-start(bf16[2,128,512]{2,1,0:T(8,128)(2,1)S(1)} %get-tuple-element.27), channel_id=1, source_target_pairs={{0,1},{1,0},{2,3},{3,2},{4,5},{5,4},{6,7},{7,6},{8,9},{9,8},{10,11... | collective-permute-start | bytes 786440 | tf_op jit(solution)/shard_map/ppermute | solution.py:209
  281.2 1.9 copy-start
  283.3 25.9 %collective-permute-start.2 = (bf16[128,4096]{1,0:T(8,128)(2,1)S(1)}, bf16[128,4096]{1,0:T(8,128)(2,1)S(1)}, u32[]{:S(2)}, u32[]{:S(2)}) collective-permute-start(bf16[128,4096]{1,0:T(8,128)(2,1)S(1)} %fusion.5), channel_id=1, source_target_pairs={{0,2},{2,0},{1,3},{3,1},{4,6},{6,4},{5,7},{7,5},{8,10},{10,8},{9,1... | collective-permute-start | bytes 3145736 | tf_op jit(solution)/shard_map/ppermute | solution.py:215
Sparse Core Ops, SparseCore 0:
  46.6 115.6 all-gather.1

commit v4 on v3

--- a/solution.py
+++ b/solution.py
@@ -169,10 +169,10 @@
     piece = chunk // n_cg
     j = lax.axis_index("cg")
 
-    stacked = lax.all_to_all(jnp.stack([queries, keys, values]), "cl", 2, 1, tiled=True)
-    q1 = lax.all_to_all(stacked[0], "cg", 0, 0, tiled=True)
-    kv1 = jnp.concatenate([stacked[1], stacked[2]], axis=1)
+    stacked = lax.all_to_all(jnp.stack([keys, values]), "cl", 2, 1, tiled=True)
+    kv1 = jnp.concatenate([stacked[0], stacked[1]], axis=1)
     kv_all = lax.all_gather(kv1, "cg", axis=0, tiled=True)
+    q1 = lax.all_to_all(lax.all_to_all(queries, "cl", 1, 0, tiled=True), "cg", 0, 0, tiled=True)
     seq = kv_all.shape[0]
 
     count = doc_ids.shape[0]

time: 319 us -> 297 us (0.931)
  blocking collectives: 51.6 us -> 31.3 us
  Pallas kernels: 73.1 us -> 79.6 us
  waiting for transfers between devices: 127 us -> 122 us
  local copies, waits for them, and re-layouts: 15 us -> 10.8 us
  starting transfers between devices: 19.4 us -> 23.5 us
    all_to_all x1, blocking collectives: 28.7 us -> 17.4 us  [per_device(): stacked = lax.all_to_all(jnp.stack([keys, values]), 'cl', 2, 1, tiled=True)]
    all_to_all x1, blocking collectives: 22.9 us -> 13.9 us  [per_device(): att0 = lax.all_to_all(att1, 'cg', 0, 0, tiled=True)]
    pallas_call x1, Pallas kernels: 73.1 us -> 79.6 us  [attend_head(): pl.pallas_call(make_kernel(tq), out_shape=jax.ShapeDtypeStruct(q.shape, j...]
    all_to_all x1 -> x2, starting transfers between devices: 7.21 us -> 11.3 us  [the longest x1 7.22 us: per_device(): lax.all_to_all(lax.all_to_all(queries, 'cl', 1, 0, tiled=True), 'cg', 0,...]
    all_to_all x1 -> x2, waiting for transfers between devices: 10.1 us -> 7.72 us  [the longest x1 7.72 us: per_device(): lax.all_to_all(lax.all_to_all(queries, 'cl', 1, 0, tiled=True), 'cg', 0,...]
  transfers between devices with their start and end apart: 6 -> 7, of which waited for: 5 -> 5; matrix products, arithmetic and copies ran while one was open for 3% -> 4% of each run, Pallas kernels for 23% -> 27%
where the time goes in v4:
time: 297 us; the launch traced here: 299 us
  waiting for transfers between devices  122 us (41%)
  Pallas kernels  79.6 us (27%)
  blocking collectives  31.3 us (11%)
  starting transfers between devices  23.5 us (8%)
  between operations  13.7 us (5%)
  local copies, waits for them, and re-layouts  10.8 us (4%)
  other arithmetic  10.5 us (4%)
  matrix products  7.45 us (3%)
    all_gather x1, waiting for transfers between devices, per_device(): kv_all = lax.all_gather(kv1, 'cg', axis=0, tiled=True)  84.4 us
    pallas_call x1, Pallas kernels, attend_head(): pl.pallas_call(make_kernel(tq), out_shape=jax.ShapeDtypeStruct(q.shape, j...  79.6 us
    ppermute x1, waiting for transfers between devices, per_device(): recv = lax.ppermute(other_half, 'th', swap)  23.1 us
    all_to_all x1, blocking collectives, per_device(): stacked = lax.all_to_all(jnp.stack([keys, values]), 'cl', 2, 1, tiled=True)  17.4 us
    all_to_all x1, blocking collectives, per_device(): att0 = lax.all_to_all(att1, 'cg', 0, 0, tiled=True)  13.9 us
    all_to_all x1, waiting for transfers between devices, per_device(): lax.all_to_all(lax.all_to_all(queries, 'cl', 1, 0, tiled=True), 'cg', 0,...  7.72 us
    dot_general x1, matrix products, per_device(): jnp.dot(a_pair.reshape(2 * quarter, 2 * local_width), w_pair, preferred_e...  7.45 us
    all_to_all x1, starting transfers between devices, per_device(): lax.all_to_all(lax.all_to_all(queries, 'cl', 1, 0, tiled=True), 'cg', 0,...  7.22 us
  transfers between devices with their start and end apart: 7, of which 5 were waited for; matrix products, arithmetic and copies ran while one was open for 4% of the time, Pallas kernels for 27%

profile of v4, /device:TPU:1, one launch (start us, length us, event | category | flops | bytes accessed | tf_op | source)
XLA Modules:
  0.0 298.7 jit_solution(10722518874774941258)
XLA Ops:
  6.5 1.3 pad_maximum_fusion
  7.8 1.0 copy.44
  8.8 17.4 %all_to_all.67 = bf16[2,512,512]{1,0,2:T(2,128)(2,1)S(1)} all-to-all(bf16[2,512,512]{1,0,2:T(2,128)(2,1)S(1)} %copy.44), channel_id=1, replica_groups=mesh['cg'=8,'cl'=4,'th'=2,'tc'=2] {'cl'}, dimensions={2} | all-to-all | bytes 2097152 | tf_op jit(solution)/shard_map/all_to_all | solution.py:172
  26.2 0.9 copy.45
  27.3 1.1 pad_maximum_fusion.1
  28.6 1.0 copy.43
  29.6 4.1 %all-to-all-start = ((bf16[512,4,128]{2,0,1:T(8,128)(2,1)}), bf16[512,4,128]{2,0,1:T(8,128)(2,1)}, u32[]{:S(2)}, u32[]{:S(2)}) async-start(bf16[512,4,128]{2,0,1:T(8,128)(2,1)} %copy.43), calls=%async_computation | async-start | bytes 1048576 | tf_op jit(solution)/shard_map/all_to_all | solution.py:175
  33.8 2.2 collective-permute-start.1
  37.1 0.6 slice.18
  38.2 0.6 broadcast_multiply_fusion
  38.8 0.4 select_reduce_fusion
  39.4 0.7 compare_select_fusion.ks_ref
  40.4 7.2 %all-to-all-start.1 = ((bf16[8,256,128]{2,1,0:T(8,128)(2,1)}), bf16[8,256,128]{2,1,0:T(8,128)(2,1)S(1)}, u32[]{:S(2)}, u32[]{:S(2)}) async-start(bf16[8,256,128]{2,1,0:T(8,128)(2,1)} %bitcast.6), calls=%async_computation.1 | async-start | bytes 1048576 | tf_op jit(solution)/shard_map/all_to_all | solution.py:175
  47.7 1.4 copy.52
  49.1 1.3 copy.54
  50.5 1.2 and_convert_fusion
  51.7 1.2 fusion.16.mode_ref
  52.9 7.7 %all-to-all-done.1 = bf16[8,256,128]{2,1,0:T(8,128)(2,1)S(1)} async-done(((bf16[8,256,128]{2,1,0:T(8,128)(2,1)}), bf16[8,256,128]{2,1,0:T(8,128)(2,1)S(1)}, u32[]{:S(2)}, u32[]{:S(2)}) %all-to-all-start.1) | async-done | bytes 524320 | tf_op jit(solution)/shard_map/all_to_all | solution.py:175
  60.6 84.4 %all-gather.2.cloned.1.call-done.k_ref.v_ref = bf16[16384,256]{1,0:T(8,128)(2,1)} async-done(((bf16[2048,256]{1,0:T(8,128)(2,1)}), bf16[16384,256]{1,0:T(8,128)(2,1)}) %all-gather.2.cloned.1.call-update) | async-done | bytes 8388624 | tf_op jit(solution)/shard_map/all_gather | solution.py:174
  145.0 0.7 eq.64
  145.7 79.6 %shard_map.73 = bf16[2048,128]{1,0:T(8,128)(2,1)} custom-call(s32[176]{0:T(256)} %copy-done.4, s32[176]{0:T(256)} %copy-done.5, s32[176]{0:T(256)} %get-tuple-element.28.first_ref, s32[176]{0:T(256)} %get-tuple-element.27.last_ref, s32[176]{0:T(256)} %fusion.16.mode_ref, s32[8]{0:T(128)} %copy-done.6, bf16[2048,128]{1,0:T(8,128)(2,1)} %bitcast.70, ...), custom_call_target="tpu_custom_call" | custom-call | tf_op jit(solution)/shard_map/pallas_call | solution.py:112
  225.3 13.9 %all_to_all.68 = bf16[8,256,128]{2,1,0:T(8,128)(2,1)} all-to-all(bf16[8,256,128]{2,1,0:T(8,128)(2,1)} %bitcast.71), channel_id=1, replica_groups=mesh['cg'=8,'cl'=4,'th'=2,'tc'=2] {'cg'}, dimensions={0} | all-to-all | bytes 1048576 | tf_op jit(solution)/shard_map/all_to_all | solution.py:197
  239.2 3.5 %all-to-all-start.4 = ((bf16[4,512,128]{2,1,0:T(8,128)(2,1)}), bf16[4,512,128]{2,1,0:T(8,128)(2,1)S(1)}, u32[]{:S(2)}, u32[]{:S(2)}) async-start(bf16[4,512,128]{2,1,0:T(8,128)(2,1)} %bitcast.19), calls=%async_computation.4 | async-start | bytes 1048576 | tf_op jit(solution)/shard_map/all_to_all | solution.py:198
  242.7 5.4 %all-to-all-done.4 = bf16[4,512,128]{2,1,0:T(8,128)(2,1)S(1)} async-done(((bf16[4,512,128]{2,1,0:T(8,128)(2,1)}), bf16[4,512,128]{2,1,0:T(8,128)(2,1)S(1)}, u32[]{:S(2)}, u32[]{:S(2)}) %all-to-all-start.4) | async-done | bytes 524320 | tf_op jit(solution)/shard_map/all_to_all | solution.py:198
  248.1 0.4 copy.50
  248.8 3.7 %collective-permute-start = (bf16[2,128,512]{2,1,0:T(8,128)(2,1)S(1)}, bf16[2,128,512]{2,1,0:T(8,128)(2,1)S(1)}, u32[]{:S(2)}, u32[]{:S(2)}) collective-permute-start(bf16[2,128,512]{2,1,0:T(8,128)(2,1)S(1)} %get-tuple-element.26), channel_id=1, source_target_pairs={{0,1},{1,0},{2,3},{3,2},{4,5},{5,4},{6,7},{7,6},{8,9},{9,8},{10,11... | collective-permute-start | bytes 786440 | tf_op jit(solution)/shard_map/ppermute | solution.py:209
  252.5 1.2 collective-permute-done
  253.6 7.5 %fusion.1 = f32[2,128,4096]{2,1,0:T(8,128)S(1)} fusion(bf16[512,4096]{1,0:T(8,128)(2,1)} %collective-permute-done.1, bf16[512,4096]{1,0:T(8,128)(2,1)} %param.13, pred[]{:T(512)S(6)} %eq.57, bf16[2,128,512]{2,1,0:T(8,128)(2,1)S(1)} %collective-permute-done, bf16[2,128,512]{2,1,0:T(8,128)(2,1)S(1)} %get-tuple-element.25), kind=kOutput, calls=%fused_computation.2 | convolution fusion | flops 2187591680 | bytes 13107201 | tf_op jit(solution)/shard_map/dot_general | solution.py:211
  261.1 1.9 copy-done
  263.1 2.8 collective-permute-start.2
  265.9 23.1 %collective-permute-done.2 = bf16[128,4096]{1,0:T(8,128)(2,1)S(1)} collective-permute-done((bf16[128,4096]{1,0:T(8,128)(2,1)S(1)}, bf16[128,4096]{1,0:T(8,128)(2,1)S(1)}, u32[]{:S(2)}, u32[]{:S(2)}) %collective-permute-start.2) | collective-permute-done | bytes 1048608 | tf_op jit(solution)/shard_map/ppermute | solution.py:215
  289.1 2.8 fusion.4
  (60 shorter events, 2.7 us)
Async XLA Ops:
  6.5 138.5 %all-gather.2.cloned.1.call-start = ((), (), s32[]{:S(2)}) async-start(), calls=%async_computation.5 | async-start | bytes 9437184 | tf_op jit(solution)/shard_map/all_gather | solution.py:174
  26.2 2.2 copy-start.2
  27.1 8.9 %copy-start.7 = (s32[16]{0:T(128)S(1)}, s32[16]{0:T(128)}, u32[]{:S(2)}) copy-start(s32[16]{0:T(128)} %param.11) | copy-start | bytes 196
  27.2 8.9 %copy-start.8 = (s32[16]{0:T(128)S(1)}, s32[16]{0:T(128)}, u32[]{:S(2)}) copy-start(s32[16]{0:T(128)} %param.12) | copy-start | bytes 196
  27.2 9.2 %copy-start.3 = (s32[128]{0:T(128)S(1)}, s32[128]{0:T(128)}, u32[]{:S(2)}) copy-start(s32[128]{0:T(128)} %param.10) | copy-start | bytes 1540
  29.6 10.8 %all-to-all-start = ((bf16[512,4,128]{2,0,1:T(8,128)(2,1)}), bf16[512,4,128]{2,0,1:T(8,128)(2,1)}, u32[]{:S(2)}, u32[]{:S(2)}) async-start(bf16[512,4,128]{2,0,1:T(8,128)(2,1)} %copy.43), calls=%async_computation | async-start | bytes 1048576 | tf_op jit(solution)/shard_map/all_to_all | solution.py:175
  33.8 218.7 %collective-permute-start.1 = (bf16[512,4096]{1,0:T(8,128)(2,1)}, bf16[512,4096]{1,0:T(8,128)(2,1)}, u32[]{:S(2)}, u32[]{:S(2)}) collective-permute-start(bf16[512,4096]{1,0:T(8,128)(2,1)} %param.13), channel_id=1, source_target_pairs={{0,1},{1,0},{2,3},{3,2},{4,5},{5,4},{6,7},{7,6},{8,9},{9,8},{10,11... | collective-permute-start | bytes 12582920 | tf_op jit(solution)/shard_map/ppermute | solution.py:202
  37.8 107.9 %copy-start.6 = (s32[8]{0:T(128)}, s32[8]{0:T(128)S(1)}, u32[]{:S(2)}) copy-start(s32[8]{0:T(128)S(1)} %multiply_add_fusion.qstart_ref) | copy-start | bytes 100
  37.9 107.8 %copy-start.4 = (s32[176]{0:T(256)}, s32[176]{0:T(256)S(1)}, u32[]{:S(2)}) copy-start(s32[176]{0:T(256)S(1)} %broadcast_minimum_fusion.qt_ref) | copy-start | bytes 2116
  38.8 106.9 %copy-start.5 = (s32[176]{0:T(256)}, s32[176]{0:T(256)S(1)}, u32[]{:S(2)}) copy-start(s32[176]{0:T(256)S(1)} %get-tuple-element.19.kt_ref) | copy-start | bytes 2116
  40.4 20.2 %all-to-all-start.1 = ((bf16[8,256,128]{2,1,0:T(8,128)(2,1)}), bf16[8,256,128]{2,1,0:T(8,128)(2,1)S(1)}, u32[]{:S(2)}, u32[]{:S(2)}) async-start(bf16[8,256,128]{2,1,0:T(8,128)(2,1)} %bitcast.6), calls=%async_computation.1 | async-start | bytes 1048576 | tf_op jit(solution)/shard_map/all_to_all | solution.py:175
  60.6 85.1 %copy-start.1 = (bf16[8,256,128]{2,1,0:T(8,128)(2,1)}, bf16[8,256,128]{2,1,0:T(8,128)(2,1)S(1)}, u32[]{:S(2)}) copy-start(bf16[8,256,128]{2,1,0:T(8,128)(2,1)S(1)} %all-to-all-done.1) | copy-start | bytes 1572868
  239.2 8.9 %all-to-all-start.4 = ((bf16[4,512,128]{2,1,0:T(8,128)(2,1)}), bf16[4,512,128]{2,1,0:T(8,128)(2,1)S(1)}, u32[]{:S(2)}, u32[]{:S(2)}) async-start(bf16[4,512,128]{2,1,0:T(8,128)(2,1)} %bitcast.19), calls=%async_computation.4 | async-start | bytes 1048576 | tf_op jit(solution)/shard_map/all_to_all | solution.py:198
  248.8 4.8 %collective-permute-start = (bf16[2,128,512]{2,1,0:T(8,128)(2,1)S(1)}, bf16[2,128,512]{2,1,0:T(8,128)(2,1)S(1)}, u32[]{:S(2)}, u32[]{:S(2)}) collective-permute-start(bf16[2,128,512]{2,1,0:T(8,128)(2,1)S(1)} %get-tuple-element.26), channel_id=1, source_target_pairs={{0,1},{1,0},{2,3},{3,2},{4,5},{5,4},{6,7},{7,6},{8,9},{9,8},{10,11... | collective-permute-start | bytes 786440 | tf_op jit(solution)/shard_map/ppermute | solution.py:209
  261.1 1.9 copy-start
  263.1 25.9 %collective-permute-start.2 = (bf16[128,4096]{1,0:T(8,128)(2,1)S(1)}, bf16[128,4096]{1,0:T(8,128)(2,1)S(1)}, u32[]{:S(2)}, u32[]{:S(2)}) collective-permute-start(bf16[128,4096]{1,0:T(8,128)(2,1)S(1)} %fusion.5), channel_id=1, source_target_pairs={{0,2},{2,0},{1,3},{3,1},{4,6},{6,4},{5,7},{7,5},{8,10},{10,8},{9,1... | collective-permute-start | bytes 3145736 | tf_op jit(solution)/shard_map/ppermute | solution.py:215
Sparse Core Ops, SparseCore 0:
  28.5 116.4 all-gather.1

commit v5 on v4

--- a/solution.py
+++ b/solution.py
@@ -142,7 +142,13 @@
     cnt = jnp.clip(hi_t - lo_t + 1, 1, most)
     ends = jnp.cumsum(cnt)
     starts = ends - cnt
-    total = nq * most
+    stride = seq // nq // BLOCK
+    rest, spread = count, 0
+    while rest > 0:
+        size = min(DOC_MOST, rest)
+        spread += sum(max(0, size - 1 - stride * i) for i in range(size // stride + 1))
+        rest -= size
+    total = min(nq * most, nq * 3 + spread // per_k + 1)
     pos = jnp.arange(total, dtype=jnp.int32)
     qt = jnp.minimum(jnp.sum((pos[:, None] >= ends[None, :]).astype(jnp.int32), axis=1), nq - 1)
     live = pos < ends[-1]
@@ -208,11 +214,11 @@
     give = lax.dynamic_index_in_dim(blocks, 1 - tc, axis=1, keepdims=False)
     got = lax.ppermute(give, "tc", swap)
     a_pair = jnp.where(tc == 0, jnp.concatenate([keep, got], axis=2), jnp.concatenate([got, keep], axis=2))
-    partial = jnp.dot(a_pair.reshape(2 * quarter, 2 * local_width), w_pair,
-                      preferred_element_type=jnp.float32).reshape(2, quarter, -1)
-    mine_half = lax.dynamic_index_in_dim(partial, th, axis=0, keepdims=False)
-    other_half = lax.dynamic_index_in_dim(partial, 1 - th, axis=0, keepdims=False).astype(jnp.bfloat16)
+    a_other = lax.dynamic_index_in_dim(a_pair, 1 - th, axis=0, keepdims=False)
+    a_mine = lax.dynamic_index_in_dim(a_pair, th, axis=0, keepdims=False)
+    other_half = jnp.dot(a_other, w_pair, preferred_element_type=jnp.float32).astype(jnp.bfloat16)
     recv = lax.ppermute(other_half, "th", swap)
+    mine_half = lax.optimization_barrier(jnp.dot(a_mine, w_pair, preferred_element_type=jnp.float32))
     return (mine_half + recv.astype(jnp.float32)).astype(jnp.bfloat16)
 
 

time: 297 us -> 285 us (0.960); the launches traced: 299 us -> 283 us
  Pallas kernels: 79.6 us -> 61.9 us
  waiting for transfers between devices: 122 us -> 113 us
  matrix products: 7.45 us -> 14.8 us
  blocking collectives: 31.3 us -> 36.2 us
    pallas_call x1, Pallas kernels: 79.6 us -> 61.9 us  [attend_head(): pl.pallas_call(make_kernel(tq), out_shape=jax.ShapeDtypeStruct(q.shape, j...]
    ppermute x1, waiting for transfers between devices: 23.1 us -> 15.8 us  [per_device(): recv = lax.ppermute(other_half, 'th', swap)]
    dot_general x1 -> x2, matrix products: 7.45 us -> 14.8 us  [the longest x1 7.41 us: per_device(): jnp.dot(a_other, w_pair, preferred_element_type=jnp.float32)]
    all_to_all x1, blocking collectives: 13.9 us -> 18.8 us  [per_device(): att0 = lax.all_to_all(att1, 'cg', 0, 0, tiled=True)]
  transfers between devices with their start and end apart: 7 -> 7, of which waited for: 5 -> 5; matrix products, arithmetic and copies ran while one was open for 4% -> 8% of each run, Pallas kernels for 27% -> 22%
where the time goes in v5:
time: 285 us; the launch traced here: 283 us
  waiting for transfers between devices  113 us (40%)
  Pallas kernels  61.9 us (22%)
  blocking collectives  36.2 us (13%)
  starting transfers between devices  23.6 us (8%)
  matrix products  14.8 us (5%)
  between operations  13.7 us (5%)
  other arithmetic  10.9 us (4%)
  local copies, waits for them, and re-layouts  8.85 us (3%)
    all_gather x1, waiting for transfers between devices, per_device(): kv_all = lax.all_gather(kv1, 'cg', axis=0, tiled=True)  82.5 us
    pallas_call x1, Pallas kernels, attend_head(): pl.pallas_call(make_kernel(tq), out_shape=jax.ShapeDtypeStruct(q.shape, j...  61.9 us
    all_to_all x1, blocking collectives, per_device(): att0 = lax.all_to_all(att1, 'cg', 0, 0, tiled=True)  18.8 us
    all_to_all x1, blocking collectives, per_device(): stacked = lax.all_to_all(jnp.stack([keys, values]), 'cl', 2, 1, tiled=True)  17.4 us
    ppermute x1, waiting for transfers between devices, per_device(): recv = lax.ppermute(other_half, 'th', swap)  15.8 us
    all_to_all x1, waiting for transfers between devices, per_device(): lax.all_to_all(lax.all_to_all(queries, 'cl', 1, 0, tiled=True), 'cg', 0,...  7.73 us
    dot_general x1, matrix products, per_device(): jnp.dot(a_other, w_pair, preferred_element_type=jnp.float32)  7.41 us
    dot_general x1, matrix products, per_device(): jnp.dot(a_mine, w_pair, preferred_element_type=jnp.float32)  7.38 us
  transfers between devices with their start and end apart: 7, of which 5 were waited for; matrix products, arithmetic and copies ran while one was open for 8% of the time, Pallas kernels for 22%

profile of v5, /device:TPU:1, one launch (start us, length us, event | category | flops | bytes accessed | tf_op | source)
XLA Modules:
  0.0 282.7 jit_solution(11528908344771951943)
XLA Ops:
  6.5 1.4 pad_maximum_fusion
  7.9 1.0 copy.45
  8.9 17.4 %all_to_all.67 = bf16[2,512,512]{1,0,2:T(2,128)(2,1)S(1)} all-to-all(bf16[2,512,512]{1,0,2:T(2,128)(2,1)S(1)} %copy.45), channel_id=1, replica_groups=mesh['cg'=8,'cl'=4,'th'=2,'tc'=2] {'cl'}, dimensions={2} | all-to-all | bytes 2097152 | tf_op jit(solution)/shard_map/all_to_all | solution.py:178
  26.3 0.9 copy.46
  27.3 1.1 pad_maximum_fusion.1
  28.6 1.0 copy.44
  29.7 4.1 %all-to-all-start = ((bf16[512,4,128]{2,0,1:T(8,128)(2,1)}), bf16[512,4,128]{2,0,1:T(8,128)(2,1)}, u32[]{:S(2)}, u32[]{:S(2)}) async-start(bf16[512,4,128]{2,0,1:T(8,128)(2,1)} %copy.44), calls=%async_computation | async-start | bytes 1048576 | tf_op jit(solution)/shard_map/all_to_all | solution.py:181
  33.8 2.2 collective-permute-start.1
  37.2 0.6 slice.18
  38.3 0.7 compare_select_fusion.ks_ref
  39.1 0.6 broadcast_multiply_fusion
  40.1 2.0 select_reduce_fusion
  42.3 7.2 %all-to-all-start.1 = ((bf16[8,256,128]{2,1,0:T(8,128)(2,1)}), bf16[8,256,128]{2,1,0:T(8,128)(2,1)S(1)}, u32[]{:S(2)}, u32[]{:S(2)}) async-start(bf16[8,256,128]{2,1,0:T(8,128)(2,1)} %bitcast.7), calls=%async_computation.1 | async-start | bytes 1048576 | tf_op jit(solution)/shard_map/all_to_all | solution.py:181
  49.6 1.4 copy.54
  51.1 1.3 copy.56
  52.4 1.2 and_convert_fusion
  53.6 1.2 fusion.15.mode_ref
  54.8 7.7 %all-to-all-done.1 = bf16[8,256,128]{2,1,0:T(8,128)(2,1)S(1)} async-done(((bf16[8,256,128]{2,1,0:T(8,128)(2,1)}), bf16[8,256,128]{2,1,0:T(8,128)(2,1)S(1)}, u32[]{:S(2)}, u32[]{:S(2)}) %all-to-all-start.1) | async-done | bytes 524320 | tf_op jit(solution)/shard_map/all_to_all | solution.py:181
  62.6 82.5 %all-gather.2.cloned.1.call-done.k_ref.v_ref = bf16[16384,256]{1,0:T(8,128)(2,1)} async-done(((bf16[2048,256]{1,0:T(8,128)(2,1)}), bf16[16384,256]{1,0:T(8,128)(2,1)}) %all-gather.2.cloned.1.call-update) | async-done | bytes 8388624 | tf_op jit(solution)/shard_map/all_gather | solution.py:180
  145.1 0.7 eq.64
  145.8 61.9 %shard_map.73 = bf16[2048,128]{1,0:T(8,128)(2,1)} custom-call(s32[107]{0:T(128)} %copy-done.5, s32[107]{0:T(128)} %copy-done.3, s32[107]{0:T(128)} %get-tuple-element.28.first_ref, s32[107]{0:T(128)} %get-tuple-element.27.last_ref, s32[107]{0:T(128)} %fusion.15.mode_ref, s32[8]{0:T(128)} %copy-done.4, bf16[2048,128]{1,0:T(8,128)(2,1)} %bitcast.76, ...), custom_call_target="tpu_custom_call" | custom-call | tf_op jit(solution)/shard_map/pallas_call | solution.py:112
  207.8 18.8 %all_to_all.68 = bf16[8,256,128]{2,1,0:T(8,128)(2,1)} all-to-all(bf16[8,256,128]{2,1,0:T(8,128)(2,1)} %bitcast.77), channel_id=1, replica_groups=mesh['cg'=8,'cl'=4,'th'=2,'tc'=2] {'cg'}, dimensions={0} | all-to-all | bytes 1048576 | tf_op jit(solution)/shard_map/all_to_all | solution.py:203
  226.6 3.5 %all-to-all-start.4 = ((bf16[4,512,128]{2,1,0:T(8,128)(2,1)}), bf16[4,512,128]{2,1,0:T(8,128)(2,1)S(1)}, u32[]{:S(2)}, u32[]{:S(2)}) async-start(bf16[4,512,128]{2,1,0:T(8,128)(2,1)} %bitcast.20), calls=%async_computation.4 | async-start | bytes 1048576 | tf_op jit(solution)/shard_map/all_to_all | solution.py:204
  230.1 5.4 %all-to-all-done.4 = bf16[4,512,128]{2,1,0:T(8,128)(2,1)S(1)} async-done(((bf16[4,512,128]{2,1,0:T(8,128)(2,1)}), bf16[4,512,128]{2,1,0:T(8,128)(2,1)S(1)}, u32[]{:S(2)}, u32[]{:S(2)}) %all-to-all-start.4) | async-done | bytes 524320 | tf_op jit(solution)/shard_map/all_to_all | solution.py:204
  235.5 0.4 copy.51
  236.2 3.7 %collective-permute-start = (bf16[2,128,512]{2,1,0:T(8,128)(2,1)S(1)}, bf16[2,128,512]{2,1,0:T(8,128)(2,1)S(1)}, u32[]{:S(2)}, u32[]{:S(2)}) collective-permute-start(bf16[2,128,512]{2,1,0:T(8,128)(2,1)S(1)} %get-tuple-element.26), channel_id=1, source_target_pairs={{0,1},{1,0},{2,3},{3,2},{4,5},{5,4},{6,7},{7,6},{8,9},{9,8},{10,11... | collective-permute-start | bytes 786440 | tf_op jit(solution)/shard_map/ppermute | solution.py:215
  239.9 1.2 collective-permute-done
  241.2 7.4 %convolution_convert_fusion = bf16[128,4096]{1,0:T(8,128)(2,1)S(1)} fusion(bf16[512,4096]{1,0:T(8,128)(2,1)} %collective-permute-done.1, bf16[512,4096]{1,0:T(8,128)(2,1)} %param.13, pred[]{:T(512)S(6)} %eq.57, bf16[2,128,1024]{2,1,0:T(8,128)(2,1)S(1)} %maximum_select_fusion.3, s32[]{:T(128)S(6)} %select_n.182), kind=kOutput, calls=%fused_computation.1 | convolution fusion | flops 1112014848 | bytes 9699333 | tf_op jit(solution)/shard_map/dot_general | solution.py:219
  248.7 2.8 collective-permute-start.2
  251.4 7.4 %fusion = f32[128,4096]{1,0:T(8,128)S(1)} fusion(bf16[512,4096]{1,0:T(8,128)(2,1)} %collective-permute-done.1, bf16[512,4096]{1,0:T(8,128)(2,1)} %param.13, pred[]{:T(512)S(6)} %eq.57, bf16[2,128,1024]{2,1,0:T(8,128)(2,1)S(1)} %maximum_select_fusion.3, s32[]{:T(128)S(6)} %select_n.179), kind=kOutput, calls=%fused_computation.3 | convolution fusion | flops 1111490560 | bytes 10747909 | tf_op jit(solution)/shard_map/dot_general | solution.py:221
  258.8 15.8 %collective-permute-done.2 = bf16[128,4096]{1,0:T(8,128)(2,1)S(1)} collective-permute-done((bf16[128,4096]{1,0:T(8,128)(2,1)S(1)}, bf16[128,4096]{1,0:T(8,128)(2,1)S(1)}, u32[]{:S(2)}, u32[]{:S(2)}) %collective-permute-start.2) | collective-permute-done | bytes 1048608 | tf_op jit(solution)/shard_map/ppermute | solution.py:220
  274.6 1.2 add_convert_fusion
  (59 shorter events, 2.9 us)
Async XLA Ops:
  6.5 21.9 %copy-start.1 = (bf16[512,512]{1,0:T(8,128)(2,1)S(1)}, bf16[512,512]{1,0:T(8,128)(2,1)}, u32[]{:S(2)}) copy-start(bf16[512,512]{1,0:T(8,128)(2,1)} %param.7) | copy-start | bytes 1572868
  6.5 138.6 %all-gather.2.cloned.1.call-start = ((), (), s32[]{:S(2)}) async-start(), calls=%async_computation.5 | async-start | bytes 9437184 | tf_op jit(solution)/shard_map/all_gather | solution.py:180
  6.5 29.5 %copy-start.6 = (s32[16]{0:T(128)S(1)}, s32[16]{0:T(128)}, u32[]{:S(2)}) copy-start(s32[16]{0:T(128)} %param.11) | copy-start | bytes 196
  6.5 29.5 %copy-start.7 = (s32[16]{0:T(128)S(1)}, s32[16]{0:T(128)}, u32[]{:S(2)}) copy-start(s32[16]{0:T(128)} %param.12) | copy-start | bytes 196
  6.5 29.7 %copy-start.2 = (s32[128]{0:T(128)S(1)}, s32[128]{0:T(128)}, u32[]{:S(2)}) copy-start(s32[128]{0:T(128)} %param.10) | copy-start | bytes 1540
  29.7 12.6 %all-to-all-start = ((bf16[512,4,128]{2,0,1:T(8,128)(2,1)}), bf16[512,4,128]{2,0,1:T(8,128)(2,1)}, u32[]{:S(2)}, u32[]{:S(2)}) async-start(bf16[512,4,128]{2,0,1:T(8,128)(2,1)} %copy.44), calls=%async_computation | async-start | bytes 1048576 | tf_op jit(solution)/shard_map/all_to_all | solution.py:181
  33.8 207.4 %collective-permute-start.1 = (bf16[512,4096]{1,0:T(8,128)(2,1)}, bf16[512,4096]{1,0:T(8,128)(2,1)}, u32[]{:S(2)}, u32[]{:S(2)}) collective-permute-start(bf16[512,4096]{1,0:T(8,128)(2,1)} %param.13), channel_id=1, source_target_pairs={{0,1},{1,0},{2,3},{3,2},{4,5},{5,4},{6,7},{7,6},{8,9},{9,8},{10,11... | collective-permute-start | bytes 12582920 | tf_op jit(solution)/shard_map/ppermute | solution.py:208
  39.0 106.8 %copy-start.4 = (s32[8]{0:T(128)}, s32[8]{0:T(128)S(1)}, u32[]{:S(2)}) copy-start(s32[8]{0:T(128)S(1)} %multiply_add_fusion.qstart_ref) | copy-start | bytes 100
  39.0 106.8 %copy-start.5 = (s32[107]{0:T(128)}, s32[107]{0:T(128)S(1)}, u32[]{:S(2)}) copy-start(s32[107]{0:T(128)S(1)} %broadcast_minimum_fusion.qt_ref) | copy-start | bytes 1288
  39.8 106.0 %copy-start.3 = (s32[107]{0:T(128)}, s32[107]{0:T(128)S(1)}, u32[]{:S(2)}) copy-start(s32[107]{0:T(128)S(1)} %get-tuple-element.19.kt_ref) | copy-start | bytes 1288
  42.3 20.3 %all-to-all-start.1 = ((bf16[8,256,128]{2,1,0:T(8,128)(2,1)}), bf16[8,256,128]{2,1,0:T(8,128)(2,1)S(1)}, u32[]{:S(2)}, u32[]{:S(2)}) async-start(bf16[8,256,128]{2,1,0:T(8,128)(2,1)} %bitcast.7), calls=%async_computation.1 | async-start | bytes 1048576 | tf_op jit(solution)/shard_map/all_to_all | solution.py:181
  62.6 83.3 %copy-start = (bf16[8,256,128]{2,1,0:T(8,128)(2,1)}, bf16[8,256,128]{2,1,0:T(8,128)(2,1)S(1)}, u32[]{:S(2)}) copy-start(bf16[8,256,128]{2,1,0:T(8,128)(2,1)S(1)} %all-to-all-done.1) | copy-start | bytes 1572868
  226.6 8.9 %all-to-all-start.4 = ((bf16[4,512,128]{2,1,0:T(8,128)(2,1)}), bf16[4,512,128]{2,1,0:T(8,128)(2,1)S(1)}, u32[]{:S(2)}, u32[]{:S(2)}) async-start(bf16[4,512,128]{2,1,0:T(8,128)(2,1)} %bitcast.20), calls=%async_computation.4 | async-start | bytes 1048576 | tf_op jit(solution)/shard_map/all_to_all | solution.py:204
  236.2 4.9 %collective-permute-start = (bf16[2,128,512]{2,1,0:T(8,128)(2,1)S(1)}, bf16[2,128,512]{2,1,0:T(8,128)(2,1)S(1)}, u32[]{:S(2)}, u32[]{:S(2)}) collective-permute-start(bf16[2,128,512]{2,1,0:T(8,128)(2,1)S(1)} %get-tuple-element.26), channel_id=1, source_target_pairs={{0,1},{1,0},{2,3},{3,2},{4,5},{5,4},{6,7},{7,6},{8,9},{9,8},{10,11... | collective-permute-start | bytes 786440 | tf_op jit(solution)/shard_map/ppermute | solution.py:215
  248.7 25.9 %collective-permute-start.2 = (bf16[128,4096]{1,0:T(8,128)(2,1)S(1)}, bf16[128,4096]{1,0:T(8,128)(2,1)S(1)}, u32[]{:S(2)}, u32[]{:S(2)}) collective-permute-start(bf16[128,4096]{1,0:T(8,128)(2,1)S(1)} %convolution_convert_fusion), channel_id=1, source_target_pairs={{0,2},{2,0},{1,3},{3,1},{4,6},{6,4},{5,7},{7,5},{8,10},{10,8},{9,1... | collective-permute-start | bytes 3145736 | tf_op jit(solution)/shard_map/ppermute | solution.py:220
Sparse Core Ops, SparseCore 0:
  28.5 116.5 all-gather.1

commit v6 on v5

--- a/solution.py
+++ b/solution.py
@@ -12,7 +12,7 @@
 BLOCK = 128
 DOC_MOST = 80
 SPAN_MOST = 4
-TK = 512
+TK = 1024
 
 NEG = -1e30
 
@@ -206,19 +206,21 @@
     th = lax.axis_index("th")
     swap = [(0, 1), (1, 0)]
     w_other = lax.ppermute(out_weight, "tc", swap)
-    w_pair = jnp.where(tc == 0, jnp.concatenate([out_weight, w_other], axis=0),
-                       jnp.concatenate([w_other, out_weight], axis=0))
     quarter = rows // 4
     blocks = attended.reshape(2, 2, quarter, local_width)
     keep = lax.dynamic_index_in_dim(blocks, tc, axis=1, keepdims=False)
     give = lax.dynamic_index_in_dim(blocks, 1 - tc, axis=1, keepdims=False)
     got = lax.ppermute(give, "tc", swap)
-    a_pair = jnp.where(tc == 0, jnp.concatenate([keep, got], axis=2), jnp.concatenate([got, keep], axis=2))
-    a_other = lax.dynamic_index_in_dim(a_pair, 1 - th, axis=0, keepdims=False)
-    a_mine = lax.dynamic_index_in_dim(a_pair, th, axis=0, keepdims=False)
-    other_half = jnp.dot(a_other, w_pair, preferred_element_type=jnp.float32).astype(jnp.bfloat16)
+
+    def project(half):
+        own = lax.dynamic_index_in_dim(keep, half, axis=0, keepdims=False)
+        other = lax.dynamic_index_in_dim(got, half, axis=0, keepdims=False)
+        return jnp.dot(own, out_weight, preferred_element_type=jnp.float32) + jnp.dot(
+            other, w_other, preferred_element_type=jnp.float32)
+
+    other_half = project(1 - th).astype(jnp.bfloat16)
     recv = lax.ppermute(other_half, "th", swap)
-    mine_half = lax.optimization_barrier(jnp.dot(a_mine, w_pair, preferred_element_type=jnp.float32))
+    mine_half = lax.optimization_barrier(project(th))
     return (mine_half + recv.astype(jnp.float32)).astype(jnp.bfloat16)
 
 

time: 285 us -> 265 us (0.930)
  Pallas kernels: 61.9 us -> 46.1 us
  matrix products: 14.8 us -> 11.8 us
    pallas_call x1, Pallas kernels: 61.9 us -> 46.1 us  [attend_head(): pl.pallas_call(make_kernel(tq), out_shape=jax.ShapeDtypeStruct(q.shape, j...]
    dot_general x2 -> x4, matrix products: 14.8 us -> 11.8 us  [the longest x2 5.98 us: project(): jnp.dot(other, w_other, preferred_element_type=jnp.float32)]
  transfers between devices with their start and end apart: 7 -> 7, of which waited for: 5 -> 4; matrix products, arithmetic and copies ran while one was open for 8% -> 8% of each run, Pallas kernels for 22% -> 18%
where the time goes in v6:
time: 265 us; the launch traced here: 263 us
  waiting for transfers between devices  114 us (43%)
  Pallas kernels  46.1 us (17%)
  blocking collectives  34.8 us (13%)
  starting transfers between devices  23.6 us (9%)
  between operations  13.7 us (5%)
  matrix products  11.8 us (4%)
  other arithmetic  10 us (4%)
  local copies, waits for them, and re-layouts  8.85 us (3%)
    all_gather x1, waiting for transfers between devices, per_device(): kv_all = lax.all_gather(kv1, 'cg', axis=0, tiled=True)  83.1 us
    pallas_call x1, Pallas kernels, attend_head(): pl.pallas_call(make_kernel(tq), out_shape=jax.ShapeDtypeStruct(q.shape, j...  46.1 us
    ppermute x1, waiting for transfers between devices, per_device(): recv = lax.ppermute(other_half, 'th', swap)  17.6 us
    all_to_all x1, blocking collectives, per_device(): att0 = lax.all_to_all(att1, 'cg', 0, 0, tiled=True)  17.4 us
    all_to_all x1, blocking collectives, per_device(): stacked = lax.all_to_all(jnp.stack([keys, values]), 'cl', 2, 1, tiled=True)  17.4 us
    all_to_all x1, waiting for transfers between devices, per_device(): lax.all_to_all(lax.all_to_all(queries, 'cl', 1, 0, tiled=True), 'cg', 0,...  7.88 us
    all_to_all x1, starting transfers between devices, per_device(): lax.all_to_all(lax.all_to_all(queries, 'cl', 1, 0, tiled=True), 'cg', 0,...  7.22 us
    dot_general x2, matrix products, project(): jnp.dot(other, w_other, preferred_element_type=jnp.float32)  5.98 us
  transfers between devices with their start and end apart: 7, of which 4 were waited for; matrix products, arithmetic and copies ran while one was open for 8% of the time, Pallas kernels for 18%

profile of v6, /device:TPU:1, one launch (start us, length us, event | category | flops | bytes accessed | tf_op | source)
XLA Modules:
  0.0 262.9 jit_solution(11781300424824083770)
XLA Ops:
  6.5 1.3 pad_maximum_fusion
  7.8 1.0 copy.45
  8.8 17.4 %all_to_all.67 = bf16[2,512,512]{1,0,2:T(2,128)(2,1)S(1)} all-to-all(bf16[2,512,512]{1,0,2:T(2,128)(2,1)S(1)} %copy.45), channel_id=1, replica_groups=mesh['cg'=8,'cl'=4,'th'=2,'tc'=2] {'cl'}, dimensions={2} | all-to-all | bytes 2097152 | tf_op jit(solution)/shard_map/all_to_all | solution.py:178
  26.2 0.9 copy.46
  27.2 1.1 pad_maximum_fusion.1
  28.6 1.0 copy.44
  29.6 4.1 %all-to-all-start = ((bf16[512,4,128]{2,0,1:T(8,128)(2,1)}), bf16[512,4,128]{2,0,1:T(8,128)(2,1)}, u32[]{:S(2)}, u32[]{:S(2)}) async-start(bf16[512,4,128]{2,0,1:T(8,128)(2,1)} %copy.44), calls=%async_computation | async-start | bytes 1048576 | tf_op jit(solution)/shard_map/all_to_all | solution.py:181
  33.7 2.2 collective-permute-start.1
  36.8 0.7 compare_select_fusion.ks_ref
  38.0 0.6 slice.18
  39.1 0.6 broadcast_multiply_fusion
  39.8 1.3 select_reduce_fusion
  41.5 7.2 %all-to-all-start.1 = ((bf16[8,256,128]{2,1,0:T(8,128)(2,1)}), bf16[8,256,128]{2,1,0:T(8,128)(2,1)S(1)}, u32[]{:S(2)}, u32[]{:S(2)}) async-start(bf16[8,256,128]{2,1,0:T(8,128)(2,1)} %bitcast.7), calls=%async_computation.1 | async-start | bytes 1048576 | tf_op jit(solution)/shard_map/all_to_all | solution.py:181
  48.8 1.4 copy.54
  50.2 1.3 copy.56
  51.6 1.2 and_convert_fusion
  52.8 1.2 fusion.23.mode_ref
  54.0 7.9 %all-to-all-done.1 = bf16[8,256,128]{2,1,0:T(8,128)(2,1)S(1)} async-done(((bf16[8,256,128]{2,1,0:T(8,128)(2,1)}), bf16[8,256,128]{2,1,0:T(8,128)(2,1)S(1)}, u32[]{:S(2)}, u32[]{:S(2)}) %all-to-all-start.1) | async-done | bytes 524320 | tf_op jit(solution)/shard_map/all_to_all | solution.py:181
  61.9 83.1 %all-gather.2.cloned.1.call-done.k_ref.v_ref = bf16[16384,256]{1,0:T(8,128)(2,1)} async-done(((bf16[2048,256]{1,0:T(8,128)(2,1)}), bf16[16384,256]{1,0:T(8,128)(2,1)}) %all-gather.2.cloned.1.call-update) | async-done | bytes 8388624 | tf_op jit(solution)/shard_map/all_gather | solution.py:180
  145.0 0.7 eq.63
  145.7 46.1 %shard_map.73 = bf16[2048,128]{1,0:T(8,128)(2,1)} custom-call(s32[66]{0:T(128)} %copy-done.5, s32[66]{0:T(128)} %copy-done.3, s32[66]{0:T(128)} %get-tuple-element.26.first_ref, s32[66]{0:T(128)} %get-tuple-element.25.last_ref, s32[66]{0:T(128)} %fusion.23.mode_ref, s32[8]{0:T(128)} %copy-done.4, bf16[2048,128]{1,0:T(8,128)(2,1)} %bitcast.84, ...), custom_call_target="tpu_custom_call" | custom-call | tf_op jit(solution)/shard_map/pallas_call | solution.py:112
  191.9 17.4 %all_to_all.68 = bf16[8,256,128]{2,1,0:T(8,128)(2,1)} all-to-all(bf16[8,256,128]{2,1,0:T(8,128)(2,1)} %bitcast.85), channel_id=1, replica_groups=mesh['cg'=8,'cl'=4,'th'=2,'tc'=2] {'cg'}, dimensions={0} | all-to-all | bytes 1048576 | tf_op jit(solution)/shard_map/all_to_all | solution.py:203
  209.3 3.5 %all-to-all-start.4 = ((bf16[4,512,128]{2,1,0:T(8,128)(2,1)}), bf16[4,512,128]{2,1,0:T(8,128)(2,1)S(1)}, u32[]{:S(2)}, u32[]{:S(2)}) async-start(bf16[4,512,128]{2,1,0:T(8,128)(2,1)} %bitcast.20), calls=%async_computation.4 | async-start | bytes 1048576 | tf_op jit(solution)/shard_map/all_to_all | solution.py:204
  212.8 5.4 %all-to-all-done.4 = bf16[4,512,128]{2,1,0:T(8,128)(2,1)S(1)} async-done(((bf16[4,512,128]{2,1,0:T(8,128)(2,1)}), bf16[4,512,128]{2,1,0:T(8,128)(2,1)S(1)}, u32[]{:S(2)}, u32[]{:S(2)}) %all-to-all-start.4) | async-done | bytes 524320 | tf_op jit(solution)/shard_map/all_to_all | solution.py:204
  218.9 3.7 %collective-permute-start = (bf16[2,128,512]{2,1,0:T(8,128)(2,1)S(1)}, bf16[2,128,512]{2,1,0:T(8,128)(2,1)S(1)}, u32[]{:S(2)}, u32[]{:S(2)}) collective-permute-start(bf16[2,128,512]{2,1,0:T(8,128)(2,1)S(1)} %dynamic-slice_bitcast_fusion), channel_id=1, source_target_pairs={{0,1},{1,0},{2,3},{3,2},{4,5},{5,4},{6,7},{7,6},{8,9},{9,8},{10,11... | collective-permute-start | bytes 786440 | tf_op jit(solution)/shard_map/ppermute | solution.py:213
  222.6 2.9 %fusion.2 = f32[128,4096]{1,0:T(8,128)S(1)} fusion(bf16[512,4096]{1,0:T(8,128)(2,1)} %param.13, bf16[2,2,128,512]{3,2,1,0:T(8,128)(2,1)S(1)} %reshape.294, s32[]{:T(128)S(6)} %select_n.173, s32[]{:T(128)S(6)} %select_n.170), kind=kOutput, calls=%fused_computation.11 | convolution fusion | flops 536870912 | bytes 6422536 | tf_op jit(solution)/shard_map/dot_general | solution.py:218
  225.5 3.0 %fusion = bf16[128,4096]{1,0:T(8,128)(2,1)S(1)} fusion(f32[128,4096]{1,0:T(8,128)S(1)} %fusion.2, bf16[512,4096]{1,0:T(8,128)(2,1)} %collective-permute-done.1, bf16[2,128,512]{2,1,0:T(8,128)(2,1)S(1)} %collective-permute-done, s32[]{:T(128)S(6)} %select_n.172), kind=kOutput, calls=%fused_computation.2 | convolution fusion | flops 537919488 | bytes 7471108 | tf_op jit(solution)/shard_map/dot_general | solution.py:218
  228.5 2.8 %collective-permute-start.2 = (bf16[128,4096]{1,0:T(8,128)(2,1)S(1)}, bf16[128,4096]{1,0:T(8,128)(2,1)S(1)}, u32[]{:S(2)}, u32[]{:S(2)}) collective-permute-start(bf16[128,4096]{1,0:T(8,128)(2,1)S(1)} %fusion), channel_id=1, source_target_pairs={{0,2},{2,0},{1,3},{3,1},{4,6},{6,4},{5,7},{7,5},{8,10},{10,8},{9,1... | collective-permute-start | bytes 3145736 | tf_op jit(solution)/shard_map/ppermute | solution.py:222
  231.3 2.9 %fusion.5 = f32[128,4096]{1,0:T(8,128)S(1)} fusion(bf16[512,4096]{1,0:T(8,128)(2,1)} %param.13, bf16[2,2,128,512]{3,2,1,0:T(8,128)(2,1)S(1)} %reshape.294, s32[]{:T(128)S(6)} %select_n.168, s32[]{:T(128)S(6)} %select_n.170), kind=kOutput, calls=%fused_computation.14 | convolution fusion | flops 536870912 | bytes 6422536 | tf_op jit(solution)/shard_map/dot_general | solution.py:218
  234.2 3.0 %convolution_add_fusion.1 = f32[128,4096]{1,0:T(8,128)S(1)} fusion(f32[128,4096]{1,0:T(8,128)S(1)} %fusion.5, bf16[512,4096]{1,0:T(8,128)(2,1)} %collective-permute-done.1, bf16[2,128,512]{2,1,0:T(8,128)(2,1)S(1)} %collective-permute-done, s32[]{:T(128)S(6)} %select_n.167), kind=kOutput, calls=%fused_computation.1 | convolution fusion | flops 537395200 | bytes 8519684 | tf_op jit(solution)/shard_map/dot_general | solution.py:218
  237.2 17.6 %collective-permute-done.2 = bf16[128,4096]{1,0:T(8,128)(2,1)S(1)} collective-permute-done((bf16[128,4096]{1,0:T(8,128)(2,1)S(1)}, bf16[128,4096]{1,0:T(8,128)(2,1)S(1)}, u32[]{:S(2)}, u32[]{:S(2)}) %collective-permute-start.2) | collective-permute-done | bytes 1048608 | tf_op jit(solution)/shard_map/ppermute | solution.py:222
  254.8 1.2 add_convert_fusion
  (60 shorter events, 3.2 us)
Async XLA Ops:
  6.5 138.5 %all-gather.2.cloned.1.call-start = ((), (), s32[]{:S(2)}) async-start(), calls=%async_computation.5 | async-start | bytes 9437184 | tf_op jit(solution)/shard_map/all_gather | solution.py:180
  27.2 1.1 copy-start.1
  28.3 7.7 %copy-start.6 = (s32[16]{0:T(128)S(1)}, s32[16]{0:T(128)}, u32[]{:S(2)}) copy-start(s32[16]{0:T(128)} %param.11) | copy-start | bytes 196
  28.3 7.7 %copy-start.7 = (s32[16]{0:T(128)S(1)}, s32[16]{0:T(128)}, u32[]{:S(2)}) copy-start(s32[16]{0:T(128)} %param.12) | copy-start | bytes 196
  28.3 7.9 %copy-start.2 = (s32[128]{0:T(128)S(1)}, s32[128]{0:T(128)}, u32[]{:S(2)}) copy-start(s32[128]{0:T(128)} %param.10) | copy-start | bytes 1540
  29.6 11.9 %all-to-all-start = ((bf16[512,4,128]{2,0,1:T(8,128)(2,1)}), bf16[512,4,128]{2,0,1:T(8,128)(2,1)}, u32[]{:S(2)}, u32[]{:S(2)}) async-start(bf16[512,4,128]{2,0,1:T(8,128)(2,1)} %copy.44), calls=%async_computation | async-start | bytes 1048576 | tf_op jit(solution)/shard_map/all_to_all | solution.py:181
  33.7 191.8 %collective-permute-start.1 = (bf16[512,4096]{1,0:T(8,128)(2,1)}, bf16[512,4096]{1,0:T(8,128)(2,1)}, u32[]{:S(2)}, u32[]{:S(2)}) collective-permute-start(bf16[512,4096]{1,0:T(8,128)(2,1)} %param.13), channel_id=1, source_target_pairs={{0,1},{1,0},{2,3},{3,2},{4,5},{5,4},{6,7},{7,6},{8,9},{9,8},{10,11... | collective-permute-start | bytes 12582920 | tf_op jit(solution)/shard_map/ppermute | solution.py:208
  37.5 108.2 %copy-start.4 = (s32[8]{0:T(128)}, s32[8]{0:T(128)S(1)}, u32[]{:S(2)}) copy-start(s32[8]{0:T(128)S(1)} %multiply_add_fusion.qstart_ref) | copy-start | bytes 100
  39.0 106.8 %copy-start.5 = (s32[66]{0:T(128)}, s32[66]{0:T(128)S(1)}, u32[]{:S(2)}) copy-start(s32[66]{0:T(128)S(1)} %broadcast_minimum_fusion.qt_ref) | copy-start | bytes 796
  39.7 106.0 %copy-start.3 = (s32[66]{0:T(128)}, s32[66]{0:T(128)S(1)}, u32[]{:S(2)}) copy-start(s32[66]{0:T(128)S(1)} %get-tuple-element.19.kt_ref) | copy-start | bytes 796
  41.5 20.4 %all-to-all-start.1 = ((bf16[8,256,128]{2,1,0:T(8,128)(2,1)}), bf16[8,256,128]{2,1,0:T(8,128)(2,1)S(1)}, u32[]{:S(2)}, u32[]{:S(2)}) async-start(bf16[8,256,128]{2,1,0:T(8,128)(2,1)} %bitcast.7), calls=%async_computation.1 | async-start | bytes 1048576 | tf_op jit(solution)/shard_map/all_to_all | solution.py:181
  61.9 83.8 %copy-start = (bf16[8,256,128]{2,1,0:T(8,128)(2,1)}, bf16[8,256,128]{2,1,0:T(8,128)(2,1)S(1)}, u32[]{:S(2)}) copy-start(bf16[8,256,128]{2,1,0:T(8,128)(2,1)S(1)} %all-to-all-done.1) | copy-start | bytes 1572868
  209.3 8.9 %all-to-all-start.4 = ((bf16[4,512,128]{2,1,0:T(8,128)(2,1)}), bf16[4,512,128]{2,1,0:T(8,128)(2,1)S(1)}, u32[]{:S(2)}, u32[]{:S(2)}) async-start(bf16[4,512,128]{2,1,0:T(8,128)(2,1)} %bitcast.20), calls=%async_computation.4 | async-start | bytes 1048576 | tf_op jit(solution)/shard_map/all_to_all | solution.py:204
  218.9 6.7 %collective-permute-start = (bf16[2,128,512]{2,1,0:T(8,128)(2,1)S(1)}, bf16[2,128,512]{2,1,0:T(8,128)(2,1)S(1)}, u32[]{:S(2)}, u32[]{:S(2)}) collective-permute-start(bf16[2,128,512]{2,1,0:T(8,128)(2,1)S(1)} %dynamic-slice_bitcast_fusion), channel_id=1, source_target_pairs={{0,1},{1,0},{2,3},{3,2},{4,5},{5,4},{6,7},{7,6},{8,9},{9,8},{10,11... | collective-permute-start | bytes 786440 | tf_op jit(solution)/shard_map/ppermute | solution.py:213
  228.5 26.3 %collective-permute-start.2 = (bf16[128,4096]{1,0:T(8,128)(2,1)S(1)}, bf16[128,4096]{1,0:T(8,128)(2,1)S(1)}, u32[]{:S(2)}, u32[]{:S(2)}) collective-permute-start(bf16[128,4096]{1,0:T(8,128)(2,1)S(1)} %fusion), channel_id=1, source_target_pairs={{0,2},{2,0},{1,3},{3,1},{4,6},{6,4},{5,7},{7,5},{8,10},{10,8},{9,1... | collective-permute-start | bytes 3145736 | tf_op jit(solution)/shard_map/ppermute | solution.py:222
Sparse Core Ops, SparseCore 0:
  28.5 116.4 all-gather.1

commit v7 on v6

--- a/solution.py
+++ b/solution.py
@@ -15,6 +15,7 @@
 TK = 1024
 
 NEG = -1e30
+CG = ("cy", "cz")
 
 
 def block_spans(span_start, span_end, count):
@@ -170,15 +171,15 @@
 def per_device(queries, keys, values, doc_ids, span_start, span_end, out_weight):
     rows, local_width = queries.shape
     group = lax.axis_size("cl")
-    n_cg = lax.axis_size("cg")
+    n_cg = lax.axis_size(CG)
     chunk = rows * group
     piece = chunk // n_cg
-    j = lax.axis_index("cg")
+    j = lax.axis_index(CG)
 
     stacked = lax.all_to_all(jnp.stack([keys, values]), "cl", 2, 1, tiled=True)
     kv1 = jnp.concatenate([stacked[0], stacked[1]], axis=1)
-    kv_all = lax.all_gather(kv1, "cg", axis=0, tiled=True)
-    q1 = lax.all_to_all(lax.all_to_all(queries, "cl", 1, 0, tiled=True), "cg", 0, 0, tiled=True)
+    kv_all = lax.all_gather(lax.all_gather(kv1, "cz", axis=0, tiled=True), "cy", axis=0, tiled=True)
+    q1 = lax.all_to_all(lax.all_to_all(queries, "cl", 1, 0, tiled=True), CG, 0, 0, tiled=True)
     seq = kv_all.shape[0]
 
     count = doc_ids.shape[0]
@@ -200,7 +201,7 @@
 
     tables = step_tables(doc_ids, span_blocks, span_end, qstart, piece, seq)
     att1 = attend_head(tables, q1, kv_all, qd, qs, kd, ks, piece)
-    att0 = lax.all_to_all(att1, "cg", 0, 0, tiled=True)
+    att0 = lax.all_to_all(att1, CG, 0, 0, tiled=True)
     attended = lax.all_to_all(att0, "cl", 0, 1, tiled=True)
     tc = lax.axis_index("tc")
     th = lax.axis_index("th")
@@ -227,14 +228,14 @@
 def solution(mesh):
     n_ctx = mesh.shape["ctx"]
     group = 4
-    inner = Mesh(np.asarray(mesh.devices).reshape(n_ctx // group, group, 2, 2), ("cg", "cl", "th", "tc"))
+    inner = Mesh(np.asarray(mesh.devices).reshape(n_ctx // group // 2, 2, group, 2, 2), ("cy", "cz", "cl", "th", "tc"))
     out_sharding = NamedSharding(mesh, P(("ctx", "tp"), None))
-    split = P(("cg", "cl"), ("th", "tc"))
+    split = P(("cy", "cz", "cl"), ("th", "tc"))
     body = jax.shard_map(
         per_device,
         mesh=inner,
         in_specs=(split, split, split, P(), P(), P(), P(("th", "tc"), None)),
-        out_specs=P(("cg", "cl", "th", "tc"), None),
+        out_specs=P(("cy", "cz", "cl", "th", "tc"), None),
         check_vma=False,
     )
 

time: 265 us -> 279 us (1.053)
  waiting for transfers between devices: 114 us -> 132 us
  Pallas kernels: 46.1 us -> 51.3 us
  starting transfers between devices: 23.6 us -> 19.3 us
  blocking collectives: 34.8 us -> 31.3 us
    all_gather x1 -> x2, waiting for transfers between devices: 83.1 us -> 97.7 us  [the longest x1 57.4 us: per_device(): lax.all_gather(lax.all_gather(kv1, 'cz', axis=0, tiled=True), 'cy', axis=...]
    pallas_call x1, Pallas kernels: 46.1 us -> 51.3 us  [attend_head(): pl.pallas_call(make_kernel(tq), out_shape=jax.ShapeDtypeStruct(q.shape, j...]
    all_to_all x1, blocking collectives: 17.4 us -> 13.9 us  [per_device(): att0 = lax.all_to_all(att1, CG, 0, 0, tiled=True)]
    all_to_all x1, starting transfers between devices: 7.22 us -> 4.36 us  [per_device(): lax.all_to_all(lax.all_to_all(queries, 'cl', 1, 0, tiled=True), CG, 0, 0,...]
  transfers between devices with their start and end apart: 7 -> 8, of which waited for: 4 -> 6; matrix products, arithmetic and copies ran while one was open for 8% -> 8% of each run, Pallas kernels for 18% -> 18%
where the time goes in v7:
time: 279 us; the launch traced here: 278 us
  waiting for transfers between devices  132 us (47%)
  Pallas kernels  51.3 us (18%)
  blocking collectives  31.3 us (11%)
  starting transfers between devices  19.3 us (7%)
  between operations  13.7 us (5%)
  matrix products  11.8 us (4%)
  other arithmetic  9.82 us (4%)
  local copies, waits for them, and re-layouts  8.68 us (3%)
    all_gather x1, waiting for transfers between devices, per_device(): lax.all_gather(lax.all_gather(kv1, 'cz', axis=0, tiled=True), 'cy', axis=...  57.4 us
    pallas_call x1, Pallas kernels, attend_head(): pl.pallas_call(make_kernel(tq), out_shape=jax.ShapeDtypeStruct(q.shape, j...  51.3 us
    all_gather x1, waiting for transfers between devices, per_device(): lax.all_gather(kv1, 'cz', axis=0, tiled=True)  40.3 us
    ppermute x1, waiting for transfers between devices, per_device(): recv = lax.ppermute(other_half, 'th', swap)  17.9 us
    all_to_all x1, blocking collectives, per_device(): stacked = lax.all_to_all(jnp.stack([keys, values]), 'cl', 2, 1, tiled=True)  17.4 us
    all_to_all x1, blocking collectives, per_device(): att0 = lax.all_to_all(att1, CG, 0, 0, tiled=True)  13.9 us
    all_to_all x1, waiting for transfers between devices, per_device(): lax.all_to_all(lax.all_to_all(queries, 'cl', 1, 0, tiled=True), CG, 0, 0,...  9.96 us
    dot_general x2, matrix products, project(): jnp.dot(other, w_other, preferred_element_type=jnp.float32)  5.98 us
  transfers between devices with their start and end apart: 8, of which 6 were waited for; matrix products, arithmetic and copies ran while one was open for 8% of the time, Pallas kernels for 18%

profile of v7, /device:TPU:1, one launch (start us, length us, event | category | flops | bytes accessed | tf_op | source)
XLA Modules:
  0.0 278.1 jit_solution(4357840870203233017)
XLA Ops:
  6.5 1.3 pad_maximum_fusion
  7.8 1.0 copy.45
  8.8 17.4 %all_to_all.67 = bf16[2,512,512]{1,0,2:T(2,128)(2,1)S(1)} all-to-all(bf16[2,512,512]{1,0,2:T(2,128)(2,1)S(1)} %copy.45), channel_id=1, replica_groups=mesh['cy'=4,'cz'=2,'cl'=4,'th'=2,'tc'=2] {'cl'}, dimensions={2} | all-to-all | bytes 2097152 | tf_op jit(solution)/shard_map/all_to_all | solution.py:179
  26.2 0.9 copy.46
  27.2 1.1 pad_maximum_fusion.1
  28.4 40.3 %all-gather.3.cloned.1.call-done = bf16[4096,256]{1,0:T(8,128)(2,1)} async-done(((bf16[2048,256]{1,0:T(8,128)(2,1)}), bf16[4096,256]{1,0:T(8,128)(2,1)}) %all-gather.3.cloned.1.call-update) | async-done | bytes 2097168 | tf_op jit(solution)/shard_map/all_gather | solution.py:181
  69.0 1.0 copy.44
  70.0 4.1 %all-to-all-start = ((bf16[512,4,128]{2,0,1:T(8,128)(2,1)}), bf16[512,4,128]{2,0,1:T(8,128)(2,1)}, u32[]{:S(2)}, u32[]{:S(2)}) async-start(bf16[512,4,128]{2,0,1:T(8,128)(2,1)} %copy.44), calls=%async_computation | async-start | bytes 1048576 | tf_op jit(solution)/shard_map/all_to_all | solution.py:182
  74.2 0.9 collective-permute-start.1
  75.9 0.7 compare_select_fusion.ks_ref
  78.8 1.3 select_reduce_fusion
  80.4 1.1 all-to-all-done
  81.5 4.4 %all-to-all-start.1 = ((bf16[8,256,128]{2,1,0:T(8,128)(2,1)}), bf16[8,256,128]{2,1,0:T(8,128)(2,1)S(1)}, u32[]{:S(2)}, u32[]{:S(2)}) async-start(bf16[8,256,128]{2,1,0:T(8,128)(2,1)} %bitcast.7), calls=%async_computation.1 | async-start | bytes 1048576 | tf_op jit(solution)/shard_map/all_to_all | solution.py:182
  86.0 1.3 copy.54
  87.4 1.4 copy.56
  88.7 1.2 and_convert_fusion
  89.9 1.1 fusion.23.mode_ref
  91.0 10.0 %all-to-all-done.1 = bf16[8,256,128]{2,1,0:T(8,128)(2,1)S(1)} async-done(((bf16[8,256,128]{2,1,0:T(8,128)(2,1)}), bf16[8,256,128]{2,1,0:T(8,128)(2,1)S(1)}, u32[]{:S(2)}, u32[]{:S(2)}) %all-to-all-start.1) | async-done | bytes 524320 | tf_op jit(solution)/shard_map/all_to_all | solution.py:182
  101.0 57.4 %all-gather.5.cloned.1.call-done.k_ref.v_ref = bf16[16384,256]{1,0:T(8,128)(2,1)} async-done(((bf16[4096,256]{1,0:T(8,128)(2,1)}), bf16[16384,256]{1,0:T(8,128)(2,1)}) %all-gather.5.cloned.1.call-update) | async-done | bytes 8388624 | tf_op jit(solution)/shard_map/all_gather | solution.py:181
  158.3 0.7 eq.63
  159.1 51.3 %shard_map.73 = bf16[2048,128]{1,0:T(8,128)(2,1)} custom-call(s32[66]{0:T(128)} %copy-done.5, s32[66]{0:T(128)} %copy-done.3, s32[66]{0:T(128)} %get-tuple-element.26.first_ref, s32[66]{0:T(128)} %get-tuple-element.25.last_ref, s32[66]{0:T(128)} %fusion.23.mode_ref, s32[8]{0:T(128)} %copy-done.4, bf16[2048,128]{1,0:T(8,128)(2,1)} %bitcast.84, ...), custom_call_target="tpu_custom_call" | custom-call | tf_op jit(solution)/shard_map/pallas_call | solution.py:113
  210.4 13.9 %all_to_all.68 = bf16[8,256,128]{2,1,0:T(8,128)(2,1)} all-to-all(bf16[8,256,128]{2,1,0:T(8,128)(2,1)} %bitcast.85), channel_id=1, replica_groups=mesh['cy'=4,'cz'=2,'cl'=4,'th'=2,'tc'=2] {'cy','cz'}, dimensions={0} | all-to-all | bytes 1048576 | tf_op jit(solution)/shard_map/all_to_all | solution.py:204
  224.3 3.6 %all-to-all-start.4 = ((bf16[4,512,128]{2,1,0:T(8,128)(2,1)}), bf16[4,512,128]{2,1,0:T(8,128)(2,1)S(1)}, u32[]{:S(2)}, u32[]{:S(2)}) async-start(bf16[4,512,128]{2,1,0:T(8,128)(2,1)} %bitcast.20), calls=%async_computation.4 | async-start | bytes 1048576 | tf_op jit(solution)/shard_map/all_to_all | solution.py:205
  227.9 5.5 %all-to-all-done.4 = bf16[4,512,128]{2,1,0:T(8,128)(2,1)S(1)} async-done(((bf16[4,512,128]{2,1,0:T(8,128)(2,1)}), bf16[4,512,128]{2,1,0:T(8,128)(2,1)S(1)}, u32[]{:S(2)}, u32[]{:S(2)}) %all-to-all-start.4) | async-done | bytes 524320 | tf_op jit(solution)/shard_map/all_to_all | solution.py:205
  234.0 3.8 %collective-permute-start = (bf16[2,128,512]{2,1,0:T(8,128)(2,1)S(1)}, bf16[2,128,512]{2,1,0:T(8,128)(2,1)S(1)}, u32[]{:S(2)}, u32[]{:S(2)}) collective-permute-start(bf16[2,128,512]{2,1,0:T(8,128)(2,1)S(1)} %dynamic-slice_bitcast_fusion), channel_id=1, source_target_pairs={{0,1},{1,0},{2,3},{3,2},{4,5},{5,4},{6,7},{7,6},{8,9},{9,8},{10,11... | collective-permute-start | bytes 786440 | tf_op jit(solution)/shard_map/ppermute | solution.py:214
  237.8 2.9 %fusion.2 = f32[128,4096]{1,0:T(8,128)S(1)} fusion(bf16[512,4096]{1,0:T(8,128)(2,1)} %param.13, bf16[2,2,128,512]{3,2,1,0:T(8,128)(2,1)S(1)} %reshape.294, s32[]{:T(128)S(6)} %select_n.173, s32[]{:T(128)S(6)} %select_n.170), kind=kOutput, calls=%fused_computation.11 | convolution fusion | flops 536870912 | bytes 6422536 | tf_op jit(solution)/shard_map/dot_general | solution.py:219
  240.8 3.0 %fusion = bf16[128,4096]{1,0:T(8,128)(2,1)S(1)} fusion(f32[128,4096]{1,0:T(8,128)S(1)} %fusion.2, bf16[512,4096]{1,0:T(8,128)(2,1)} %collective-permute-done.1, bf16[2,128,512]{2,1,0:T(8,128)(2,1)S(1)} %collective-permute-done, s32[]{:T(128)S(6)} %select_n.172), kind=kOutput, calls=%fused_computation.2 | convolution fusion | flops 537919488 | bytes 7471108 | tf_op jit(solution)/shard_map/dot_general | solution.py:219
  243.7 2.4 collective-permute-start.2
  246.2 2.9 %fusion.5 = f32[128,4096]{1,0:T(8,128)S(1)} fusion(bf16[512,4096]{1,0:T(8,128)(2,1)} %param.13, bf16[2,2,128,512]{3,2,1,0:T(8,128)(2,1)S(1)} %reshape.294, s32[]{:T(128)S(6)} %select_n.168, s32[]{:T(128)S(6)} %select_n.170), kind=kOutput, calls=%fused_computation.14 | convolution fusion | flops 536870912 | bytes 6422536 | tf_op jit(solution)/shard_map/dot_general | solution.py:219
  249.1 3.0 %convolution_add_fusion.1 = f32[128,4096]{1,0:T(8,128)S(1)} fusion(f32[128,4096]{1,0:T(8,128)S(1)} %fusion.5, bf16[512,4096]{1,0:T(8,128)(2,1)} %collective-permute-done.1, bf16[2,128,512]{2,1,0:T(8,128)(2,1)S(1)} %collective-permute-done, s32[]{:T(128)S(6)} %select_n.167), kind=kOutput, calls=%fused_computation.1 | convolution fusion | flops 537395200 | bytes 8519684 | tf_op jit(solution)/shard_map/dot_general | solution.py:219
  252.1 17.9 %collective-permute-done.2 = bf16[128,4096]{1,0:T(8,128)(2,1)S(1)} collective-permute-done((bf16[128,4096]{1,0:T(8,128)(2,1)S(1)}, bf16[128,4096]{1,0:T(8,128)(2,1)S(1)}, u32[]{:S(2)}, u32[]{:S(2)}) %collective-permute-start.2) | collective-permute-done | bytes 1048608 | tf_op jit(solution)/shard_map/ppermute | solution.py:223
  270.0 1.2 add_convert_fusion
  (63 shorter events, 4.4 us)
Async XLA Ops:
  6.5 62.2 %all-gather.3.cloned.1.call-start = ((), (), s32[]{:S(2)}) async-start(), calls=%async_computation.5 | async-start | bytes 3145728 | tf_op jit(solution)/shard_map/all_gather | solution.py:181
  28.3 40.4 %copy-start.1 = (bf16[512,512]{1,0:T(8,128)(2,1)S(1)}, bf16[512,512]{1,0:T(8,128)(2,1)}, u32[]{:S(2)}) copy-start(bf16[512,512]{1,0:T(8,128)(2,1)} %param.7) | copy-start | bytes 1572868
  28.3 130.0 %all-gather.5.cloned.1.call-start = ((), (), s32[]{:S(2)}) async-start(), calls=%async_computation.6 | async-start | bytes 10485760 | tf_op jit(solution)/shard_map/all_gather | solution.py:181
  68.8 6.3 %copy-start.6 = (s32[16]{0:T(128)S(1)}, s32[16]{0:T(128)}, u32[]{:S(2)}) copy-start(s32[16]{0:T(128)} %param.11) | copy-start | bytes 196
  68.8 6.3 %copy-start.7 = (s32[16]{0:T(128)S(1)}, s32[16]{0:T(128)}, u32[]{:S(2)}) copy-start(s32[16]{0:T(128)} %param.12) | copy-start | bytes 196
  68.8 6.5 %copy-start.2 = (s32[128]{0:T(128)S(1)}, s32[128]{0:T(128)}, u32[]{:S(2)}) copy-start(s32[128]{0:T(128)} %param.10) | copy-start | bytes 1540
  70.0 11.5 %all-to-all-start = ((bf16[512,4,128]{2,0,1:T(8,128)(2,1)}), bf16[512,4,128]{2,0,1:T(8,128)(2,1)}, u32[]{:S(2)}, u32[]{:S(2)}) async-start(bf16[512,4,128]{2,0,1:T(8,128)(2,1)} %copy.44), calls=%async_computation | async-start | bytes 1048576 | tf_op jit(solution)/shard_map/all_to_all | solution.py:182
  74.2 166.6 %collective-permute-start.1 = (bf16[512,4096]{1,0:T(8,128)(2,1)}, bf16[512,4096]{1,0:T(8,128)(2,1)}, u32[]{:S(2)}, u32[]{:S(2)}) collective-permute-start(bf16[512,4096]{1,0:T(8,128)(2,1)} %param.13), channel_id=1, source_target_pairs={{0,1},{1,0},{2,3},{3,2},{4,5},{5,4},{6,7},{7,6},{8,9},{9,8},{10,11... | collective-permute-start | bytes 12582920 | tf_op jit(solution)/shard_map/ppermute | solution.py:209
  76.6 82.4 %copy-start.4 = (s32[8]{0:T(128)}, s32[8]{0:T(128)S(1)}, u32[]{:S(2)}) copy-start(s32[8]{0:T(128)S(1)} %multiply_add_fusion.qstart_ref) | copy-start | bytes 100
  78.0 81.1 %copy-start.5 = (s32[66]{0:T(128)}, s32[66]{0:T(128)S(1)}, u32[]{:S(2)}) copy-start(s32[66]{0:T(128)S(1)} %broadcast_minimum_fusion.qt_ref) | copy-start | bytes 796
  78.7 80.4 %copy-start.3 = (s32[66]{0:T(128)}, s32[66]{0:T(128)S(1)}, u32[]{:S(2)}) copy-start(s32[66]{0:T(128)S(1)} %get-tuple-element.19.kt_ref) | copy-start | bytes 796
  81.5 19.4 %all-to-all-start.1 = ((bf16[8,256,128]{2,1,0:T(8,128)(2,1)}), bf16[8,256,128]{2,1,0:T(8,128)(2,1)S(1)}, u32[]{:S(2)}, u32[]{:S(2)}) async-start(bf16[8,256,128]{2,1,0:T(8,128)(2,1)} %bitcast.7), calls=%async_computation.1 | async-start | bytes 1048576 | tf_op jit(solution)/shard_map/all_to_all | solution.py:182
  101.0 58.1 %copy-start = (bf16[8,256,128]{2,1,0:T(8,128)(2,1)}, bf16[8,256,128]{2,1,0:T(8,128)(2,1)S(1)}, u32[]{:S(2)}) copy-start(bf16[8,256,128]{2,1,0:T(8,128)(2,1)S(1)} %all-to-all-done.1) | copy-start | bytes 1572868
  224.3 9.1 %all-to-all-start.4 = ((bf16[4,512,128]{2,1,0:T(8,128)(2,1)}), bf16[4,512,128]{2,1,0:T(8,128)(2,1)S(1)}, u32[]{:S(2)}, u32[]{:S(2)}) async-start(bf16[4,512,128]{2,1,0:T(8,128)(2,1)} %bitcast.20), calls=%async_computation.4 | async-start | bytes 1048576 | tf_op jit(solution)/shard_map/all_to_all | solution.py:205
  234.0 6.7 %collective-permute-start = (bf16[2,128,512]{2,1,0:T(8,128)(2,1)S(1)}, bf16[2,128,512]{2,1,0:T(8,128)(2,1)S(1)}, u32[]{:S(2)}, u32[]{:S(2)}) collective-permute-start(bf16[2,128,512]{2,1,0:T(8,128)(2,1)S(1)} %dynamic-slice_bitcast_fusion), channel_id=1, source_target_pairs={{0,1},{1,0},{2,3},{3,2},{4,5},{5,4},{6,7},{7,6},{8,9},{9,8},{10,11... | collective-permute-start | bytes 786440 | tf_op jit(solution)/shard_map/ppermute | solution.py:214
  243.7 26.3 %collective-permute-start.2 = (bf16[128,4096]{1,0:T(8,128)(2,1)S(1)}, bf16[128,4096]{1,0:T(8,128)(2,1)S(1)}, u32[]{:S(2)}, u32[]{:S(2)}) collective-permute-start(bf16[128,4096]{1,0:T(8,128)(2,1)S(1)} %fusion), channel_id=1, source_target_pairs={{0,2},{2,0},{1,3},{3,1},{4,6},{6,4},{5,7},{7,5},{8,10},{10,8},{9,1... | collective-permute-start | bytes 3145736 | tf_op jit(solution)/shard_map/ppermute | solution.py:223
Sparse Core Ops, SparseCore 0:
  28.4 40.2 all-gather.2
  70.4 87.9 all-gather.4

commit v8 on v7

--- a/solution.py
+++ b/solution.py
@@ -15,7 +15,7 @@
 TK = 1024
 
 NEG = -1e30
-CG = ("cy", "cz")
+CG = ("cy", "cx")
 
 
 def block_spans(span_start, span_end, count):
@@ -123,7 +123,19 @@
     return jnp.sum(jnp.where(index[..., None] == slots, table, 0), axis=-1)
 
 
-def step_tables(doc_ids, span_blocks, span_end, qstart, tq, seq):
+def grid_bound(tiles, count, per_q, per_k, most):
+    best = [0] + [-1] * count
+    for end in range(1, count + 1):
+        for start in range(max(0, end - DOC_MOST), end):
+            if best[start] < 0:
+                continue
+            steps = sum(min(most, (b + per_q + SPAN_MOST - 2) // per_k - start // per_k + 1)
+                        for b in tiles if start <= b < end)
+            best[end] = max(best[end], best[start] + steps)
+    return best[count]
+
+
+def step_tables(doc_ids, span_blocks, span_end, qstart, tq, seq, layouts):
     count = doc_ids.shape[0]
     nq = qstart.shape[0]
     per_q = tq // BLOCK
@@ -141,6 +153,7 @@
     window = (DOC_MOST - 1) + per_q + (SPAN_MOST - 1)
     most = min(ntk, (window - 1) // per_k + 2)
     cnt = jnp.clip(hi_t - lo_t + 1, 1, most)
+    total = min(nq * most, max(grid_bound(tiles, count, per_q, per_k, most) for tiles in layouts))
     ends = jnp.cumsum(cnt)
     starts = ends - cnt
     stride = seq // nq // BLOCK
@@ -171,14 +184,18 @@
 def per_device(queries, keys, values, doc_ids, span_start, span_end, out_weight):
     rows, local_width = queries.shape
     group = lax.axis_size("cl")
-    n_cg = lax.axis_size(CG)
+    n_cy = lax.axis_size("cy")
+    n_cx = lax.axis_size("cx")
+    n_cg = n_cy * n_cx
     chunk = rows * group
     piece = chunk // n_cg
     j = lax.axis_index(CG)
 
     stacked = lax.all_to_all(jnp.stack([keys, values]), "cl", 2, 1, tiled=True)
     kv1 = jnp.concatenate([stacked[0], stacked[1]], axis=1)
-    kv_all = lax.all_gather(lax.all_gather(kv1, "cz", axis=0, tiled=True), "cy", axis=0, tiled=True)
+    kv_g = lax.all_gather(kv1, CG, axis=0, tiled=True)
+    kv_all = kv_g.reshape(n_cy, n_cx, group, rows, 2 * HEAD_DIM).transpose(0, 2, 1, 3, 4).reshape(
+        -1, 2 * HEAD_DIM)
     q1 = lax.all_to_all(lax.all_to_all(queries, "cl", 1, 0, tiled=True), CG, 0, 0, tiled=True)
     seq = kv_all.shape[0]
 
@@ -188,18 +205,30 @@
     span_tok = jnp.broadcast_to(span_blocks[:, None], (count, BLOCK)).reshape(seq)
     key_span = jnp.where(span_tok >= 0, span_tok, -2)
     query_span = jnp.where(span_tok >= 0, span_tok, -1)
+    halves = rows // piece
+    zq = j // halves
+    hq = j % halves
 
     def mine(x):
-        return lax.dynamic_index_in_dim(x.reshape(n_cg, n_cg, piece), j, axis=1, keepdims=False).reshape(
-            chunk, 1)
+        x = x.reshape(n_cy, group, n_cx, halves, piece)
+        x = lax.dynamic_index_in_dim(x, zq, axis=1, keepdims=False)
+        x = lax.dynamic_index_in_dim(x, hq, axis=2, keepdims=False)
+        return x.reshape(chunk, 1)
 
     qd = mine(doc_tok)
     qs = mine(query_span)
     kd = doc_tok.reshape(1, seq)
     ks = key_span.reshape(1, seq)
-    qstart = jnp.arange(n_cg, dtype=jnp.int32) * chunk + j * piece
-
-    tables = step_tables(doc_ids, span_blocks, span_end, qstart, piece, seq)
+    g = jnp.arange(n_cg, dtype=jnp.int32)
+    qstart = (g // n_cx) * (rows * group * n_cx) + zq * (rows * n_cx) + (g % n_cx) * rows + hq * piece
+    qstart = qstart.astype(jnp.int32)
+
+    def first_blocks(jj, gg):
+        return ((gg // n_cx) * (rows * group * n_cx) + (jj // halves) * (rows * n_cx) + (gg % n_cx) * rows
+                + (jj % halves) * piece) // BLOCK
+
+    layouts = [[first_blocks(jj, gg) for gg in range(n_cg)] for jj in range(n_cg)]
+    tables = step_tables(doc_ids, span_blocks, span_end, qstart, piece, seq, layouts)
     att1 = attend_head(tables, q1, kv_all, qd, qs, kd, ks, piece)
     att0 = lax.all_to_all(att1, CG, 0, 0, tiled=True)
     attended = lax.all_to_all(att0, "cl", 0, 1, tiled=True)
@@ -228,14 +257,15 @@
 def solution(mesh):
     n_ctx = mesh.shape["ctx"]
     group = 4
-    inner = Mesh(np.asarray(mesh.devices).reshape(n_ctx // group // 2, 2, group, 2, 2), ("cy", "cz", "cl", "th", "tc"))
+    inner = Mesh(np.asarray(mesh.devices).reshape(n_ctx // group // 2, group, 2, 2, 2),
+                 ("cy", "cl", "cx", "th", "tc"))
     out_sharding = NamedSharding(mesh, P(("ctx", "tp"), None))
-    split = P(("cy", "cz", "cl"), ("th", "tc"))
+    split = P(("cy", "cl", "cx"), ("th", "tc"))
     body = jax.shard_map(
         per_device,
         mesh=inner,
         in_specs=(split, split, split, P(), P(), P(), P(("th", "tc"), None)),
-        out_specs=P(("cy", "cz", "cl", "th", "tc"), None),
+        out_specs=P(("cy", "cl", "cx", "th", "tc"), None),
         check_vma=False,
     )
 

time: 279 us -> 338 us (1.21); the launches traced: 278 us -> 342 us
  waiting for transfers between devices: 132 us -> 175 us
  blocking collectives: 31.3 us -> 50.4 us
  Pallas kernels: 51.3 us -> 41.7 us
  local copies, waits for them, and re-layouts: 8.68 us -> 17.2 us
    all_gather x2 -> x1, waiting for transfers between devices: 97.7 us -> 150 us  [per_device(): kv_g = lax.all_gather(kv1, CG, axis=0, tiled=True)]
    all_to_all x1, blocking collectives: 13.9 us -> 30.6 us  [per_device(): att0 = lax.all_to_all(att1, CG, 0, 0, tiled=True)]
    all_to_all x1, waiting for transfers between devices: 9.96 us -> 0.01 us  [per_device(): lax.all_to_all(lax.all_to_all(queries, 'cl', 1, 0, tiled=True), CG, 0, 0,...]
    pallas_call x1, Pallas kernels: 51.3 us -> 41.7 us  [attend_head(): pl.pallas_call(make_kernel(tq), out_shape=jax.ShapeDtypeStruct(q.shape, j...]
    transpose x0 -> x1, local copies, waits for them, and re-layouts: none -> 7.47 us  [per_device(): kv_g.reshape(n_cy, n_cx, group, rows, 2 * HEAD_DIM).transpose(0, 2, 1, 3, 4)]
    reshape x0 -> x2, local copies, waits for them, and re-layouts: none -> 3.87 us  [mine(): return x.reshape(chunk, 1)]
  transfers between devices with their start and end apart: 8 -> 7, of which waited for: 6 -> 4; matrix products, arithmetic and copies ran while one was open for 8% -> 9% of each run, Pallas kernels for 18% -> 12%
where the time goes in v8:
time: 338 us; the launch traced here: 342 us
  waiting for transfers between devices  175 us (52%)
  blocking collectives  50.4 us (15%)
  Pallas kernels  41.7 us (12%)
  starting transfers between devices  21.4 us (6%)
  local copies, waits for them, and re-layouts  17.2 us (5%)
  between operations  13.7 us (4%)
  matrix products  11.8 us (3%)
  other arithmetic  9.82 us (3%)
    all_gather x1, waiting for transfers between devices, per_device(): kv_g = lax.all_gather(kv1, CG, axis=0, tiled=True)  150 us
    pallas_call x1, Pallas kernels, attend_head(): pl.pallas_call(make_kernel(tq), out_shape=jax.ShapeDtypeStruct(q.shape, j...  41.7 us
    all_to_all x1, blocking collectives, per_device(): att0 = lax.all_to_all(att1, CG, 0, 0, tiled=True)  30.6 us
    all_to_all x1, blocking collectives, per_device(): stacked = lax.all_to_all(jnp.stack([keys, values]), 'cl', 2, 1, tiled=True)  19.9 us
    ppermute x1, waiting for transfers between devices, per_device(): recv = lax.ppermute(other_half, 'th', swap)  18 us
    transpose x1, local copies, waits for them, and re-layouts, per_device(): kv_g.reshape(n_cy, n_cx, group, rows, 2 * HEAD_DIM).transpose(0, 2, 1, 3, 4)  7.47 us
    all_to_all x1, waiting for transfers between devices, per_device(): attended = lax.all_to_all(att0, 'cl', 0, 1, tiled=True)  7 us
  transfers between devices with their start and end apart: 7, of which 4 were waited for; matrix products, arithmetic and copies ran while one was open for 9% of the time, Pallas kernels for 12%

profile of v8, /device:TPU:1, one launch (start us, length us, event | category | flops | bytes accessed | tf_op | source)
XLA Modules:
  0.0 341.5 jit_solution(6279097323189809679)
XLA Ops:
  6.5 1.3 pad_maximum_fusion
  7.8 1.0 copy.54
  8.8 19.9 %all_to_all.67 = bf16[2,512,512]{1,0,2:T(2,128)(2,1)S(1)} all-to-all(bf16[2,512,512]{1,0,2:T(2,128)(2,1)S(1)} %copy.54), channel_id=1, replica_groups=mesh['cy'=4,'cl'=4,'cx'=2,'th'=2,'tc'=2] {'cl'}, dimensions={2} | all-to-all | bytes 2097152 | tf_op jit(solution)/shard_map/all_to_all | solution.py:194
  29.5 1.1 pad_maximum_fusion.1
  30.9 1.0 copy.53
  31.9 4.1 %all-to-all-start = ((bf16[512,4,128]{2,0,1:T(8,128)(2,1)}), bf16[512,4,128]{2,0,1:T(8,128)(2,1)}, u32[]{:S(2)}, u32[]{:S(2)}) async-start(bf16[512,4,128]{2,0,1:T(8,128)(2,1)} %copy.53), calls=%async_computation | async-start | bytes 1048576 | tf_op jit(solution)/shard_map/all_to_all | solution.py:199
  36.0 1.9 collective-permute-start.1
  38.7 0.7 compare_select_fusion.ks_ref
  39.9 0.6 slice.18
  41.2 0.6 broadcast_multiply_fusion
  41.9 1.3 select_reduce_fusion
  43.5 5.1 %all-to-all-start.1 = ((bf16[8,256,128]{2,1,0:T(8,128)(2,1)}), bf16[8,256,128]{2,1,0:T(8,128)(2,1)S(1)}, u32[]{:S(2)}, u32[]{:S(2)}) async-start(bf16[8,256,128]{2,1,0:T(8,128)(2,1)} %bitcast.7), calls=%async_computation.1 | async-start | bytes 1048576 | tf_op jit(solution)/shard_map/all_to_all | solution.py:199
  48.8 1.9 reshape.327.qd_ref
  50.7 2.0 reshape.328.qs_ref
  52.6 1.1 and_convert_fusion
  53.8 1.1 fusion.27.mode_ref
  54.9 150.2 %all-gather.2.cloned.1.call-done = bf16[16384,256]{1,0:T(8,128)(2,1)} async-done(((bf16[2048,256]{1,0:T(8,128)(2,1)}), bf16[16384,256]{1,0:T(8,128)(2,1)}) %all-gather.2.cloned.1.call-update) | async-done | bytes 8388624 | tf_op jit(solution)/shard_map/all_gather | solution.py:196
  205.1 7.5 %copy.58 = bf16[4,4,2,512,256]{4,3,2,1,0:T(8,128)(2,1)} copy(bf16[4,4,2,512,256]{4,3,1,2,0:T(8,128)(2,1)} %bitcast.81) | data formatting | bytes 16777216 | tf_op jit(solution)/shard_map/transpose | solution.py:197
  212.6 0.8 eq.67
  213.4 41.7 %shard_map.73 = bf16[2048,128]{1,0:T(8,128)(2,1)} custom-call(s32[66]{0:T(128)} %copy-done.5, s32[66]{0:T(128)} %copy-done.4, s32[66]{0:T(128)} %get-tuple-element.28.first_ref, s32[66]{0:T(128)} %get-tuple-element.27.last_ref, s32[66]{0:T(128)} %fusion.27.mode_ref, s32[8]{0:T(128)} %copy-done.3, bf16[2048,128]{1,0:T(8,128)(2,1)} %bitcast.83, ...), custom_call_target="tpu_custom_call" | custom-call | tf_op jit(solution)/shard_map/pallas_call | solution.py:113
  255.1 30.6 %all_to_all.68 = bf16[8,256,128]{2,1,0:T(8,128)(2,1)} all-to-all(bf16[8,256,128]{2,1,0:T(8,128)(2,1)} %bitcast.84), channel_id=1, replica_groups=mesh['cy'=4,'cl'=4,'cx'=2,'th'=2,'tc'=2] {'cy','cx'}, dimensions={0} | all-to-all | bytes 1048576 | tf_op jit(solution)/shard_map/all_to_all | solution.py:233
  285.7 4.4 %all-to-all-start.4 = ((bf16[4,512,128]{2,1,0:T(8,128)(2,1)}), bf16[4,512,128]{2,1,0:T(8,128)(2,1)S(1)}, u32[]{:S(2)}, u32[]{:S(2)}) async-start(bf16[4,512,128]{2,1,0:T(8,128)(2,1)} %bitcast.22), calls=%async_computation.4 | async-start | bytes 1048576 | tf_op jit(solution)/shard_map/all_to_all | solution.py:234
  290.1 7.0 %all-to-all-done.4 = bf16[4,512,128]{2,1,0:T(8,128)(2,1)S(1)} async-done(((bf16[4,512,128]{2,1,0:T(8,128)(2,1)}), bf16[4,512,128]{2,1,0:T(8,128)(2,1)S(1)}, u32[]{:S(2)}, u32[]{:S(2)}) %all-to-all-start.4) | async-done | bytes 524320 | tf_op jit(solution)/shard_map/all_to_all | solution.py:234
  297.1 0.4 copy.63
  297.7 3.5 %collective-permute-start = (bf16[2,128,512]{2,1,0:T(8,128)(2,1)S(1)}, bf16[2,128,512]{2,1,0:T(8,128)(2,1)S(1)}, u32[]{:S(2)}, u32[]{:S(2)}) collective-permute-start(bf16[2,128,512]{2,1,0:T(8,128)(2,1)S(1)} %dynamic-slice_bitcast_fusion), channel_id=1, source_target_pairs={{0,1},{1,0},{2,3},{3,2},{4,5},{5,4},{6,7},{7,6},{8,9},{9,8},{10,11... | collective-permute-start | bytes 786440 | tf_op jit(solution)/shard_map/ppermute | solution.py:243
  301.2 2.9 fusion.2
  304.2 3.0 fusion
  307.1 2.4 collective-permute-start.2
  309.5 2.9 fusion.5
  312.4 3.0 convolution_add_fusion.1
  315.4 18.0 %collective-permute-done.2 = bf16[128,4096]{1,0:T(8,128)(2,1)S(1)} collective-permute-done((bf16[128,4096]{1,0:T(8,128)(2,1)S(1)}, bf16[128,4096]{1,0:T(8,128)(2,1)S(1)}, u32[]{:S(2)}, u32[]{:S(2)}) %collective-permute-start.2) | collective-permute-done | bytes 1048608 | tf_op jit(solution)/shard_map/ppermute | solution.py:252
  333.4 1.2 add_convert_fusion
  (62 shorter events, 3.7 us)
Async XLA Ops:
  6.5 198.6 %all-gather.2.cloned.1.call-start = ((), (), s32[]{:S(2)}) async-start(), calls=%async_computation.5 | async-start | bytes 9437184 | tf_op jit(solution)/shard_map/all_gather | solution.py:196
  29.2 1.4 copy-start.1
  30.6 7.3 %copy-start.6 = (s32[16]{0:T(128)S(1)}, s32[16]{0:T(128)}, u32[]{:S(2)}) copy-start(s32[16]{0:T(128)} %param.11) | copy-start | bytes 196
  30.6 7.3 %copy-start.7 = (s32[16]{0:T(128)S(1)}, s32[16]{0:T(128)}, u32[]{:S(2)}) copy-start(s32[16]{0:T(128)} %param.12) | copy-start | bytes 196
  30.6 7.6 %copy-start.2 = (s32[128]{0:T(128)S(1)}, s32[128]{0:T(128)}, u32[]{:S(2)}) copy-start(s32[128]{0:T(128)} %param.10) | copy-start | bytes 1540
  31.9 11.7 %all-to-all-start = ((bf16[512,4,128]{2,0,1:T(8,128)(2,1)}), bf16[512,4,128]{2,0,1:T(8,128)(2,1)}, u32[]{:S(2)}, u32[]{:S(2)}) async-start(bf16[512,4,128]{2,0,1:T(8,128)(2,1)} %copy.53), calls=%async_computation | async-start | bytes 1048576 | tf_op jit(solution)/shard_map/all_to_all | solution.py:199
  36.0 268.1 %collective-permute-start.1 = (bf16[512,4096]{1,0:T(8,128)(2,1)}, bf16[512,4096]{1,0:T(8,128)(2,1)}, u32[]{:S(2)}, u32[]{:S(2)}) collective-permute-start(bf16[512,4096]{1,0:T(8,128)(2,1)} %param.13), channel_id=1, source_target_pairs={{0,1},{1,0},{2,3},{3,2},{4,5},{5,4},{6,7},{7,6},{8,9},{9,8},{10,11... | collective-permute-start | bytes 12582920 | tf_op jit(solution)/shard_map/ppermute | solution.py:238
  38.4 14.3 %copy-start.3 = (s32[8]{0:T(128)}, s32[8]{0:T(128)S(1)}, u32[]{:S(2)}) copy-start(s32[8]{0:T(128)S(1)} %get-tuple-element.24.qstart_ref) | copy-start | bytes 100
  41.1 171.5 %copy-start.5 = (s32[66]{0:T(128)}, s32[66]{0:T(128)S(1)}, u32[]{:S(2)}) copy-start(s32[66]{0:T(128)S(1)} %broadcast_minimum_fusion.qt_ref) | copy-start | bytes 796
  41.8 170.8 %copy-start.4 = (s32[66]{0:T(128)}, s32[66]{0:T(128)S(1)}, u32[]{:S(2)}) copy-start(s32[66]{0:T(128)S(1)} %get-tuple-element.19.kt_ref) | copy-start | bytes 796
  43.5 169.1 %all-to-all-start.1 = ((bf16[8,256,128]{2,1,0:T(8,128)(2,1)}), bf16[8,256,128]{2,1,0:T(8,128)(2,1)S(1)}, u32[]{:S(2)}, u32[]{:S(2)}) async-start(bf16[8,256,128]{2,1,0:T(8,128)(2,1)} %bitcast.7), calls=%async_computation.1 | async-start | bytes 1048576 | tf_op jit(solution)/shard_map/all_to_all | solution.py:199
  212.6 0.8 copy-start
  285.7 11.4 %all-to-all-start.4 = ((bf16[4,512,128]{2,1,0:T(8,128)(2,1)}), bf16[4,512,128]{2,1,0:T(8,128)(2,1)S(1)}, u32[]{:S(2)}, u32[]{:S(2)}) async-start(bf16[4,512,128]{2,1,0:T(8,128)(2,1)} %bitcast.22), calls=%async_computation.4 | async-start | bytes 1048576 | tf_op jit(solution)/shard_map/all_to_all | solution.py:234
  297.7 6.4 %collective-permute-start = (bf16[2,128,512]{2,1,0:T(8,128)(2,1)S(1)}, bf16[2,128,512]{2,1,0:T(8,128)(2,1)S(1)}, u32[]{:S(2)}, u32[]{:S(2)}) collective-permute-start(bf16[2,128,512]{2,1,0:T(8,128)(2,1)S(1)} %dynamic-slice_bitcast_fusion), channel_id=1, source_target_pairs={{0,1},{1,0},{2,3},{3,2},{4,5},{5,4},{6,7},{7,6},{8,9},{9,8},{10,11... | collective-permute-start | bytes 786440 | tf_op jit(solution)/shard_map/ppermute | solution.py:243
  307.1 26.3 %collective-permute-start.2 = (bf16[128,4096]{1,0:T(8,128)(2,1)S(1)}, bf16[128,4096]{1,0:T(8,128)(2,1)S(1)}, u32[]{:S(2)}, u32[]{:S(2)}) collective-permute-start(bf16[128,4096]{1,0:T(8,128)(2,1)S(1)} %fusion), channel_id=1, source_target_pairs={{0,2},{2,0},{1,3},{3,1},{4,6},{6,4},{5,7},{7,5},{8,10},{10,8},{9,1... | collective-permute-start | bytes 3145736 | tf_op jit(solution)/shard_map/ppermute | solution.py:252
Sparse Core Ops, SparseCore 0:
  30.8 174.3 all-gather.1

commit v9 on v6

--- a/solution.py
+++ b/solution.py
@@ -122,7 +122,19 @@
     return jnp.sum(jnp.where(index[..., None] == slots, table, 0), axis=-1)
 
 
-def step_tables(doc_ids, span_blocks, span_end, qstart, tq, seq):
+def grid_bound(tiles, count, per_q, per_k, most):
+    best = [0] + [-1] * count
+    for end in range(1, count + 1):
+        for start in range(max(0, end - DOC_MOST), end):
+            if best[start] < 0:
+                continue
+            steps = sum(min(most, (b + per_q + SPAN_MOST - 2) // per_k - start // per_k + 1)
+                        for b in tiles if start <= b < end)
+            best[end] = max(best[end], best[start] + steps)
+    return best[count]
+
+
+def step_tables(doc_ids, span_blocks, span_end, qstart, tq, seq, layouts):
     count = doc_ids.shape[0]
     nq = qstart.shape[0]
     per_q = tq // BLOCK
@@ -140,15 +152,9 @@
     window = (DOC_MOST - 1) + per_q + (SPAN_MOST - 1)
     most = min(ntk, (window - 1) // per_k + 2)
     cnt = jnp.clip(hi_t - lo_t + 1, 1, most)
+    total = min(nq * most, max(grid_bound(tiles, count, per_q, per_k, most) for tiles in layouts))
     ends = jnp.cumsum(cnt)
     starts = ends - cnt
-    stride = seq // nq // BLOCK
-    rest, spread = count, 0
-    while rest > 0:
-        size = min(DOC_MOST, rest)
-        spread += sum(max(0, size - 1 - stride * i) for i in range(size // stride + 1))
-        rest -= size
-    total = min(nq * most, nq * 3 + spread // per_k + 1)
     pos = jnp.arange(total, dtype=jnp.int32)
     qt = jnp.minimum(jnp.sum((pos[:, None] >= ends[None, :]).astype(jnp.int32), axis=1), nq - 1)
     live = pos < ends[-1]
@@ -198,7 +204,8 @@
     ks = key_span.reshape(1, seq)
     qstart = jnp.arange(n_cg, dtype=jnp.int32) * chunk + j * piece
 
-    tables = step_tables(doc_ids, span_blocks, span_end, qstart, piece, seq)
+    layouts = [[(gg * chunk + jj * piece) // BLOCK for gg in range(n_cg)] for jj in range(n_cg)]
+    tables = step_tables(doc_ids, span_blocks, span_end, qstart, piece, seq, layouts)
     att1 = attend_head(tables, q1, kv_all, qd, qs, kd, ks, piece)
     att0 = lax.all_to_all(att1, "cg", 0, 0, tiled=True)
     attended = lax.all_to_all(att0, "cl", 0, 1, tiled=True)

time: 265 us -> 263 us (level)
  Pallas kernels: 46.1 us -> 49.6 us
  blocking collectives: 34.8 us -> 31.3 us
    all_to_all x1, blocking collectives: 17.4 us -> 13.9 us  [per_device(): att0 = lax.all_to_all(att1, 'cg', 0, 0, tiled=True)]
    pallas_call x1, Pallas kernels: 46.1 us -> 49.6 us  [attend_head(): pl.pallas_call(make_kernel(tq), out_shape=jax.ShapeDtypeStruct(q.shape, j...]
  transfers between devices with their start and end apart: 7 -> 7, of which waited for: 4 -> 4; matrix products, arithmetic and copies ran while one was open for 8% -> 8% of each run, Pallas kernels for 18% -> 19%
where the time goes in v9:
time: 263 us
  waiting for transfers between devices  114 us (43%)
  Pallas kernels  49.6 us (19%)
  blocking collectives  31.3 us (12%)
  starting transfers between devices  23.5 us (9%)
  between operations  13.7 us (5%)
  matrix products  11.8 us (4%)
  other arithmetic  9.84 us (4%)
  local copies, waits for them, and re-layouts  8.85 us (3%)
    all_gather x1, waiting for transfers between devices, per_device(): kv_all = lax.all_gather(kv1, 'cg', axis=0, tiled=True)  83.4 us
    pallas_call x1, Pallas kernels, attend_head(): pl.pallas_call(make_kernel(tq), out_shape=jax.ShapeDtypeStruct(q.shape, j...  49.6 us
    ppermute x1, waiting for transfers between devices, per_device(): recv = lax.ppermute(other_half, 'th', swap)  17.6 us
    all_to_all x1, blocking collectives, per_device(): stacked = lax.all_to_all(jnp.stack([keys, values]), 'cl', 2, 1, tiled=True)  17.4 us
    all_to_all x1, blocking collectives, per_device(): att0 = lax.all_to_all(att1, 'cg', 0, 0, tiled=True)  13.9 us
    all_to_all x1, waiting for transfers between devices, per_device(): lax.all_to_all(lax.all_to_all(queries, 'cl', 1, 0, tiled=True), 'cg', 0,...  7.84 us
    all_to_all x1, starting transfers between devices, per_device(): lax.all_to_all(lax.all_to_all(queries, 'cl', 1, 0, tiled=True), 'cg', 0,...  7.22 us
    dot_general x2, matrix products, project(): jnp.dot(other, w_other, preferred_element_type=jnp.float32)  5.98 us
  transfers between devices with their start and end apart: 7, of which 4 were waited for; matrix products, arithmetic and copies ran while one was open for 8% of the time, Pallas kernels for 19%

profile of v9, /device:TPU:1, one launch (start us, length us, event | category | flops | bytes accessed | tf_op | source)
XLA Modules:
  0.0 262.7 jit_solution(11124494459524945145)
XLA Ops:
  6.5 1.3 pad_maximum_fusion
  7.8 1.0 copy.45
  8.8 17.4 %all_to_all.67 = bf16[2,512,512]{1,0,2:T(2,128)(2,1)S(1)} all-to-all(bf16[2,512,512]{1,0,2:T(2,128)(2,1)S(1)} %copy.45), channel_id=1, replica_groups=mesh['cg'=8,'cl'=4,'th'=2,'tc'=2] {'cl'}, dimensions={2} | all-to-all | bytes 2097152 | tf_op jit(solution)/shard_map/all_to_all | solution.py:184
  26.2 0.9 copy.46
  27.2 1.1 pad_maximum_fusion.1
  28.6 1.0 copy.44
  29.6 4.1 %all-to-all-start = ((bf16[512,4,128]{2,0,1:T(8,128)(2,1)}), bf16[512,4,128]{2,0,1:T(8,128)(2,1)}, u32[]{:S(2)}, u32[]{:S(2)}) async-start(bf16[512,4,128]{2,0,1:T(8,128)(2,1)} %copy.44), calls=%async_computation | async-start | bytes 1048576 | tf_op jit(solution)/shard_map/all_to_all | solution.py:187
  33.7 2.2 collective-permute-start.1
  36.8 0.7 compare_select_fusion.ks_ref
  38.0 0.6 slice.18
  39.1 0.6 broadcast_multiply_fusion
  39.8 1.1 select_reduce_fusion
  41.3 7.2 %all-to-all-start.1 = ((bf16[8,256,128]{2,1,0:T(8,128)(2,1)}), bf16[8,256,128]{2,1,0:T(8,128)(2,1)S(1)}, u32[]{:S(2)}, u32[]{:S(2)}) async-start(bf16[8,256,128]{2,1,0:T(8,128)(2,1)} %bitcast.7), calls=%async_computation.1 | async-start | bytes 1048576 | tf_op jit(solution)/shard_map/all_to_all | solution.py:187
  48.6 1.4 copy.54
  50.1 1.3 copy.56
  51.4 1.2 and_convert_fusion
  52.6 1.2 fusion.23.mode_ref
  53.8 7.8 %all-to-all-done.1 = bf16[8,256,128]{2,1,0:T(8,128)(2,1)S(1)} async-done(((bf16[8,256,128]{2,1,0:T(8,128)(2,1)}), bf16[8,256,128]{2,1,0:T(8,128)(2,1)S(1)}, u32[]{:S(2)}, u32[]{:S(2)}) %all-to-all-start.1) | async-done | bytes 524320 | tf_op jit(solution)/shard_map/all_to_all | solution.py:187
  61.7 83.4 %all-gather.2.cloned.1.call-done.k_ref.v_ref = bf16[16384,256]{1,0:T(8,128)(2,1)} async-done(((bf16[2048,256]{1,0:T(8,128)(2,1)}), bf16[16384,256]{1,0:T(8,128)(2,1)}) %all-gather.2.cloned.1.call-update) | async-done | bytes 8388624 | tf_op jit(solution)/shard_map/all_gather | solution.py:186
  145.0 0.7 eq.63
  145.7 49.6 %shard_map.73 = bf16[2048,128]{1,0:T(8,128)(2,1)} custom-call(s32[55]{0:T(128)} %copy-done.5, s32[55]{0:T(128)} %copy-done.3, s32[55]{0:T(128)} %get-tuple-element.26.first_ref, s32[55]{0:T(128)} %get-tuple-element.25.last_ref, s32[55]{0:T(128)} %fusion.23.mode_ref, s32[8]{0:T(128)} %copy-done.4, bf16[2048,128]{1,0:T(8,128)(2,1)} %bitcast.84, ...), custom_call_target="tpu_custom_call" | custom-call | tf_op jit(solution)/shard_map/pallas_call | solution.py:112
  195.3 13.9 %all_to_all.68 = bf16[8,256,128]{2,1,0:T(8,128)(2,1)} all-to-all(bf16[8,256,128]{2,1,0:T(8,128)(2,1)} %bitcast.85), channel_id=1, replica_groups=mesh['cg'=8,'cl'=4,'th'=2,'tc'=2] {'cg'}, dimensions={0} | all-to-all | bytes 1048576 | tf_op jit(solution)/shard_map/all_to_all | solution.py:210
  209.2 3.5 %all-to-all-start.4 = ((bf16[4,512,128]{2,1,0:T(8,128)(2,1)}), bf16[4,512,128]{2,1,0:T(8,128)(2,1)S(1)}, u32[]{:S(2)}, u32[]{:S(2)}) async-start(bf16[4,512,128]{2,1,0:T(8,128)(2,1)} %bitcast.20), calls=%async_computation.4 | async-start | bytes 1048576 | tf_op jit(solution)/shard_map/all_to_all | solution.py:211
  212.7 5.4 %all-to-all-done.4 = bf16[4,512,128]{2,1,0:T(8,128)(2,1)S(1)} async-done(((bf16[4,512,128]{2,1,0:T(8,128)(2,1)}), bf16[4,512,128]{2,1,0:T(8,128)(2,1)S(1)}, u32[]{:S(2)}, u32[]{:S(2)}) %all-to-all-start.4) | async-done | bytes 524320 | tf_op jit(solution)/shard_map/all_to_all | solution.py:211
  218.8 3.7 %collective-permute-start = (bf16[2,128,512]{2,1,0:T(8,128)(2,1)S(1)}, bf16[2,128,512]{2,1,0:T(8,128)(2,1)S(1)}, u32[]{:S(2)}, u32[]{:S(2)}) collective-permute-start(bf16[2,128,512]{2,1,0:T(8,128)(2,1)S(1)} %dynamic-slice_bitcast_fusion), channel_id=1, source_target_pairs={{0,1},{1,0},{2,3},{3,2},{4,5},{5,4},{6,7},{7,6},{8,9},{9,8},{10,11... | collective-permute-start | bytes 786440 | tf_op jit(solution)/shard_map/ppermute | solution.py:220
  222.4 2.9 %fusion.2 = f32[128,4096]{1,0:T(8,128)S(1)} fusion(bf16[512,4096]{1,0:T(8,128)(2,1)} %param.13, bf16[2,2,128,512]{3,2,1,0:T(8,128)(2,1)S(1)} %reshape.294, s32[]{:T(128)S(6)} %select_n.173, s32[]{:T(128)S(6)} %select_n.170), kind=kOutput, calls=%fused_computation.11 | convolution fusion | flops 536870912 | bytes 6422536 | tf_op jit(solution)/shard_map/dot_general | solution.py:225
  225.4 3.0 %fusion = bf16[128,4096]{1,0:T(8,128)(2,1)S(1)} fusion(f32[128,4096]{1,0:T(8,128)S(1)} %fusion.2, bf16[512,4096]{1,0:T(8,128)(2,1)} %collective-permute-done.1, bf16[2,128,512]{2,1,0:T(8,128)(2,1)S(1)} %collective-permute-done, s32[]{:T(128)S(6)} %select_n.172), kind=kOutput, calls=%fused_computation.2 | convolution fusion | flops 537919488 | bytes 7471108 | tf_op jit(solution)/shard_map/dot_general | solution.py:225
  228.3 2.8 %collective-permute-start.2 = (bf16[128,4096]{1,0:T(8,128)(2,1)S(1)}, bf16[128,4096]{1,0:T(8,128)(2,1)S(1)}, u32[]{:S(2)}, u32[]{:S(2)}) collective-permute-start(bf16[128,4096]{1,0:T(8,128)(2,1)S(1)} %fusion), channel_id=1, source_target_pairs={{0,2},{2,0},{1,3},{3,1},{4,6},{6,4},{5,7},{7,5},{8,10},{10,8},{9,1... | collective-permute-start | bytes 3145736 | tf_op jit(solution)/shard_map/ppermute | solution.py:229
  231.1 2.9 %fusion.5 = f32[128,4096]{1,0:T(8,128)S(1)} fusion(bf16[512,4096]{1,0:T(8,128)(2,1)} %param.13, bf16[2,2,128,512]{3,2,1,0:T(8,128)(2,1)S(1)} %reshape.294, s32[]{:T(128)S(6)} %select_n.168, s32[]{:T(128)S(6)} %select_n.170), kind=kOutput, calls=%fused_computation.14 | convolution fusion | flops 536870912 | bytes 6422536 | tf_op jit(solution)/shard_map/dot_general | solution.py:225
  234.0 3.0 %convolution_add_fusion.1 = f32[128,4096]{1,0:T(8,128)S(1)} fusion(f32[128,4096]{1,0:T(8,128)S(1)} %fusion.5, bf16[512,4096]{1,0:T(8,128)(2,1)} %collective-permute-done.1, bf16[2,128,512]{2,1,0:T(8,128)(2,1)S(1)} %collective-permute-done, s32[]{:T(128)S(6)} %select_n.167), kind=kOutput, calls=%fused_computation.1 | convolution fusion | flops 537395200 | bytes 8519684 | tf_op jit(solution)/shard_map/dot_general | solution.py:225
  237.0 17.6 %collective-permute-done.2 = bf16[128,4096]{1,0:T(8,128)(2,1)S(1)} collective-permute-done((bf16[128,4096]{1,0:T(8,128)(2,1)S(1)}, bf16[128,4096]{1,0:T(8,128)(2,1)S(1)}, u32[]{:S(2)}, u32[]{:S(2)}) %collective-permute-start.2) | collective-permute-done | bytes 1048608 | tf_op jit(solution)/shard_map/ppermute | solution.py:229
  254.6 1.2 add_convert_fusion
  (60 shorter events, 3.2 us)
Async XLA Ops:
  6.5 138.5 %all-gather.2.cloned.1.call-start = ((), (), s32[]{:S(2)}) async-start(), calls=%async_computation.5 | async-start | bytes 9437184 | tf_op jit(solution)/shard_map/all_gather | solution.py:186
  27.2 1.1 copy-start.1
  28.3 7.7 %copy-start.6 = (s32[16]{0:T(128)S(1)}, s32[16]{0:T(128)}, u32[]{:S(2)}) copy-start(s32[16]{0:T(128)} %param.11) | copy-start | bytes 196
  28.3 7.7 %copy-start.7 = (s32[16]{0:T(128)S(1)}, s32[16]{0:T(128)}, u32[]{:S(2)}) copy-start(s32[16]{0:T(128)} %param.12) | copy-start | bytes 196
  28.3 7.9 %copy-start.2 = (s32[128]{0:T(128)S(1)}, s32[128]{0:T(128)}, u32[]{:S(2)}) copy-start(s32[128]{0:T(128)} %param.10) | copy-start | bytes 1540
  29.6 11.7 %all-to-all-start = ((bf16[512,4,128]{2,0,1:T(8,128)(2,1)}), bf16[512,4,128]{2,0,1:T(8,128)(2,1)}, u32[]{:S(2)}, u32[]{:S(2)}) async-start(bf16[512,4,128]{2,0,1:T(8,128)(2,1)} %copy.44), calls=%async_computation | async-start | bytes 1048576 | tf_op jit(solution)/shard_map/all_to_all | solution.py:187
  33.7 191.6 %collective-permute-start.1 = (bf16[512,4096]{1,0:T(8,128)(2,1)}, bf16[512,4096]{1,0:T(8,128)(2,1)}, u32[]{:S(2)}, u32[]{:S(2)}) collective-permute-start(bf16[512,4096]{1,0:T(8,128)(2,1)} %param.13), channel_id=1, source_target_pairs={{0,1},{1,0},{2,3},{3,2},{4,5},{5,4},{6,7},{7,6},{8,9},{9,8},{10,11... | collective-permute-start | bytes 12582920 | tf_op jit(solution)/shard_map/ppermute | solution.py:215
  37.5 108.2 %copy-start.4 = (s32[8]{0:T(128)}, s32[8]{0:T(128)S(1)}, u32[]{:S(2)}) copy-start(s32[8]{0:T(128)S(1)} %multiply_add_fusion.qstart_ref) | copy-start | bytes 100
  39.0 106.8 %copy-start.5 = (s32[55]{0:T(128)}, s32[55]{0:T(128)S(1)}, u32[]{:S(2)}) copy-start(s32[55]{0:T(128)S(1)} %broadcast_minimum_fusion.qt_ref) | copy-start | bytes 664
  39.7 106.0 %copy-start.3 = (s32[55]{0:T(128)}, s32[55]{0:T(128)S(1)}, u32[]{:S(2)}) copy-start(s32[55]{0:T(128)S(1)} %get-tuple-element.19.kt_ref) | copy-start | bytes 664
  41.3 20.4 %all-to-all-start.1 = ((bf16[8,256,128]{2,1,0:T(8,128)(2,1)}), bf16[8,256,128]{2,1,0:T(8,128)(2,1)S(1)}, u32[]{:S(2)}, u32[]{:S(2)}) async-start(bf16[8,256,128]{2,1,0:T(8,128)(2,1)} %bitcast.7), calls=%async_computation.1 | async-start | bytes 1048576 | tf_op jit(solution)/shard_map/all_to_all | solution.py:187
  61.7 84.1 %copy-start = (bf16[8,256,128]{2,1,0:T(8,128)(2,1)}, bf16[8,256,128]{2,1,0:T(8,128)(2,1)S(1)}, u32[]{:S(2)}) copy-start(bf16[8,256,128]{2,1,0:T(8,128)(2,1)S(1)} %all-to-all-done.1) | copy-start | bytes 1572868
  209.2 8.9 %all-to-all-start.4 = ((bf16[4,512,128]{2,1,0:T(8,128)(2,1)}), bf16[4,512,128]{2,1,0:T(8,128)(2,1)S(1)}, u32[]{:S(2)}, u32[]{:S(2)}) async-start(bf16[4,512,128]{2,1,0:T(8,128)(2,1)} %bitcast.20), calls=%async_computation.4 | async-start | bytes 1048576 | tf_op jit(solution)/shard_map/all_to_all | solution.py:211
  218.8 6.6 %collective-permute-start = (bf16[2,128,512]{2,1,0:T(8,128)(2,1)S(1)}, bf16[2,128,512]{2,1,0:T(8,128)(2,1)S(1)}, u32[]{:S(2)}, u32[]{:S(2)}) collective-permute-start(bf16[2,128,512]{2,1,0:T(8,128)(2,1)S(1)} %dynamic-slice_bitcast_fusion), channel_id=1, source_target_pairs={{0,1},{1,0},{2,3},{3,2},{4,5},{5,4},{6,7},{7,6},{8,9},{9,8},{10,11... | collective-permute-start | bytes 786440 | tf_op jit(solution)/shard_map/ppermute | solution.py:220
  228.3 26.3 %collective-permute-start.2 = (bf16[128,4096]{1,0:T(8,128)(2,1)S(1)}, bf16[128,4096]{1,0:T(8,128)(2,1)S(1)}, u32[]{:S(2)}, u32[]{:S(2)}) collective-permute-start(bf16[128,4096]{1,0:T(8,128)(2,1)S(1)} %fusion), channel_id=1, source_target_pairs={{0,2},{2,0},{1,3},{3,1},{4,6},{6,4},{5,7},{7,5},{8,10},{10,8},{9,1... | collective-permute-start | bytes 3145736 | tf_op jit(solution)/shard_map/ppermute | solution.py:229
Sparse Core Ops, SparseCore 0:
  28.5 116.5 all-gather.1

commit v10 on v9

--- a/solution.py
+++ b/solution.py
@@ -27,8 +27,8 @@
 def make_kernel(tq):
     scale = 1.0 / math.sqrt(HEAD_DIM)
 
-    def kernel(qt_ref, kt_ref, first_ref, last_ref, mode_ref, qstart_ref,
-               q_ref, k_ref, v_ref, qd_ref, qs_ref, kd_ref, ks_ref, o_ref, m_sc, l_sc, acc_sc):
+    def kernel(qt_ref, kt_ref, first_ref, last_ref, mode_ref, qstart_ref, bdoc_ref, qspan_ref, kspan_ref,
+               q_ref, k_ref, v_ref, o_ref, m_sc, l_sc, acc_sc):
         p = pl.program_id(0)
         mode = mode_ref[p]
 
@@ -46,7 +46,21 @@
             if masked:
                 qpos = qstart_ref[qt_ref[p]] + lax.broadcasted_iota(jnp.int32, (tq, TK), 0)
                 kpos = kt_ref[p] * TK + lax.broadcasted_iota(jnp.int32, (tq, TK), 1)
-                allowed = (qd_ref[...] == kd_ref[...]) & ((kpos <= qpos) | (qs_ref[...] == ks_ref[...]))
+                qb0 = qstart_ref[qt_ref[p]] // BLOCK
+                kb0 = kt_ref[p] * (TK // BLOCK)
+                qrow = lax.broadcasted_iota(jnp.int32, (tq, 1), 0) // BLOCK
+                kcol = lax.broadcasted_iota(jnp.int32, (1, TK), 1) // BLOCK
+                qd = jnp.zeros((tq, 1), jnp.int32)
+                qs = jnp.zeros((tq, 1), jnp.int32)
+                for b in range(tq // BLOCK):
+                    qd = jnp.where(qrow == b, bdoc_ref[qb0 + b], qd)
+                    qs = jnp.where(qrow == b, qspan_ref[qb0 + b], qs)
+                kd = jnp.zeros((1, TK), jnp.int32)
+                ks = jnp.zeros((1, TK), jnp.int32)
+                for b in range(TK // BLOCK):
+                    kd = jnp.where(kcol == b, bdoc_ref[kb0 + b], kd)
+                    ks = jnp.where(kcol == b, kspan_ref[kb0 + b], ks)
+                allowed = (qd == kd) & ((kpos <= qpos) | (qs == ks))
                 scores = jnp.where(allowed, scores, NEG)
                 m_new = jnp.maximum(m_old, jnp.max(scores, axis=1, keepdims=True))
                 weights = jnp.where(allowed, jnp.exp(scores - m_new), 0.0)
@@ -75,7 +89,7 @@
     return kernel
 
 
-def attend_head(tables, q, kv, qd, qs, kd, ks, tq):
+def attend_head(tables, q, kv, tq):
     total = tables[0].shape[0]
 
     def qmap(p, qt, kt, *_):
@@ -97,10 +111,6 @@
             pl.BlockSpec((tq, HEAD_DIM), qmap),
             pl.BlockSpec((TK, HEAD_DIM), kmap),
             pl.BlockSpec((TK, HEAD_DIM), vmap),
-            pl.BlockSpec((tq, 1), qmap),
-            pl.BlockSpec((tq, 1), qmap),
-            pl.BlockSpec((1, TK), klab),
-            pl.BlockSpec((1, TK), klab),
         ],
         out_specs=pl.BlockSpec((tq, HEAD_DIM), qmap),
         scratch_shapes=[
@@ -114,7 +124,7 @@
         out_shape=jax.ShapeDtypeStruct(q.shape, jnp.bfloat16),
         grid_spec=grid_spec,
         compiler_params=pltpu.CompilerParams(dimension_semantics=("arbitrary",)),
-    )(*tables, q, kv, kv, qd, qs, kd, ks)
+    )(*tables, q, kv, kv)
 
 
 def take(table, index):
@@ -206,7 +216,9 @@
 
     layouts = [[(gg * chunk + jj * piece) // BLOCK for gg in range(n_cg)] for jj in range(n_cg)]
     tables = step_tables(doc_ids, span_blocks, span_end, qstart, piece, seq, layouts)
-    att1 = attend_head(tables, q1, kv_all, qd, qs, kd, ks, piece)
+    tables = tables + (doc_ids.astype(jnp.int32), jnp.where(span_blocks >= 0, span_blocks, -1).astype(jnp.int32),
+                       jnp.where(span_blocks >= 0, span_blocks, -2).astype(jnp.int32))
+    att1 = attend_head(tables, q1, kv_all, piece)
     att0 = lax.all_to_all(att1, "cg", 0, 0, tiled=True)
     attended = lax.all_to_all(att0, "cl", 0, 1, tiled=True)
     tc = lax.axis_index("tc")

time: 263 us -> 260 us (0.989)
  local copies, waits for them, and re-layouts: 8.85 us -> 4.63 us
  waiting for transfers between devices: 114 us -> 118 us
  Pallas kernels: 49.6 us -> 46.3 us
    pallas_call x1, Pallas kernels: 49.6 us -> 46.3 us  [attend_head(): pl.pallas_call(make_kernel(tq), out_shape=jax.ShapeDtypeStruct(q.shape, j...]
    unnamed x22 -> x18, local copies, waits for them, and re-layouts: 3.12 us -> 0.33 us
  transfers between devices with their start and end apart: 7 -> 7, of which waited for: 4 -> 4; matrix products, arithmetic and copies ran while one was open for 8% -> 7% of each run, Pallas kernels for 19% -> 18%
where the time goes in v10:
time: 260 us; the launch traced here: 259 us
  waiting for transfers between devices  118 us (45%)
  Pallas kernels  46.3 us (18%)
  blocking collectives  31.3 us (12%)
  starting transfers between devices  23.5 us (9%)
  between operations  13.6 us (5%)
  matrix products  11.8 us (5%)
  other arithmetic  9.71 us (4%)
  local copies, waits for them, and re-layouts  4.63 us (2%)
    all_gather x1, waiting for transfers between devices, per_device(): kv_all = lax.all_gather(kv1, 'cg', axis=0, tiled=True)  84.4 us
    pallas_call x1, Pallas kernels, attend_head(): pl.pallas_call(make_kernel(tq), out_shape=jax.ShapeDtypeStruct(q.shape, j...  46.3 us
    ppermute x1, waiting for transfers between devices, per_device(): recv = lax.ppermute(other_half, 'th', swap)  17.6 us
    all_to_all x1, blocking collectives, per_device(): stacked = lax.all_to_all(jnp.stack([keys, values]), 'cl', 2, 1, tiled=True)  17.4 us
    all_to_all x1, blocking collectives, per_device(): att0 = lax.all_to_all(att1, 'cg', 0, 0, tiled=True)  13.9 us
    all_to_all x1, waiting for transfers between devices, per_device(): lax.all_to_all(lax.all_to_all(queries, 'cl', 1, 0, tiled=True), 'cg', 0,...  10.5 us
    all_to_all x1, starting transfers between devices, per_device(): lax.all_to_all(lax.all_to_all(queries, 'cl', 1, 0, tiled=True), 'cg', 0,...  7.22 us
    dot_general x2, matrix products, project(): jnp.dot(other, w_other, preferred_element_type=jnp.float32)  5.98 us
  transfers between devices with their start and end apart: 7, of which 4 were waited for; matrix products, arithmetic and copies ran while one was open for 7% of the time, Pallas kernels for 18%

profile of v10, /device:TPU:1, one launch (start us, length us, event | category | flops | bytes accessed | tf_op | source)
XLA Modules:
  0.0 258.7 jit_solution(2294337041345893556)
XLA Ops:
  6.5 1.3 pad_maximum_fusion
  7.8 1.0 copy.27
  8.8 17.4 %all_to_all.67 = bf16[2,512,512]{1,0,2:T(2,128)(2,1)S(1)} all-to-all(bf16[2,512,512]{1,0,2:T(2,128)(2,1)S(1)} %copy.27), channel_id=1, replica_groups=mesh['cg'=8,'cl'=4,'th'=2,'tc'=2] {'cl'}, dimensions={2} | all-to-all | bytes 2097152 | tf_op jit(solution)/shard_map/all_to_all | solution.py:194
  26.2 0.9 copy.28
  27.2 1.1 pad_maximum_fusion.1
  28.4 0.2 copy.25
  28.6 1.1 copy.26
  29.6 4.1 %all-to-all-start = ((bf16[512,4,128]{2,0,1:T(8,128)(2,1)}), bf16[512,4,128]{2,0,1:T(8,128)(2,1)}, u32[]{:S(2)}, u32[]{:S(2)}) async-start(bf16[512,4,128]{2,0,1:T(8,128)(2,1)} %copy.26), calls=%async_computation | async-start | bytes 1048576 | tf_op jit(solution)/shard_map/all_to_all | solution.py:197
  33.8 2.2 collective-permute-start.1
  36.4 0.5 compare_select_fusion.2
  37.0 0.2 select_reduce_fusion.2
  37.5 0.6 slice.18
  38.3 0.7 broadcast_multiply_fusion
  39.1 1.1 select_reduce_fusion
  40.4 7.2 %all-to-all-start.1 = ((bf16[8,256,128]{2,1,0:T(8,128)(2,1)}), bf16[8,256,128]{2,1,0:T(8,128)(2,1)S(1)}, u32[]{:S(2)}, u32[]{:S(2)}) async-start(bf16[8,256,128]{2,1,0:T(8,128)(2,1)} %bitcast.7), calls=%async_computation.1 | async-start | bytes 1048576 | tf_op jit(solution)/shard_map/all_to_all | solution.py:197
  47.7 1.2 and_convert_fusion
  48.9 1.2 fusion.22.mode_ref
  50.1 10.5 %all-to-all-done.1 = bf16[8,256,128]{2,1,0:T(8,128)(2,1)S(1)} async-done(((bf16[8,256,128]{2,1,0:T(8,128)(2,1)}), bf16[8,256,128]{2,1,0:T(8,128)(2,1)S(1)}, u32[]{:S(2)}, u32[]{:S(2)}) %all-to-all-start.1) | async-done | bytes 524320 | tf_op jit(solution)/shard_map/all_to_all | solution.py:197
  60.6 84.4 %all-gather.2.cloned.1.call-done.k_ref.v_ref = bf16[16384,256]{1,0:T(8,128)(2,1)} async-done(((bf16[2048,256]{1,0:T(8,128)(2,1)}), bf16[16384,256]{1,0:T(8,128)(2,1)}) %all-gather.2.cloned.1.call-update) | async-done | bytes 8388624 | tf_op jit(solution)/shard_map/all_gather | solution.py:196
  145.0 46.3 %shard_map.73 = bf16[2048,128]{1,0:T(8,128)(2,1)} custom-call(s32[55]{0:T(128)} %copy-done.5, s32[55]{0:T(128)} %copy-done.3, s32[55]{0:T(128)} %get-tuple-element.26.first_ref, s32[55]{0:T(128)} %get-tuple-element.25.last_ref, s32[55]{0:T(128)} %fusion.22.mode_ref, s32[8]{0:T(128)} %copy-done.4, s32[128]{0:T(128)} %bdoc_ref.1, ...), custom_call_target="tpu_custom_call" | custom-call | tf_op jit(solution)/shard_map/pallas_call | solution.py:122
  191.3 13.9 %all_to_all.68 = bf16[8,256,128]{2,1,0:T(8,128)(2,1)} all-to-all(bf16[8,256,128]{2,1,0:T(8,128)(2,1)} %bitcast.67), channel_id=1, replica_groups=mesh['cg'=8,'cl'=4,'th'=2,'tc'=2] {'cg'}, dimensions={0} | all-to-all | bytes 1048576 | tf_op jit(solution)/shard_map/all_to_all | solution.py:222
  205.2 3.5 %all-to-all-start.4 = ((bf16[4,512,128]{2,1,0:T(8,128)(2,1)}), bf16[4,512,128]{2,1,0:T(8,128)(2,1)S(1)}, u32[]{:S(2)}, u32[]{:S(2)}) async-start(bf16[4,512,128]{2,1,0:T(8,128)(2,1)} %bitcast.16), calls=%async_computation.4 | async-start | bytes 1048576 | tf_op jit(solution)/shard_map/all_to_all | solution.py:223
  208.7 5.4 %all-to-all-done.4 = bf16[4,512,128]{2,1,0:T(8,128)(2,1)S(1)} async-done(((bf16[4,512,128]{2,1,0:T(8,128)(2,1)}), bf16[4,512,128]{2,1,0:T(8,128)(2,1)S(1)}, u32[]{:S(2)}, u32[]{:S(2)}) %all-to-all-start.4) | async-done | bytes 524320 | tf_op jit(solution)/shard_map/all_to_all | solution.py:223
  214.1 0.4 copy.29
  214.7 3.7 %collective-permute-start = (bf16[2,128,512]{2,1,0:T(8,128)(2,1)S(1)}, bf16[2,128,512]{2,1,0:T(8,128)(2,1)S(1)}, u32[]{:S(2)}, u32[]{:S(2)}) collective-permute-start(bf16[2,128,512]{2,1,0:T(8,128)(2,1)S(1)} %dynamic-slice_bitcast_fusion), channel_id=1, source_target_pairs={{0,1},{1,0},{2,3},{3,2},{4,5},{5,4},{6,7},{7,6},{8,9},{9,8},{10,11... | collective-permute-start | bytes 786440 | tf_op jit(solution)/shard_map/ppermute | solution.py:232
  218.4 2.9 %fusion.2 = f32[128,4096]{1,0:T(8,128)S(1)} fusion(bf16[512,4096]{1,0:T(8,128)(2,1)} %param.13, bf16[2,2,128,512]{3,2,1,0:T(8,128)(2,1)S(1)} %reshape.250, s32[]{:T(128)S(6)} %select_n.159, s32[]{:T(128)S(6)} %select_n.156), kind=kOutput, calls=%fused_computation.10 | convolution fusion | flops 536870912 | bytes 6422536 | tf_op jit(solution)/shard_map/dot_general | solution.py:237
  221.3 3.0 %fusion = bf16[128,4096]{1,0:T(8,128)(2,1)S(1)} fusion(f32[128,4096]{1,0:T(8,128)S(1)} %fusion.2, bf16[512,4096]{1,0:T(8,128)(2,1)} %collective-permute-done.1, bf16[2,128,512]{2,1,0:T(8,128)(2,1)S(1)} %collective-permute-done, s32[]{:T(128)S(6)} %select_n.158), kind=kOutput, calls=%fused_computation.2 | convolution fusion | flops 537919488 | bytes 7471108 | tf_op jit(solution)/shard_map/dot_general | solution.py:237
  224.3 2.8 %collective-permute-start.2 = (bf16[128,4096]{1,0:T(8,128)(2,1)S(1)}, bf16[128,4096]{1,0:T(8,128)(2,1)S(1)}, u32[]{:S(2)}, u32[]{:S(2)}) collective-permute-start(bf16[128,4096]{1,0:T(8,128)(2,1)S(1)} %fusion), channel_id=1, source_target_pairs={{0,2},{2,0},{1,3},{3,1},{4,6},{6,4},{5,7},{7,5},{8,10},{10,8},{9,1... | collective-permute-start | bytes 3145736 | tf_op jit(solution)/shard_map/ppermute | solution.py:241
  227.1 2.9 %fusion.5 = f32[128,4096]{1,0:T(8,128)S(1)} fusion(bf16[512,4096]{1,0:T(8,128)(2,1)} %param.13, bf16[2,2,128,512]{3,2,1,0:T(8,128)(2,1)S(1)} %reshape.250, s32[]{:T(128)S(6)} %select_n.154, s32[]{:T(128)S(6)} %select_n.156), kind=kOutput, calls=%fused_computation.13 | convolution fusion | flops 536870912 | bytes 6422536 | tf_op jit(solution)/shard_map/dot_general | solution.py:237
  230.0 3.0 %convolution_add_fusion.1 = f32[128,4096]{1,0:T(8,128)S(1)} fusion(f32[128,4096]{1,0:T(8,128)S(1)} %fusion.5, bf16[512,4096]{1,0:T(8,128)(2,1)} %collective-permute-done.1, bf16[2,128,512]{2,1,0:T(8,128)(2,1)S(1)} %collective-permute-done, s32[]{:T(128)S(6)} %select_n.153), kind=kOutput, calls=%fused_computation.1 | convolution fusion | flops 537395200 | bytes 8519684 | tf_op jit(solution)/shard_map/dot_general | solution.py:237
  233.0 17.6 %collective-permute-done.2 = bf16[128,4096]{1,0:T(8,128)(2,1)S(1)} collective-permute-done((bf16[128,4096]{1,0:T(8,128)(2,1)S(1)}, bf16[128,4096]{1,0:T(8,128)(2,1)S(1)}, u32[]{:S(2)}, u32[]{:S(2)}) %collective-permute-start.2) | collective-permute-done | bytes 1048608 | tf_op jit(solution)/shard_map/ppermute | solution.py:241
  250.6 1.2 add_convert_fusion
  (46 shorter events, 1.6 us)
Async XLA Ops:
  6.5 138.5 %all-gather.2.cloned.1.call-start = ((), (), s32[]{:S(2)}) async-start(), calls=%async_computation.5 | async-start | bytes 9437184 | tf_op jit(solution)/shard_map/all_gather | solution.py:196
  27.2 1.1 copy-start.1
  28.3 7.7 %copy-start.6 = (s32[16]{0:T(128)S(1)}, s32[16]{0:T(128)}, u32[]{:S(2)}) copy-start(s32[16]{0:T(128)} %param.11) | copy-start | bytes 196
  28.3 7.7 %copy-start.7 = (s32[16]{0:T(128)S(1)}, s32[16]{0:T(128)}, u32[]{:S(2)}) copy-start(s32[16]{0:T(128)} %param.12) | copy-start | bytes 196
  28.3 7.9 %copy-start.2 = (s32[128]{0:T(128)S(1)}, s32[128]{0:T(128)}, u32[]{:S(2)}) copy-start(s32[128]{0:T(128)} %bdoc_ref.1) | copy-start | bytes 1540
  29.6 10.8 %all-to-all-start = ((bf16[512,4,128]{2,0,1:T(8,128)(2,1)}), bf16[512,4,128]{2,0,1:T(8,128)(2,1)}, u32[]{:S(2)}, u32[]{:S(2)}) async-start(bf16[512,4,128]{2,0,1:T(8,128)(2,1)} %copy.26), calls=%async_computation | async-start | bytes 1048576 | tf_op jit(solution)/shard_map/all_to_all | solution.py:197
  33.8 187.5 %collective-permute-start.1 = (bf16[512,4096]{1,0:T(8,128)(2,1)}, bf16[512,4096]{1,0:T(8,128)(2,1)}, u32[]{:S(2)}, u32[]{:S(2)}) collective-permute-start(bf16[512,4096]{1,0:T(8,128)(2,1)} %param.13), channel_id=1, source_target_pairs={{0,1},{1,0},{2,3},{3,2},{4,5},{5,4},{6,7},{7,6},{8,9},{9,8},{10,11... | collective-permute-start | bytes 12582920 | tf_op jit(solution)/shard_map/ppermute | solution.py:227
  38.1 106.9 %copy-start.4 = (s32[8]{0:T(128)}, s32[8]{0:T(128)S(1)}, u32[]{:S(2)}) copy-start(s32[8]{0:T(128)S(1)} %multiply_add_fusion.qstart_ref) | copy-start | bytes 100
  38.2 106.8 %copy-start.5 = (s32[55]{0:T(128)}, s32[55]{0:T(128)S(1)}, u32[]{:S(2)}) copy-start(s32[55]{0:T(128)S(1)} %broadcast_minimum_fusion.qt_ref) | copy-start | bytes 664
  39.0 106.0 %copy-start.3 = (s32[55]{0:T(128)}, s32[55]{0:T(128)S(1)}, u32[]{:S(2)}) copy-start(s32[55]{0:T(128)S(1)} %get-tuple-element.19.kt_ref) | copy-start | bytes 664
  40.4 20.2 %all-to-all-start.1 = ((bf16[8,256,128]{2,1,0:T(8,128)(2,1)}), bf16[8,256,128]{2,1,0:T(8,128)(2,1)S(1)}, u32[]{:S(2)}, u32[]{:S(2)}) async-start(bf16[8,256,128]{2,1,0:T(8,128)(2,1)} %bitcast.7), calls=%async_computation.1 | async-start | bytes 1048576 | tf_op jit(solution)/shard_map/all_to_all | solution.py:197
  60.6 84.4 %copy-start = (bf16[8,256,128]{2,1,0:T(8,128)(2,1)}, bf16[8,256,128]{2,1,0:T(8,128)(2,1)S(1)}, u32[]{:S(2)}) copy-start(bf16[8,256,128]{2,1,0:T(8,128)(2,1)S(1)} %all-to-all-done.1) | copy-start | bytes 1572868
  205.2 8.9 %all-to-all-start.4 = ((bf16[4,512,128]{2,1,0:T(8,128)(2,1)}), bf16[4,512,128]{2,1,0:T(8,128)(2,1)S(1)}, u32[]{:S(2)}, u32[]{:S(2)}) async-start(bf16[4,512,128]{2,1,0:T(8,128)(2,1)} %bitcast.16), calls=%async_computation.4 | async-start | bytes 1048576 | tf_op jit(solution)/shard_map/all_to_all | solution.py:223
  214.7 6.6 %collective-permute-start = (bf16[2,128,512]{2,1,0:T(8,128)(2,1)S(1)}, bf16[2,128,512]{2,1,0:T(8,128)(2,1)S(1)}, u32[]{:S(2)}, u32[]{:S(2)}) collective-permute-start(bf16[2,128,512]{2,1,0:T(8,128)(2,1)S(1)} %dynamic-slice_bitcast_fusion), channel_id=1, source_target_pairs={{0,1},{1,0},{2,3},{3,2},{4,5},{5,4},{6,7},{7,6},{8,9},{9,8},{10,11... | collective-permute-start | bytes 786440 | tf_op jit(solution)/shard_map/ppermute | solution.py:232
  224.3 26.3 %collective-permute-start.2 = (bf16[128,4096]{1,0:T(8,128)(2,1)S(1)}, bf16[128,4096]{1,0:T(8,128)(2,1)S(1)}, u32[]{:S(2)}, u32[]{:S(2)}) collective-permute-start(bf16[128,4096]{1,0:T(8,128)(2,1)S(1)} %fusion), channel_id=1, source_target_pairs={{0,2},{2,0},{1,3},{3,1},{4,6},{6,4},{5,7},{7,5},{8,10},{10,8},{9,1... | collective-permute-start | bytes 3145736 | tf_op jit(solution)/shard_map/ppermute | solution.py:241
Sparse Core Ops, SparseCore 0:
  28.5 116.4 all-gather.1

commit v11 on v10

--- a/solution.py
+++ b/solution.py
@@ -12,7 +12,7 @@
 BLOCK = 128
 DOC_MOST = 80
 SPAN_MOST = 4
-TK = 1024
+TK = 2048
 
 NEG = -1e30
 

time: 260 us -> 259 us (level); the launches traced: 259 us -> 260 us
  no operation moved by 1% of the time
where the time goes in v11:
time: 259 us; the launch traced here: 260 us
  waiting for transfers between devices  118 us (46%)
  Pallas kernels  48 us (19%)
  blocking collectives  31.3 us (12%)
  starting transfers between devices  23.5 us (9%)
  between operations  13.6 us (5%)
  matrix products  11.8 us (5%)
  other arithmetic  9.36 us (4%)
  local copies, waits for them, and re-layouts  4.64 us (2%)
    all_gather x1, waiting for transfers between devices, per_device(): kv_all = lax.all_gather(kv1, 'cg', axis=0, tiled=True)  84.6 us
    pallas_call x1, Pallas kernels, attend_head(): pl.pallas_call(make_kernel(tq), out_shape=jax.ShapeDtypeStruct(q.shape, j...  48 us
    ppermute x1, waiting for transfers between devices, per_device(): recv = lax.ppermute(other_half, 'th', swap)  17.6 us
    all_to_all x1, blocking collectives, per_device(): stacked = lax.all_to_all(jnp.stack([keys, values]), 'cl', 2, 1, tiled=True)  17.4 us
    all_to_all x1, blocking collectives, per_device(): att0 = lax.all_to_all(att1, 'cg', 0, 0, tiled=True)  13.9 us
    all_to_all x1, waiting for transfers between devices, per_device(): lax.all_to_all(lax.all_to_all(queries, 'cl', 1, 0, tiled=True), 'cg', 0,...  10.6 us
    all_to_all x1, starting transfers between devices, per_device(): lax.all_to_all(lax.all_to_all(queries, 'cl', 1, 0, tiled=True), 'cg', 0,...  7.22 us
    dot_general x2, matrix products, project(): jnp.dot(other, w_other, preferred_element_type=jnp.float32)  5.97 us
  transfers between devices with their start and end apart: 7, of which 4 were waited for; matrix products, arithmetic and copies ran while one was open for 7% of the time, Pallas kernels for 18%

profile of v11, /device:TPU:1, one launch (start us, length us, event | category | flops | bytes accessed | tf_op | source)
XLA Modules:
  0.0 260.4 jit_solution(14981128805011763837)
XLA Ops:
  6.5 1.3 pad_maximum_fusion
  7.8 1.0 copy.27
  8.8 17.4 %all_to_all.67 = bf16[2,512,512]{1,0,2:T(2,128)(2,1)S(1)} all-to-all(bf16[2,512,512]{1,0,2:T(2,128)(2,1)S(1)} %copy.27), channel_id=1, replica_groups=mesh['cg'=8,'cl'=4,'th'=2,'tc'=2] {'cl'}, dimensions={2} | all-to-all | bytes 2097152 | tf_op jit(solution)/shard_map/all_to_all | solution.py:194
  26.2 0.9 copy.28
  27.2 1.1 pad_maximum_fusion.1
  28.4 0.2 copy.25
  28.6 1.1 copy.26
  29.6 4.1 %all-to-all-start = ((bf16[512,4,128]{2,0,1:T(8,128)(2,1)}), bf16[512,4,128]{2,0,1:T(8,128)(2,1)}, u32[]{:S(2)}, u32[]{:S(2)}) async-start(bf16[512,4,128]{2,0,1:T(8,128)(2,1)} %copy.26), calls=%async_computation | async-start | bytes 1048576 | tf_op jit(solution)/shard_map/all_to_all | solution.py:197
  33.8 2.2 collective-permute-start.1
  36.4 0.5 compare_select_fusion.2
  37.0 0.2 select_reduce_fusion.2
  37.5 0.6 slice.18
  38.3 0.7 broadcast_multiply_fusion
  39.1 0.7 select_reduce_fusion
  40.1 7.2 %all-to-all-start.1 = ((bf16[8,256,128]{2,1,0:T(8,128)(2,1)}), bf16[8,256,128]{2,1,0:T(8,128)(2,1)S(1)}, u32[]{:S(2)}, u32[]{:S(2)}) async-start(bf16[8,256,128]{2,1,0:T(8,128)(2,1)} %bitcast.7), calls=%async_computation.1 | async-start | bytes 1048576 | tf_op jit(solution)/shard_map/all_to_all | solution.py:197
  47.4 1.2 and_convert_fusion
  48.6 1.2 fusion.22.mode_ref
  49.8 10.6 %all-to-all-done.1 = bf16[8,256,128]{2,1,0:T(8,128)(2,1)S(1)} async-done(((bf16[8,256,128]{2,1,0:T(8,128)(2,1)}), bf16[8,256,128]{2,1,0:T(8,128)(2,1)S(1)}, u32[]{:S(2)}, u32[]{:S(2)}) %all-to-all-start.1) | async-done | bytes 524320 | tf_op jit(solution)/shard_map/all_to_all | solution.py:197
  60.4 84.6 %all-gather.2.cloned.1.call-done.k_ref.v_ref = bf16[16384,256]{1,0:T(8,128)(2,1)} async-done(((bf16[2048,256]{1,0:T(8,128)(2,1)}), bf16[16384,256]{1,0:T(8,128)(2,1)}) %all-gather.2.cloned.1.call-update) | async-done | bytes 8388624 | tf_op jit(solution)/shard_map/all_gather | solution.py:196
  145.0 48.0 %shard_map.73 = bf16[2048,128]{1,0:T(8,128)(2,1)} custom-call(s32[34]{0:T(128)} %copy-done.5, s32[34]{0:T(128)} %copy-done.3, s32[34]{0:T(128)} %get-tuple-element.26.first_ref, s32[34]{0:T(128)} %get-tuple-element.25.last_ref, s32[34]{0:T(128)} %fusion.22.mode_ref, s32[8]{0:T(128)} %copy-done.4, s32[128]{0:T(128)} %bdoc_ref.1, ...), custom_call_target="tpu_custom_call" | custom-call | tf_op jit(solution)/shard_map/pallas_call | solution.py:122
  193.0 13.9 %all_to_all.68 = bf16[8,256,128]{2,1,0:T(8,128)(2,1)} all-to-all(bf16[8,256,128]{2,1,0:T(8,128)(2,1)} %bitcast.67), channel_id=1, replica_groups=mesh['cg'=8,'cl'=4,'th'=2,'tc'=2] {'cg'}, dimensions={0} | all-to-all | bytes 1048576 | tf_op jit(solution)/shard_map/all_to_all | solution.py:222
  206.9 3.5 %all-to-all-start.4 = ((bf16[4,512,128]{2,1,0:T(8,128)(2,1)}), bf16[4,512,128]{2,1,0:T(8,128)(2,1)S(1)}, u32[]{:S(2)}, u32[]{:S(2)}) async-start(bf16[4,512,128]{2,1,0:T(8,128)(2,1)} %bitcast.16), calls=%async_computation.4 | async-start | bytes 1048576 | tf_op jit(solution)/shard_map/all_to_all | solution.py:223
  210.4 5.4 %all-to-all-done.4 = bf16[4,512,128]{2,1,0:T(8,128)(2,1)S(1)} async-done(((bf16[4,512,128]{2,1,0:T(8,128)(2,1)}), bf16[4,512,128]{2,1,0:T(8,128)(2,1)S(1)}, u32[]{:S(2)}, u32[]{:S(2)}) %all-to-all-start.4) | async-done | bytes 524320 | tf_op jit(solution)/shard_map/all_to_all | solution.py:223
  215.8 0.4 copy.29
  216.5 3.7 %collective-permute-start = (bf16[2,128,512]{2,1,0:T(8,128)(2,1)S(1)}, bf16[2,128,512]{2,1,0:T(8,128)(2,1)S(1)}, u32[]{:S(2)}, u32[]{:S(2)}) collective-permute-start(bf16[2,128,512]{2,1,0:T(8,128)(2,1)S(1)} %dynamic-slice_bitcast_fusion), channel_id=1, source_target_pairs={{0,1},{1,0},{2,3},{3,2},{4,5},{5,4},{6,7},{7,6},{8,9},{9,8},{10,11... | collective-permute-start | bytes 786440 | tf_op jit(solution)/shard_map/ppermute | solution.py:232
  220.2 2.9 %fusion.2 = f32[128,4096]{1,0:T(8,128)S(1)} fusion(bf16[512,4096]{1,0:T(8,128)(2,1)} %param.13, bf16[2,2,128,512]{3,2,1,0:T(8,128)(2,1)S(1)} %reshape.250, s32[]{:T(128)S(6)} %select_n.159, s32[]{:T(128)S(6)} %select_n.156), kind=kOutput, calls=%fused_computation.10 | convolution fusion | flops 536870912 | bytes 6422536 | tf_op jit(solution)/shard_map/dot_general | solution.py:237
  223.1 3.0 %fusion = bf16[128,4096]{1,0:T(8,128)(2,1)S(1)} fusion(f32[128,4096]{1,0:T(8,128)S(1)} %fusion.2, bf16[512,4096]{1,0:T(8,128)(2,1)} %collective-permute-done.1, bf16[2,128,512]{2,1,0:T(8,128)(2,1)S(1)} %collective-permute-done, s32[]{:T(128)S(6)} %select_n.158), kind=kOutput, calls=%fused_computation.2 | convolution fusion | flops 537919488 | bytes 7471108 | tf_op jit(solution)/shard_map/dot_general | solution.py:237
  226.1 2.8 %collective-permute-start.2 = (bf16[128,4096]{1,0:T(8,128)(2,1)S(1)}, bf16[128,4096]{1,0:T(8,128)(2,1)S(1)}, u32[]{:S(2)}, u32[]{:S(2)}) collective-permute-start(bf16[128,4096]{1,0:T(8,128)(2,1)S(1)} %fusion), channel_id=1, source_target_pairs={{0,2},{2,0},{1,3},{3,1},{4,6},{6,4},{5,7},{7,5},{8,10},{10,8},{9,1... | collective-permute-start | bytes 3145736 | tf_op jit(solution)/shard_map/ppermute | solution.py:241
  228.9 2.9 %fusion.5 = f32[128,4096]{1,0:T(8,128)S(1)} fusion(bf16[512,4096]{1,0:T(8,128)(2,1)} %param.13, bf16[2,2,128,512]{3,2,1,0:T(8,128)(2,1)S(1)} %reshape.250, s32[]{:T(128)S(6)} %select_n.154, s32[]{:T(128)S(6)} %select_n.156), kind=kOutput, calls=%fused_computation.13 | convolution fusion | flops 536870912 | bytes 6422536 | tf_op jit(solution)/shard_map/dot_general | solution.py:237
  231.8 3.0 %convolution_add_fusion.1 = f32[128,4096]{1,0:T(8,128)S(1)} fusion(f32[128,4096]{1,0:T(8,128)S(1)} %fusion.5, bf16[512,4096]{1,0:T(8,128)(2,1)} %collective-permute-done.1, bf16[2,128,512]{2,1,0:T(8,128)(2,1)S(1)} %collective-permute-done, s32[]{:T(128)S(6)} %select_n.153), kind=kOutput, calls=%fused_computation.1 | convolution fusion | flops 537395200 | bytes 8519684 | tf_op jit(solution)/shard_map/dot_general | solution.py:237
  234.8 17.6 %collective-permute-done.2 = bf16[128,4096]{1,0:T(8,128)(2,1)S(1)} collective-permute-done((bf16[128,4096]{1,0:T(8,128)(2,1)S(1)}, bf16[128,4096]{1,0:T(8,128)(2,1)S(1)}, u32[]{:S(2)}, u32[]{:S(2)}) %collective-permute-start.2) | collective-permute-done | bytes 1048608 | tf_op jit(solution)/shard_map/ppermute | solution.py:241
  252.4 1.2 add_convert_fusion
  (46 shorter events, 1.6 us)
Async XLA Ops:
  6.5 138.5 %all-gather.2.cloned.1.call-start = ((), (), s32[]{:S(2)}) async-start(), calls=%async_computation.5 | async-start | bytes 9437184 | tf_op jit(solution)/shard_map/all_gather | solution.py:196
  27.2 1.1 copy-start.1
  28.3 7.7 %copy-start.6 = (s32[16]{0:T(128)S(1)}, s32[16]{0:T(128)}, u32[]{:S(2)}) copy-start(s32[16]{0:T(128)} %param.11) | copy-start | bytes 196
  28.3 7.7 %copy-start.7 = (s32[16]{0:T(128)S(1)}, s32[16]{0:T(128)}, u32[]{:S(2)}) copy-start(s32[16]{0:T(128)} %param.12) | copy-start | bytes 196
  28.3 7.9 %copy-start.2 = (s32[128]{0:T(128)S(1)}, s32[128]{0:T(128)}, u32[]{:S(2)}) copy-start(s32[128]{0:T(128)} %bdoc_ref.1) | copy-start | bytes 1540
  29.6 10.4 %all-to-all-start = ((bf16[512,4,128]{2,0,1:T(8,128)(2,1)}), bf16[512,4,128]{2,0,1:T(8,128)(2,1)}, u32[]{:S(2)}, u32[]{:S(2)}) async-start(bf16[512,4,128]{2,0,1:T(8,128)(2,1)} %copy.26), calls=%async_computation | async-start | bytes 1048576 | tf_op jit(solution)/shard_map/all_to_all | solution.py:197
  33.8 189.3 %collective-permute-start.1 = (bf16[512,4096]{1,0:T(8,128)(2,1)}, bf16[512,4096]{1,0:T(8,128)(2,1)}, u32[]{:S(2)}, u32[]{:S(2)}) collective-permute-start(bf16[512,4096]{1,0:T(8,128)(2,1)} %param.13), channel_id=1, source_target_pairs={{0,1},{1,0},{2,3},{3,2},{4,5},{5,4},{6,7},{7,6},{8,9},{9,8},{10,11... | collective-permute-start | bytes 12582920 | tf_op jit(solution)/shard_map/ppermute | solution.py:227
  38.1 106.9 %copy-start.4 = (s32[8]{0:T(128)}, s32[8]{0:T(128)S(1)}, u32[]{:S(2)}) copy-start(s32[8]{0:T(128)S(1)} %multiply_add_fusion.qstart_ref) | copy-start | bytes 100
  38.2 106.8 %copy-start.5 = (s32[34]{0:T(128)}, s32[34]{0:T(128)S(1)}, u32[]{:S(2)}) copy-start(s32[34]{0:T(128)S(1)} %broadcast_minimum_fusion.qt_ref) | copy-start | bytes 412
  39.0 106.0 %copy-start.3 = (s32[34]{0:T(128)}, s32[34]{0:T(128)S(1)}, u32[]{:S(2)}) copy-start(s32[34]{0:T(128)S(1)} %get-tuple-element.19.kt_ref) | copy-start | bytes 412
  40.1 20.4 %all-to-all-start.1 = ((bf16[8,256,128]{2,1,0:T(8,128)(2,1)}), bf16[8,256,128]{2,1,0:T(8,128)(2,1)S(1)}, u32[]{:S(2)}, u32[]{:S(2)}) async-start(bf16[8,256,128]{2,1,0:T(8,128)(2,1)} %bitcast.7), calls=%async_computation.1 | async-start | bytes 1048576 | tf_op jit(solution)/shard_map/all_to_all | solution.py:197
  60.4 84.6 %copy-start = (bf16[8,256,128]{2,1,0:T(8,128)(2,1)}, bf16[8,256,128]{2,1,0:T(8,128)(2,1)S(1)}, u32[]{:S(2)}) copy-start(bf16[8,256,128]{2,1,0:T(8,128)(2,1)S(1)} %all-to-all-done.1) | copy-start | bytes 1572868
  206.9 8.9 %all-to-all-start.4 = ((bf16[4,512,128]{2,1,0:T(8,128)(2,1)}), bf16[4,512,128]{2,1,0:T(8,128)(2,1)S(1)}, u32[]{:S(2)}, u32[]{:S(2)}) async-start(bf16[4,512,128]{2,1,0:T(8,128)(2,1)} %bitcast.16), calls=%async_computation.4 | async-start | bytes 1048576 | tf_op jit(solution)/shard_map/all_to_all | solution.py:223
  216.5 6.6 %collective-permute-start = (bf16[2,128,512]{2,1,0:T(8,128)(2,1)S(1)}, bf16[2,128,512]{2,1,0:T(8,128)(2,1)S(1)}, u32[]{:S(2)}, u32[]{:S(2)}) collective-permute-start(bf16[2,128,512]{2,1,0:T(8,128)(2,1)S(1)} %dynamic-slice_bitcast_fusion), channel_id=1, source_target_pairs={{0,1},{1,0},{2,3},{3,2},{4,5},{5,4},{6,7},{7,6},{8,9},{9,8},{10,11... | collective-permute-start | bytes 786440 | tf_op jit(solution)/shard_map/ppermute | solution.py:232
  226.1 26.3 %collective-permute-start.2 = (bf16[128,4096]{1,0:T(8,128)(2,1)S(1)}, bf16[128,4096]{1,0:T(8,128)(2,1)S(1)}, u32[]{:S(2)}, u32[]{:S(2)}) collective-permute-start(bf16[128,4096]{1,0:T(8,128)(2,1)S(1)} %fusion), channel_id=1, source_target_pairs={{0,2},{2,0},{1,3},{3,1},{4,6},{6,4},{5,7},{7,5},{8,10},{10,8},{9,1... | collective-permute-start | bytes 3145736 | tf_op jit(solution)/shard_map/ppermute | solution.py:241
Sparse Core Ops, SparseCore 0:
  28.5 116.5 all-gather.1

commit v12 on v10

--- a/solution.py
+++ b/solution.py
@@ -231,15 +231,23 @@
     give = lax.dynamic_index_in_dim(blocks, 1 - tc, axis=1, keepdims=False)
     got = lax.ppermute(give, "tc", swap)
 
-    def project(half):
+    width = out_weight.shape[1] // 2
+
+    def project(half, col):
         own = lax.dynamic_index_in_dim(keep, half, axis=0, keepdims=False)
         other = lax.dynamic_index_in_dim(got, half, axis=0, keepdims=False)
-        return jnp.dot(own, out_weight, preferred_element_type=jnp.float32) + jnp.dot(
-            other, w_other, preferred_element_type=jnp.float32)
-
-    other_half = project(1 - th).astype(jnp.bfloat16)
-    recv = lax.ppermute(other_half, "th", swap)
-    mine_half = lax.optimization_barrier(project(th))
+        w_a = out_weight[:, col * width:(col + 1) * width]
+        w_b = w_other[:, col * width:(col + 1) * width]
+        return jnp.dot(own, w_a, preferred_element_type=jnp.float32) + jnp.dot(
+            other, w_b, preferred_element_type=jnp.float32)
+
+    sent = []
+    for col in range(2):
+        sent.append(lax.ppermute(project(1 - th, col).astype(jnp.bfloat16), "th", swap))
+        if col == 0:
+            sent[0] = lax.optimization_barrier(sent[0])
+    recv = jnp.concatenate(sent, axis=1)
+    mine_half = lax.optimization_barrier(jnp.concatenate([project(th, 0), project(th, 1)], axis=1))
     return (mine_half + recv.astype(jnp.float32)).astype(jnp.bfloat16)
 
 

time: 260 us -> 260 us (level)
  Pallas kernels: 46.3 us -> 41.9 us
  blocking collectives: 31.3 us -> 34 us
    pallas_call x1, Pallas kernels: 46.3 us -> 41.9 us  [attend_head(): pl.pallas_call(make_kernel(tq), out_shape=jax.ShapeDtypeStruct(q.shape, j...]
    all_to_all x1, blocking collectives: 13.9 us -> 16.6 us  [per_device(): att0 = lax.all_to_all(att1, 'cg', 0, 0, tiled=True)]
    dot_general x4 -> x8, matrix products: 11.8 us -> 13.3 us  [the longest x4 8.16 us: project(): jnp.dot(other, w_b, preferred_element_type=jnp.float32)]
    ppermute x1 -> x2, waiting for transfers between devices: 17.6 us -> 16.8 us  [per_device(): lax.ppermute(project(1 - th, col).astype(jnp.bfloat16), 'th', swap)]
  transfers between devices with their start and end apart: 7 -> 8, of which waited for: 4 -> 5; matrix products, arithmetic and copies ran while one was open for 7% -> 8% of each run, Pallas kernels for 18% -> 16%
where the time goes in v12:
time: 260 us; the launch traced here: 258 us
  waiting for transfers between devices  117 us (45%)
  Pallas kernels  41.9 us (16%)
  blocking collectives  34 us (13%)
  starting transfers between devices  23.9 us (9%)
  between operations  13.7 us (5%)
  matrix products  13.3 us (5%)
  other arithmetic  9.81 us (4%)
  local copies, waits for them, and re-layouts  4.64 us (2%)
    all_gather x1, waiting for transfers between devices, per_device(): kv_all = lax.all_gather(kv1, 'cg', axis=0, tiled=True)  84.5 us
    pallas_call x1, Pallas kernels, attend_head(): pl.pallas_call(make_kernel(tq), out_shape=jax.ShapeDtypeStruct(q.shape, j...  41.9 us
    all_to_all x1, blocking collectives, per_device(): stacked = lax.all_to_all(jnp.stack([keys, values]), 'cl', 2, 1, tiled=True)  17.4 us
    ppermute x2, waiting for transfers between devices, per_device(): lax.ppermute(project(1 - th, col).astype(jnp.bfloat16), 'th', swap)  16.8 us
    all_to_all x1, blocking collectives, per_device(): att0 = lax.all_to_all(att1, 'cg', 0, 0, tiled=True)  16.6 us
    all_to_all x1, waiting for transfers between devices, per_device(): lax.all_to_all(lax.all_to_all(queries, 'cl', 1, 0, tiled=True), 'cg', 0,...  10.4 us
    dot_general x4, matrix products, project(): jnp.dot(other, w_b, preferred_element_type=jnp.float32)  8.16 us
    all_to_all x1, starting transfers between devices, per_device(): lax.all_to_all(lax.all_to_all(queries, 'cl', 1, 0, tiled=True), 'cg', 0,...  7.22 us
  transfers between devices with their start and end apart: 8, of which 5 were waited for; matrix products, arithmetic and copies ran while one was open for 8% of the time, Pallas kernels for 16%

profile of v12, /device:TPU:1, one launch (start us, length us, event | category | flops | bytes accessed | tf_op | source)
XLA Modules:
  0.0 258.4 jit_solution(662708963819652297)
XLA Ops:
  6.5 1.3 pad_maximum_fusion.1
  7.8 1.0 copy.27
  8.8 17.4 %all_to_all.67 = bf16[2,512,512]{1,0,2:T(2,128)(2,1)S(1)} all-to-all(bf16[2,512,512]{1,0,2:T(2,128)(2,1)S(1)} %copy.27), channel_id=1, replica_groups=mesh['cg'=8,'cl'=4,'th'=2,'tc'=2] {'cl'}, dimensions={2} | all-to-all | bytes 2097152 | tf_op jit(solution)/shard_map/all_to_all | solution.py:194
  26.2 0.9 copy.28
  27.2 1.1 pad_maximum_fusion.2
  28.6 1.1 copy.26
  29.6 4.1 %all-to-all-start = ((bf16[512,4,128]{2,0,1:T(8,128)(2,1)}), bf16[512,4,128]{2,0,1:T(8,128)(2,1)}, u32[]{:S(2)}, u32[]{:S(2)}) async-start(bf16[512,4,128]{2,0,1:T(8,128)(2,1)} %copy.26), calls=%async_computation | async-start | bytes 1048576 | tf_op jit(solution)/shard_map/all_to_all | solution.py:197
  33.8 2.2 collective-permute-start.1
  36.4 0.5 compare_select_fusion.2
  37.5 0.6 slice.34
  38.3 0.7 broadcast_multiply_fusion
  39.1 1.1 select_reduce_fusion
  40.4 7.2 %all-to-all-start.1 = ((bf16[8,256,128]{2,1,0:T(8,128)(2,1)}), bf16[8,256,128]{2,1,0:T(8,128)(2,1)S(1)}, u32[]{:S(2)}, u32[]{:S(2)}) async-start(bf16[8,256,128]{2,1,0:T(8,128)(2,1)} %bitcast.7), calls=%async_computation.1 | async-start | bytes 1048576 | tf_op jit(solution)/shard_map/all_to_all | solution.py:197
  47.7 1.2 and_convert_fusion
  49.0 1.2 fusion.45.mode_ref
  50.2 10.4 %all-to-all-done.1 = bf16[8,256,128]{2,1,0:T(8,128)(2,1)S(1)} async-done(((bf16[8,256,128]{2,1,0:T(8,128)(2,1)}), bf16[8,256,128]{2,1,0:T(8,128)(2,1)S(1)}, u32[]{:S(2)}, u32[]{:S(2)}) %all-to-all-start.1) | async-done | bytes 524320 | tf_op jit(solution)/shard_map/all_to_all | solution.py:197
  60.5 84.5 %all-gather.2.cloned.1.call-done.k_ref.v_ref = bf16[16384,256]{1,0:T(8,128)(2,1)} async-done(((bf16[2048,256]{1,0:T(8,128)(2,1)}), bf16[16384,256]{1,0:T(8,128)(2,1)}) %all-gather.2.cloned.1.call-update) | async-done | bytes 8388624 | tf_op jit(solution)/shard_map/all_gather | solution.py:196
  145.0 41.9 %shard_map.73 = bf16[2048,128]{1,0:T(8,128)(2,1)} custom-call(s32[55]{0:T(128)} %copy-done.5, s32[55]{0:T(128)} %copy-done.4, s32[55]{0:T(128)} %get-tuple-element.26.first_ref, s32[55]{0:T(128)} %get-tuple-element.25.last_ref, s32[55]{0:T(128)} %fusion.45.mode_ref, s32[8]{0:T(128)} %copy-done.6, s32[128]{0:T(128)} %bdoc_ref.1, ...), custom_call_target="tpu_custom_call" | custom-call | tf_op jit(solution)/shard_map/pallas_call | solution.py:122
  186.9 16.6 %all_to_all.68 = bf16[8,256,128]{2,1,0:T(8,128)(2,1)} all-to-all(bf16[8,256,128]{2,1,0:T(8,128)(2,1)} %bitcast.71), channel_id=1, replica_groups=mesh['cg'=8,'cl'=4,'th'=2,'tc'=2] {'cg'}, dimensions={0} | all-to-all | bytes 1048576 | tf_op jit(solution)/shard_map/all_to_all | solution.py:222
  203.6 3.5 %all-to-all-start.4 = ((bf16[4,512,128]{2,1,0:T(8,128)(2,1)}), bf16[4,512,128]{2,1,0:T(8,128)(2,1)S(1)}, u32[]{:S(2)}, u32[]{:S(2)}) async-start(bf16[4,512,128]{2,1,0:T(8,128)(2,1)} %bitcast.16), calls=%async_computation.4 | async-start | bytes 1048576 | tf_op jit(solution)/shard_map/all_to_all | solution.py:223
  207.1 5.4 %all-to-all-done.4 = bf16[4,512,128]{2,1,0:T(8,128)(2,1)S(1)} async-done(((bf16[4,512,128]{2,1,0:T(8,128)(2,1)}), bf16[4,512,128]{2,1,0:T(8,128)(2,1)S(1)}, u32[]{:S(2)}, u32[]{:S(2)}) %all-to-all-start.4) | async-done | bytes 524320 | tf_op jit(solution)/shard_map/all_to_all | solution.py:223
  213.1 3.7 %collective-permute-start = (bf16[2,128,512]{2,1,0:T(8,128)(2,1)S(1)}, bf16[2,128,512]{2,1,0:T(8,128)(2,1)S(1)}, u32[]{:S(2)}, u32[]{:S(2)}) collective-permute-start(bf16[2,128,512]{2,1,0:T(8,128)(2,1)S(1)} %dynamic-slice_bitcast_fusion), channel_id=1, source_target_pairs={{0,1},{1,0},{2,3},{3,2},{4,5},{5,4},{6,7},{7,6},{8,9},{9,8},{10,11... | collective-permute-start | bytes 786440 | tf_op jit(solution)/shard_map/ppermute | solution.py:232
  216.9 2.2 fusion.10
  219.0 2.0 fusion.6
  222.0 2.0 fusion
  224.1 2.8 %collective-permute-start.2 = (bf16[128,2048]{1,0:T(8,128)(2,1)S(1)}, bf16[128,2048]{1,0:T(8,128)(2,1)S(1)}, u32[]{:S(2)}, u32[]{:S(2)}) collective-permute-start(bf16[128,2048]{1,0:T(8,128)(2,1)S(1)} %fusion), channel_id=1, source_target_pairs={{0,2},{2,0},{1,3},{3,1},{4,6},{6,4},{5,7},{7,5},{8,10},{10,8},{9,1... | collective-permute-start | bytes 1572872 | tf_op jit(solution)/shard_map/ppermute | solution.py:246
  226.8 2.0 fusion.1
  229.2 2.0 convolution_add_fusion.3
  231.3 2.0 convolution_add_fusion.2
  233.5 5.6 %collective-permute-done.2 = bf16[128,2048]{1,0:T(8,128)(2,1)S(1)} collective-permute-done((bf16[128,2048]{1,0:T(8,128)(2,1)S(1)}, bf16[128,2048]{1,0:T(8,128)(2,1)S(1)}, u32[]{:S(2)}, u32[]{:S(2)}) %collective-permute-start.2) | collective-permute-done | bytes 524320 | tf_op jit(solution)/shard_map/ppermute | solution.py:246
  239.1 11.2 %collective-permute-done.3 = bf16[128,2048]{1,0:T(8,128)(2,1)S(1)} collective-permute-done((bf16[128,2048]{1,0:T(8,128)(2,1)S(1)}, bf16[128,2048]{1,0:T(8,128)(2,1)S(1)}, u32[]{:S(2)}, u32[]{:S(2)}) %collective-permute-start.3) | collective-permute-done | bytes 524320 | tf_op jit(solution)/shard_map/ppermute | solution.py:246
  250.3 1.2 add_convert_fusion
  (55 shorter events, 3.8 us)
Async XLA Ops:
  6.5 138.5 %all-gather.2.cloned.1.call-start = ((), (), s32[]{:S(2)}) async-start(), calls=%async_computation.5 | async-start | bytes 9437184 | tf_op jit(solution)/shard_map/all_gather | solution.py:196
  27.2 1.1 copy-start.2
  28.3 7.7 %copy-start.7 = (s32[16]{0:T(128)S(1)}, s32[16]{0:T(128)}, u32[]{:S(2)}) copy-start(s32[16]{0:T(128)} %param.11) | copy-start | bytes 196
  28.3 7.7 %copy-start.8 = (s32[16]{0:T(128)S(1)}, s32[16]{0:T(128)}, u32[]{:S(2)}) copy-start(s32[16]{0:T(128)} %param.12) | copy-start | bytes 196
  28.3 7.9 %copy-start.3 = (s32[128]{0:T(128)S(1)}, s32[128]{0:T(128)}, u32[]{:S(2)}) copy-start(s32[128]{0:T(128)} %bdoc_ref.1) | copy-start | bytes 1540
  29.6 10.8 %all-to-all-start = ((bf16[512,4,128]{2,0,1:T(8,128)(2,1)}), bf16[512,4,128]{2,0,1:T(8,128)(2,1)}, u32[]{:S(2)}, u32[]{:S(2)}) async-start(bf16[512,4,128]{2,0,1:T(8,128)(2,1)} %copy.26), calls=%async_computation | async-start | bytes 1048576 | tf_op jit(solution)/shard_map/all_to_all | solution.py:197
  33.8 188.2 %collective-permute-start.1 = (bf16[512,4096]{1,0:T(8,128)(2,1)}, bf16[512,4096]{1,0:T(8,128)(2,1)}, u32[]{:S(2)}, u32[]{:S(2)}) collective-permute-start(bf16[512,4096]{1,0:T(8,128)(2,1)} %param.13), channel_id=1, source_target_pairs={{0,1},{1,0},{2,3},{3,2},{4,5},{5,4},{6,7},{7,6},{8,9},{9,8},{10,11... | collective-permute-start | bytes 12582920 | tf_op jit(solution)/shard_map/ppermute | solution.py:227
  38.2 106.8 %copy-start.5 = (s32[55]{0:T(128)}, s32[55]{0:T(128)S(1)}, u32[]{:S(2)}) copy-start(s32[55]{0:T(128)S(1)} %broadcast_minimum_fusion.qt_ref) | copy-start | bytes 664
  38.2 106.8 %copy-start.6 = (s32[8]{0:T(128)}, s32[8]{0:T(128)S(1)}, u32[]{:S(2)}) copy-start(s32[8]{0:T(128)S(1)} %multiply_add_fusion.qstart_ref) | copy-start | bytes 100
  39.0 106.0 %copy-start.4 = (s32[55]{0:T(128)}, s32[55]{0:T(128)S(1)}, u32[]{:S(2)}) copy-start(s32[55]{0:T(128)S(1)} %get-tuple-element.19.kt_ref) | copy-start | bytes 664
  40.4 20.1 %all-to-all-start.1 = ((bf16[8,256,128]{2,1,0:T(8,128)(2,1)}), bf16[8,256,128]{2,1,0:T(8,128)(2,1)S(1)}, u32[]{:S(2)}, u32[]{:S(2)}) async-start(bf16[8,256,128]{2,1,0:T(8,128)(2,1)} %bitcast.7), calls=%async_computation.1 | async-start | bytes 1048576 | tf_op jit(solution)/shard_map/all_to_all | solution.py:197
  60.5 84.5 %copy-start.1 = (bf16[8,256,128]{2,1,0:T(8,128)(2,1)}, bf16[8,256,128]{2,1,0:T(8,128)(2,1)S(1)}, u32[]{:S(2)}) copy-start(bf16[8,256,128]{2,1,0:T(8,128)(2,1)S(1)} %all-to-all-done.1) | copy-start | bytes 1572868
  203.6 8.9 %all-to-all-start.4 = ((bf16[4,512,128]{2,1,0:T(8,128)(2,1)}), bf16[4,512,128]{2,1,0:T(8,128)(2,1)S(1)}, u32[]{:S(2)}, u32[]{:S(2)}) async-start(bf16[4,512,128]{2,1,0:T(8,128)(2,1)} %bitcast.16), calls=%async_computation.4 | async-start | bytes 1048576 | tf_op jit(solution)/shard_map/all_to_all | solution.py:223
  213.1 8.9 %collective-permute-start = (bf16[2,128,512]{2,1,0:T(8,128)(2,1)S(1)}, bf16[2,128,512]{2,1,0:T(8,128)(2,1)S(1)}, u32[]{:S(2)}, u32[]{:S(2)}) collective-permute-start(bf16[2,128,512]{2,1,0:T(8,128)(2,1)S(1)} %dynamic-slice_bitcast_fusion), channel_id=1, source_target_pairs={{0,1},{1,0},{2,3},{3,2},{4,5},{5,4},{6,7},{7,6},{8,9},{9,8},{10,11... | collective-permute-start | bytes 786440 | tf_op jit(solution)/shard_map/ppermute | solution.py:232
  216.9 4.2 %copy-start = (bf16[512,4096]{1,0:T(8,128)(2,1)S(1)}, bf16[512,4096]{1,0:T(8,128)(2,1)}, u32[]{:S(2)}) copy-start(bf16[512,4096]{1,0:T(8,128)(2,1)} %param.13) | copy-start | bytes 12582916
  224.1 15.0 %collective-permute-start.2 = (bf16[128,2048]{1,0:T(8,128)(2,1)S(1)}, bf16[128,2048]{1,0:T(8,128)(2,1)S(1)}, u32[]{:S(2)}, u32[]{:S(2)}) collective-permute-start(bf16[128,2048]{1,0:T(8,128)(2,1)S(1)} %fusion), channel_id=1, source_target_pairs={{0,2},{2,0},{1,3},{3,1},{4,6},{6,4},{5,7},{7,5},{8,10},{10,8},{9,1... | collective-permute-start | bytes 1572872 | tf_op jit(solution)/shard_map/ppermute | solution.py:246
  228.9 21.5 %collective-permute-start.3 = (bf16[128,2048]{1,0:T(8,128)(2,1)S(1)}, bf16[128,2048]{1,0:T(8,128)(2,1)S(1)}, u32[]{:S(2)}, u32[]{:S(2)}) collective-permute-start(bf16[128,2048]{1,0:T(8,128)(2,1)S(1)} %fusion.1), channel_id=1, source_target_pairs={{0,2},{2,0},{1,3},{3,1},{4,6},{6,4},{5,7},{7,5},{8,10},{10,8},{9,1... | collective-permute-start | bytes 1572872 | tf_op jit(solution)/shard_map/ppermute | solution.py:246
Sparse Core Ops, SparseCore 0:
  28.5 116.5 all-gather.1
